TPU v7x, 128 devices: a whole 4x4x4 slice. The times are simulated.
128 devices in a mesh: grid: 32 (over x, y, core), orb: 4 (over z).
Axes of the slice: x: 4, y: 4, z: 4, core: 2. Of those that a mesh axis runs over, the one named last changes fastest.
Arguments:
- orbital_block: float32 [128, 192, 48, 128], P('orb', 'grid'), may hold values from -30 to 30
- potential: float32 [192, 48, 128], P('grid'), may hold values from -6 to -0.5
Outputs:
- orbitals: float32 [128, 192, 48, 128], P('orb', 'grid')
- triangle: float32 [128, 128], replicated
All inputs are finite; a program needn't handle non-finite values.
Results may differ from a plain program's by a relative error of at most 0.0003.
Values sent between devices are 32-bit elements; how exact they have to be, the bound alone decides.
No kernel may reach another device: no remote copies, remote signals or barrier semaphores. Data moves between devices by JAX's collectives and lax.ppermute only.
A program may use at most 128 MiB of HBM per device.

v0:
```python
import functools

import jax
import jax.numpy as jnp
from jax import lax
from jax.experimental import pallas as pl
from jax.experimental.pallas import tpu as pltpu
from jax.sharding import PartitionSpec as P

coefs = (
    -5369.0 / 1800.0,
    12.0 / 7.0,
    -15.0 / 56.0,
    10.0 / 189.0,
    -1.0 / 112.0,
    2.0 / 1925.0,
    -1.0 / 16632.0,
)
centre = 23.5
radius = 19.5
matmul_precision = lax.Precision.HIGH


def halo_planes(value, axis, width):
    size, length = (lax.axis_size(axis), value.shape[1])
    up = [(i, (i + 1) % size) for i in range(size - 1)]
    down = [(j, i) for i, j in up]
    last = lax.slice_in_dim(value, length - width, length, axis=1)
    first = lax.slice_in_dim(value, 0, width, axis=1)
    before = lax.ppermute(last, axis, up)
    after = lax.ppermute(first, axis, down)
    return before, after


def local_terms(orbital_field, potential):
    across = orbital_field.shape[2]
    depth_cells = orbital_field.shape[3]
    padded = jnp.pad(orbital_field, ((0, 0), (0, 0), (6, 6), (6, 6)))
    total = 3.0 * coefs[0] * orbital_field
    for k in range(1, 7):
        total = total + coefs[k] * (
            padded[:, :, 6 + k : 6 + k + across, 6 : 6 + depth_cells]
            + padded[:, :, 6 - k : 6 - k + across, 6 : 6 + depth_cells]
        )
        total = total + coefs[k] * (
            padded[:, :, 6 : 6 + across, 6 + k : 6 + k + depth_cells]
            + padded[:, :, 6 : 6 + across, 6 - k : 6 - k + depth_cells]
        )
    return -2.0 * total + potential[None] * orbital_field


def combine_kernel(scale, with_base, *refs):
    if with_base:
        local_ref, own_ref, before_ref, after_ref, base_ref, out_ref = refs
    else:
        local_ref, own_ref, before_ref, after_ref, out_ref = refs
    width = before_ref.shape[1]
    planes_own = own_ref.shape[1]

    def plane(q):
        if q < 0:
            return before_ref[:, width + q]
        if q >= planes_own:
            return after_ref[:, q - planes_own]
        return own_ref[:, q]

    for p in range(planes_own):
        acc = coefs[1] * (plane(p + 1) + plane(p - 1))
        for k in range(2, 7):
            acc = acc + coefs[k] * (plane(p + k) + plane(p - k))
        value = local_ref[:, p] - 2.0 * acc
        value = scale * (value - centre * own_ref[:, p]) / radius
        if with_base:
            value = value - base_ref[:, p]
        out_ref[:, p] = value


def filter_step(local, orbital_field, before, after, scale, base=None, start=0, count=None, base_start=0):
    count = orbital_field.shape[0] if count is None else count
    block_rows = 4 if count % 4 == 0 and start % 4 == 0 and base_start % 4 == 0 else 1
    offset = start // block_rows
    base_offset = base_start // block_rows
    block = (block_rows,) + orbital_field.shape[1:]
    halo_block = (block_rows,) + before.shape[1:]
    spec = pl.BlockSpec(block, lambda i: (i + offset, 0, 0, 0))
    halo_spec = pl.BlockSpec(halo_block, lambda i: (i + offset, 0, 0, 0))
    operands = [local, orbital_field, before, after]
    specs = [spec, spec, halo_spec, halo_spec]
    if base is not None:
        operands.append(base)
        specs.append(pl.BlockSpec(block, lambda i: (i + base_offset, 0, 0, 0)))
    return pl.pallas_call(
        functools.partial(combine_kernel, scale, base is not None),
        grid=(count // block_rows,),
        in_specs=specs,
        out_specs=pl.BlockSpec(block, lambda i: (i, 0, 0, 0)),
        out_shape=jax.ShapeDtypeStruct((count,) + orbital_field.shape[1:], jnp.float32),
    )(*operands)


def spread_cells(filtered):
    rows = filtered.shape[0]
    parts = lax.axis_size("orb")
    lanes = filtered.shape[3]
    rows_per_part = filtered.shape[1] * filtered.shape[2] // parts
    chunks = filtered.reshape(rows, parts, rows_per_part, lanes)
    return lax.all_to_all(chunks, "orb", 1, 0, tiled=True).reshape(parts, rows, rows_per_part, lanes)


def gram_matrix(left_rows, right_rows):
    return lax.dot_general(
        left_rows,
        right_rows,
        (((1, 2), (1, 2)), ((), ())),
        precision=matmul_precision,
        preferred_element_type=jnp.float32,
    )


def apply_rows(inverse, source_rows):
    return lax.dot_general(
        inverse,
        source_rows,
        (((0,), (0,)), ((), ())),
        precision=matmul_precision,
        preferred_element_type=jnp.float32,
    )


def mix_rows(weights, source_rows):
    return lax.dot_general(
        weights,
        source_rows,
        (((1,), (0,)), ((), ())),
        precision=matmul_precision,
        preferred_element_type=jnp.float32,
    )


def group_round(value, axis, stride, radix):
    size = lax.axis_size(axis)
    position = (lax.axis_index(axis) // stride) % radix
    received = [value]
    for shift in range(1, radix):
        pairs = []
        for i in range(size):
            p = (i // stride) % radix
            pairs.append((i, i + ((p + shift) % radix - p) * stride))
        received.append(lax.ppermute(value, axis, pairs))
    total = None
    for q in range(radix):
        choice = (position - q) % radix
        term = received[0]
        for shift in range(1, radix):
            term = jnp.where(choice == shift, received[shift], term)
        total = term if total is None else total + term
    return total


def exchange_sum(value, axis):
    size = lax.axis_size(axis)
    if size & (size - 1):
        return lax.psum(value, axis)
    stride = 1
    if size.bit_length() % 2 == 0:
        value = group_round(value, axis, 1, 2)
        stride = 2
    while stride < size:
        value = group_round(value, axis, stride, 4)
        stride *= 4
    return value


def cell_sum(value):
    return exchange_sum(exchange_sum(value, "grid"), "orb")


def eliminate_kernel(source_ref, result_ref):
    result_ref[...] = source_ref[...]
    rows, width = result_ref.shape
    lanes = lax.broadcasted_iota(jnp.int32, (1, width), 1)
    cols = lax.broadcasted_iota(jnp.int32, (rows, width), 1)
    row_ids = lax.broadcasted_iota(jnp.int32, (rows, 1), 0)

    def column_step(column, carry):
        current = result_ref[pl.ds(column, 1), :]
        pivot_value = jnp.sum(jnp.where(lanes == column, current, 0.0), axis=1, keepdims=True)
        root = jnp.sqrt(pivot_value)
        scaled = jnp.where(lanes >= column, current, 0.0) / root
        whole = result_ref[...]
        below = jnp.sum(jnp.where(cols == column, whole, 0.0), axis=1, keepdims=True) / root
        below = jnp.where(row_ids > column, below, 0.0)
        whole = whole - below * scaled
        result_ref[...] = jnp.where(row_ids == column, scaled, whole)
        return carry

    lax.fori_loop(0, rows, column_step, 0)


def eliminate(matrix, extra):
    source = jnp.concatenate([matrix, extra], axis=1)
    return pl.pallas_call(
        eliminate_kernel,
        out_shape=jax.ShapeDtypeStruct(source.shape, jnp.float32),
    )(source)


def factorize(rows_block, inv_cells):
    panel_rows = rows_block.shape[0] // 2
    leading = cell_sum(gram_matrix(rows_block[:panel_rows], rows_block)) * inv_cells
    eye = jnp.eye(panel_rows, dtype=jnp.float32)
    first = eliminate(leading, eye)
    first_r = first[:, :panel_rows]
    coupling = first[:, panel_rows : 2 * panel_rows]
    first_lower_inv = first[:, 2 * panel_rows :]
    first_q = mix_rows(first_lower_inv, rows_block[:panel_rows])
    remainder = rows_block[panel_rows:] - apply_rows(coupling, first_q)
    trailing = cell_sum(gram_matrix(remainder, remainder)) * inv_cells
    second = eliminate(trailing, eye)
    second_r = second[:, :panel_rows]
    second_lower_inv = second[:, panel_rows:]
    upper_rows = jnp.concatenate([first_r, coupling], axis=1)
    lower_rows = jnp.concatenate(
        [jnp.zeros((second_r.shape[0], panel_rows), jnp.float32), second_r], axis=1
    )
    triangle = jnp.concatenate([upper_rows, lower_rows], axis=0)
    return triangle, first_q, second_lower_inv, remainder


def local(orbital_block, potential):
    orb_rows = orbital_block.shape[0]
    half = orb_rows // 2
    before, after = halo_planes(orbital_block, "grid", 6)
    local_part = local_terms(orbital_block, potential)
    local_part, before, after = lax.optimization_barrier((local_part, before, after))
    first_a = filter_step(local_part, orbital_block, before, after, 1.0, start=0, count=half)
    first_b = filter_step(local_part, orbital_block, before, after, 1.0, start=half, count=orb_rows - half)
    before_a, after_a = halo_planes(first_a, "grid", 6)
    local_a = local_terms(first_a, potential)
    local_a, before_a, after_a, first_b = lax.optimization_barrier((local_a, before_a, after_a, first_b))
    before_b, after_b = halo_planes(first_b, "grid", 6)
    filtered_a = filter_step(local_a, first_a, before_a, after_a, 2.0, base=orbital_block)
    spread_a = spread_cells(filtered_a)
    local_b = local_terms(first_b, potential)
    local_b, before_b, after_b = lax.optimization_barrier((local_b, before_b, after_b))
    filtered_b = lax.optimization_barrier(
        filter_step(local_b, first_b, before_b, after_b, 2.0, base=orbital_block, base_start=half)
    )
    spread_b = spread_cells(filtered_b)
    parts, _, rows_per_part, lanes = spread_a.shape
    spread = jnp.stack([spread_a, spread_b], axis=1).reshape(-1, rows_per_part, lanes)
    inv_cells = 1.0 / (lax.axis_size("grid") * parts * rows_per_part * lanes)
    triangle, first_q, second_lower_inv, remainder = factorize(spread, inv_cells)
    second_q = mix_rows(second_lower_inv, remainder)
    orbitals = jnp.concatenate([first_q, second_q], axis=0)
    orbitals = orbitals.reshape(orbitals.shape[0], 1, rows_per_part, lanes)
    orbitals = lax.all_to_all(orbitals, "orb", 0, 1, tiled=True)
    return (orbitals.reshape(orbital_block.shape), triangle)


def solution(mesh):
    in_specs = (P("orb", "grid", None, None), P("grid", None, None))
    out_specs = (P("orb", "grid", None, None), P())
    return jax.shard_map(local, mesh=mesh, in_specs=in_specs, out_specs=out_specs, check_vma=False)
```

profile of v0, /device:TPU:0, one launch (start us, length us, event | category | flops | bytes accessed | tf_op | source)
XLA Modules:
  0.0 340.4 jit_solution(11661881530167771490)
XLA Ops:
  1.9 5.2 %collective-permute-start = (f32[32,6,48,128]{3,2,1,0:T(8,128)}, f32[32,6,48,128]{3,2,1,0:T(8,128)}, u32[]{:S(2)}, u32[]{:S(2)}) collective-permute-start(f32[32,6,48,128]{3,2,1,0:T(8,128)} %refs_4_.3), channel_id=1, source_target_pairs={{0,4},{4,8},{8,12},{12,16},{16,20},{20,24},{24,28},{28,32},{32,36}... | collective-permute-start | bytes 14155784 | tf_op jit(solution)/shard_map/ppermute | solution.py:30
  7.1 52.5 %multiply_add_fusion.refs_0_ = f32[32,6,48,128]{3,2,1,0:T(8,128)} fusion(f32[32,6,48,128]{3,2,1,0:T(8,128)} %refs_4_.3, f32[6,48,128]{2,1,0:T(8,128)} %param.3), kind=kLoop, calls=%fused_computation.114 | loop fusion | flops 47185920 | bytes 9584640 | tf_op jit(solution)/shard_map/add | solution.py:49
  59.6 6.2 %shard_map.41.refs_1_ = f32[16,6,48,128]{3,2,1,0:T(8,128)} custom-call(f32[32,6,48,128]{3,2,1,0:T(8,128)} %multiply_add_fusion.refs_0_, f32[32,6,48,128]{3,2,1,0:T(8,128)} %refs_4_.3, f32[32,6,48,128]{3,2,1,0:T(8,128)} %collective-permute-done.refs_2_, f32[32,6,48,128]{3,2,1,0:T(8,128)} %collective-permute-done.1.refs_3_), custom_call_target="tpu_custom_call" | custom-call | tf_op jit(solution)/shard_map/pallas_call | solution.py:92
  65.8 2.8 collective-permute-start.2
  69.9 6.2 %shard_map.42.refs_1_ = f32[16,6,48,128]{3,2,1,0:T(8,128)} custom-call(f32[32,6,48,128]{3,2,1,0:T(8,128)} %multiply_add_fusion.refs_0_, f32[32,6,48,128]{3,2,1,0:T(8,128)} %refs_4_.3, f32[32,6,48,128]{3,2,1,0:T(8,128)} %collective-permute-done.refs_2_, f32[32,6,48,128]{3,2,1,0:T(8,128)} %collective-permute-done.1.refs_3_), custom_call_target="tpu_custom_call" | custom-call | tf_op jit(solution)/shard_map/pallas_call | solution.py:92
  76.1 30.7 %multiply_add_fusion.2.refs_0_ = f32[16,6,48,128]{3,2,1,0:T(8,128)} fusion(f32[16,6,48,128]{3,2,1,0:T(8,128)} %shard_map.41.refs_1_, f32[6,48,128]{2,1,0:T(8,128)S(1)} %copy-done.4), kind=kLoop, calls=%fused_computation.191 | loop fusion | flops 23592960 | bytes 4866048 | tf_op jit(solution)/shard_map/add | solution.py:49
  106.8 4.5 %collective-permute-start.4 = (f32[16,6,48,128]{3,2,1,0:T(8,128)S(1)}, f32[16,6,48,128]{3,2,1,0:T(8,128)}, u32[]{:S(2)}, u32[]{:S(2)}) collective-permute-start(f32[16,6,48,128]{3,2,1,0:T(8,128)S(1)} %copy-done.2), channel_id=1, source_target_pairs={{0,4},{4,8},{8,12},{12,16},{16,20},{20,24},{24,28},{28,32},{32,36}... | collective-permute-start | bytes 7077896 | tf_op jit(solution)/shard_map/ppermute | solution.py:30
  112.5 6.8 %shard_map.43 = f32[16,6,48,128]{3,2,1,0:T(8,128)} custom-call(f32[16,6,48,128]{3,2,1,0:T(8,128)} %multiply_add_fusion.2.refs_0_, f32[16,6,48,128]{3,2,1,0:T(8,128)} %shard_map.41.refs_1_, f32[16,6,48,128]{3,2,1,0:T(8,128)} %collective-permute-done.2.refs_2_, f32[16,6,48,128]{3,2,1,0:T(8,128)} %collective-permute-done.3.refs_3_, f32[32,6,48,128]{3,2,1,0:T(8,128)} %refs_4_.3), custom_call_target="tpu_custom_call" | custom-call | tf_op jit(solution)/shard_map/pallas_call | solution.py:92
  119.3 3.2 copy.9
  122.6 5.4 %all-to-all-start = ((f32[16,4,72,128]{3,2,0,1:T(8,128)}), f32[16,4,72,128]{3,2,0,1:T(8,128)}, u32[]{:S(2)}, u32[]{:S(2)}) async-start(f32[16,4,72,128]{3,2,0,1:T(8,128)} %copy.9), calls=%async_computation | async-start | bytes 4718592 | tf_op jit(solution)/shard_map/all_to_all | solution.py:107
  128.0 8.5 %multiply_add_fusion.1.refs_0_ = f32[16,6,48,128]{3,2,1,0:T(8,128)} fusion(f32[16,6,48,128]{3,2,1,0:T(8,128)S(1)} %copy-done.2, f32[6,48,128]{2,1,0:T(8,128)S(1)} %copy-done.4), kind=kLoop, calls=%fused_computation.190 | loop fusion | flops 23592960 | bytes 4866048 | tf_op jit(solution)/shard_map/add | solution.py:49
  136.5 6.8 %shard_map.44 = f32[16,6,48,128]{3,2,1,0:T(8,128)} custom-call(f32[16,6,48,128]{3,2,1,0:T(8,128)} %multiply_add_fusion.1.refs_0_, f32[16,6,48,128]{3,2,1,0:T(8,128)} %shard_map.42.refs_1_, f32[16,6,48,128]{3,2,1,0:T(8,128)} %collective-permute-done.4.refs_2_, f32[16,6,48,128]{3,2,1,0:T(8,128)} %collective-permute-done.5.refs_3_, f32[32,6,48,128]{3,2,1,0:T(8,128)} %refs_4_.3), custom_call_target="tpu_custom_call" | custom-call | tf_op jit(solution)/shard_map/pallas_call | solution.py:92
  143.3 3.2 copy.10
  146.5 12.1 %all-to-all-done = f32[16,4,72,128]{3,2,0,1:T(8,128)} async-done(((f32[16,4,72,128]{3,2,0,1:T(8,128)}), f32[16,4,72,128]{3,2,0,1:T(8,128)}, u32[]{:S(2)}, u32[]{:S(2)}) %all-to-all-start) | async-done | bytes 2359328 | tf_op jit(solution)/shard_map/all_to_all | solution.py:107
  158.6 33.2 %all_to_all.45 = f32[16,4,72,128]{3,2,0,1:T(8,128)S(1)} all-to-all(f32[16,4,72,128]{3,2,0,1:T(8,128)} %copy.10), channel_id=1, replica_groups=mesh['grid'=32,'orb'=4] {'orb'}, dimensions={1} | all-to-all | bytes 4718592 | tf_op jit(solution)/shard_map/all_to_all | solution.py:107
  191.8 2.0 pad_maximum_fusion
  193.8 3.4 fusion.36
  198.6 2.6 convolution_bitcast_fusion.1
  202.5 4.6 %collective-permute-start.8 = (f32[64,128]{1,0:T(8,128)S(1)}, f32[64,128]{1,0:T(8,128)S(1)}, u32[]{:S(2)}, u32[]{:S(2)}) collective-permute-start(f32[64,128]{1,0:T(8,128)S(1)} %select_add_fusion.5), channel_id=1, source_target_pairs={{0,16},{4,20},{8,24},{12,28},{16,0},{20,4},{24,8},{28,12},{32,48},... | collective-permute-start | bytes 98312 | tf_op jit(solution)/shard_map/ppermute | solution.py:149
  212.6 2.5 collective-permute-start.11
  219.8 2.1 collective-permute-start.14
  222.6 3.5 %copy.13 = f32[2,2,16,72,128]{4,2,1,0,3:T(8,128)} copy(f32[2,2,16,72,128]{4,3,2,0,1:T(8,128)} %get-tuple-element.23) | data formatting | bytes 4718592 | tf_op jit(solution)/shard_map/slice | solution.py:217
  226.9 8.4 %shard_map.45 = f32[64,192]{1,0:T(8,128)} custom-call(f32[64,192]{1,0:T(8,128)} %pad_maximum_fusion.1.source_ref), custom_call_target="tpu_custom_call" | custom-call | tf_op jit(solution)/shard_map/pallas_call | solution.py:202
  241.6 3.7 %collective-permute-start.18 = (f32[64,64]{1,0:T(8,128)S(1)}, f32[64,64]{1,0:T(8,128)S(1)}, u32[]{:S(2)}, u32[]{:S(2)}) collective-permute-start(f32[64,64]{1,0:T(8,128)S(1)} %select_add_fusion.2), channel_id=1, source_target_pairs={{0,16},{4,20},{8,24},{12,28},{16,0},{20,4},{24,8},{28,12},{32,48},... | collective-permute-start | bytes 49160 | tf_op jit(solution)/shard_map/ppermute | solution.py:149
  249.3 3.0 collective-permute-start.21
  257.5 2.2 collective-permute-start.24
  264.3 8.0 %shard_map.46 = f32[64,128]{1,0:T(8,128)} custom-call(f32[64,128]{1,0:T(8,128)} %pad_maximum_fusion.2.source_ref), custom_call_target="tpu_custom_call" | custom-call | tf_op jit(solution)/shard_map/pallas_call | solution.py:202
  272.4 2.1 fusion.110
  275.0 4.9 %copy.15 = f32[128,1,72,128]{3,2,1,0:T(8,128)} copy(f32[128,1,72,128]{3,0,2,1:T(8,128)S(1)} %maximum_bitcast_fusion) | data formatting | bytes 9437184 | tf_op jit(solution)/shard_map/reshape | solution.py:256
  279.9 5.1 %all-to-all-start.2 = ((f32[128,1,72,128]{3,2,1,0:T(8,128)}), f32[128,1,72,128]{3,2,1,0:T(8,128)}, u32[]{:S(2)}, u32[]{:S(2)}) async-start(f32[128,1,72,128]{3,2,1,0:T(8,128)} %copy.15), calls=%async_computation.2 | async-start | bytes 9437184 | tf_op jit(solution)/shard_map/all_to_all | solution.py:257
  285.8 49.5 %all-to-all-done.2 = f32[128,1,72,128]{3,2,1,0:T(8,128)} async-done(((f32[128,1,72,128]{3,2,1,0:T(8,128)}), f32[128,1,72,128]{3,2,1,0:T(8,128)}, u32[]{:S(2)}, u32[]{:S(2)}) %all-to-all-start.2) | async-done | bytes 4718624 | tf_op jit(solution)/shard_map/all_to_all | solution.py:257
  335.3 5.1 %copy.16 = f32[32,4,1,72,128]{4,3,1,0,2:T(8,128)} copy(f32[32,4,1,72,128]{4,3,0,1,2:T(8,128)} %bitcast.18) | data formatting | bytes 9437184 | tf_op jit(solution)/shard_map/all_to_all | solution.py:257
  (77 shorter events, 39.6 us)
Async XLA Ops:
  0.6 59.0 %collective-permute-start.1 = (f32[32,6,48,128]{3,2,1,0:T(8,128)}, f32[32,6,48,128]{3,2,1,0:T(8,128)}, u32[]{:S(2)}, u32[]{:S(2)}) collective-permute-start(f32[32,6,48,128]{3,2,1,0:T(8,128)} %refs_4_.3), channel_id=1, source_target_pairs={{4,0},{8,4},{12,8},{16,12},{20,16},{24,20},{28,24},{32,28},{36,32}... | collective-permute-start | bytes 14155784 | tf_op jit(solution)/shard_map/ppermute | solution.py:31
  1.9 57.7 %collective-permute-start = (f32[32,6,48,128]{3,2,1,0:T(8,128)}, f32[32,6,48,128]{3,2,1,0:T(8,128)}, u32[]{:S(2)}, u32[]{:S(2)}) collective-permute-start(f32[32,6,48,128]{3,2,1,0:T(8,128)} %refs_4_.3), channel_id=1, source_target_pairs={{0,4},{4,8},{8,12},{12,16},{16,20},{20,24},{24,28},{28,32},{32,36}... | collective-permute-start | bytes 14155784 | tf_op jit(solution)/shard_map/ppermute | solution.py:30
  65.8 10.3 %copy-start.4 = (f32[6,48,128]{2,1,0:T(8,128)S(1)}, f32[6,48,128]{2,1,0:T(8,128)}, u32[]{:S(2)}) copy-start(f32[6,48,128]{2,1,0:T(8,128)} %param.3) | copy-start | bytes 442372
  65.8 41.0 %collective-permute-start.2 = (f32[16,6,48,128]{3,2,1,0:T(8,128)}, f32[16,6,48,128]{3,2,1,0:T(8,128)}, u32[]{:S(2)}, u32[]{:S(2)}) collective-permute-start(f32[16,6,48,128]{3,2,1,0:T(8,128)} %shard_map.41.refs_1_), channel_id=1, source_target_pairs={{0,4},{4,8},{8,12},{12,16},{16,20},{20,24},{24,28},{28,32},{32,36}... | collective-permute-start | bytes 7077896 | tf_op jit(solution)/shard_map/ppermute | solution.py:30
  68.6 38.2 %collective-permute-start.3 = (f32[16,6,48,128]{3,2,1,0:T(8,128)}, f32[16,6,48,128]{3,2,1,0:T(8,128)}, u32[]{:S(2)}, u32[]{:S(2)}) collective-permute-start(f32[16,6,48,128]{3,2,1,0:T(8,128)} %shard_map.41.refs_1_), channel_id=1, source_target_pairs={{4,0},{8,4},{12,8},{16,12},{20,16},{24,20},{28,24},{32,28},{36,32}... | collective-permute-start | bytes 7077896 | tf_op jit(solution)/shard_map/ppermute | solution.py:31
  76.1 30.7 %copy-start.2 = (f32[16,6,48,128]{3,2,1,0:T(8,128)S(1)}, f32[16,6,48,128]{3,2,1,0:T(8,128)}, u32[]{:S(2)}) copy-start(f32[16,6,48,128]{3,2,1,0:T(8,128)} %shard_map.42.refs_1_) | copy-start | bytes 7077892
  106.8 29.7 %collective-permute-start.4 = (f32[16,6,48,128]{3,2,1,0:T(8,128)S(1)}, f32[16,6,48,128]{3,2,1,0:T(8,128)}, u32[]{:S(2)}, u32[]{:S(2)}) collective-permute-start(f32[16,6,48,128]{3,2,1,0:T(8,128)S(1)} %copy-done.2), channel_id=1, source_target_pairs={{0,4},{4,8},{8,12},{12,16},{16,20},{20,24},{24,28},{28,32},{32,36}... | collective-permute-start | bytes 7077896 | tf_op jit(solution)/shard_map/ppermute | solution.py:30
  111.3 25.2 %collective-permute-start.5 = (f32[16,6,48,128]{3,2,1,0:T(8,128)S(1)}, f32[16,6,48,128]{3,2,1,0:T(8,128)}, u32[]{:S(2)}, u32[]{:S(2)}) collective-permute-start(f32[16,6,48,128]{3,2,1,0:T(8,128)S(1)} %copy-done.2), channel_id=1, source_target_pairs={{4,0},{8,4},{12,8},{16,12},{20,16},{24,20},{28,24},{32,28},{36,32}... | collective-permute-start | bytes 7077896 | tf_op jit(solution)/shard_map/ppermute | solution.py:31
  122.6 36.0 %all-to-all-start = ((f32[16,4,72,128]{3,2,0,1:T(8,128)}), f32[16,4,72,128]{3,2,0,1:T(8,128)}, u32[]{:S(2)}, u32[]{:S(2)}) async-start(f32[16,4,72,128]{3,2,0,1:T(8,128)} %copy.9), calls=%async_computation | async-start | bytes 4718592 | tf_op jit(solution)/shard_map/all_to_all | solution.py:107
  201.1 1.3 collective-permute-start.6
  202.4 5.2 %collective-permute-start.9 = (f32[64,128]{1,0:T(8,128)S(1)}, f32[64,128]{1,0:T(8,128)S(1)}, u32[]{:S(2)}, u32[]{:S(2)}) collective-permute-start(f32[64,128]{1,0:T(8,128)S(1)} %select_add_fusion.5), channel_id=1, source_target_pairs={{0,8},{4,12},{8,16},{12,20},{16,24},{20,28},{24,0},{28,4},{32,40},... | collective-permute-start | bytes 98312 | tf_op jit(solution)/shard_map/ppermute | solution.py:149
  202.5 7.0 %collective-permute-start.8 = (f32[64,128]{1,0:T(8,128)S(1)}, f32[64,128]{1,0:T(8,128)S(1)}, u32[]{:S(2)}, u32[]{:S(2)}) collective-permute-start(f32[64,128]{1,0:T(8,128)S(1)} %select_add_fusion.5), channel_id=1, source_target_pairs={{0,16},{4,20},{8,24},{12,28},{16,0},{20,4},{24,8},{28,12},{32,48},... | collective-permute-start | bytes 98312 | tf_op jit(solution)/shard_map/ppermute | solution.py:149
  207.1 3.9 %collective-permute-start.7 = (f32[64,128]{1,0:T(8,128)S(1)}, f32[64,128]{1,0:T(8,128)S(1)}, u32[]{:S(2)}, u32[]{:S(2)}) collective-permute-start(f32[64,128]{1,0:T(8,128)S(1)} %select_add_fusion.5), channel_id=1, source_target_pairs={{0,24},{4,28},{8,0},{12,4},{16,8},{20,12},{24,16},{28,20},{32,56},... | collective-permute-start | bytes 98312 | tf_op jit(solution)/shard_map/ppermute | solution.py:149
  211.1 5.7 %collective-permute-start.12 = (f32[64,128]{1,0:T(8,128)S(1)}, f32[64,128]{1,0:T(8,128)S(1)}, u32[]{:S(2)}, u32[]{:S(2)}) collective-permute-start(f32[64,128]{1,0:T(8,128)S(1)} %select_add_fusion.4), channel_id=1, source_target_pairs={{0,32},{4,36},{8,40},{12,44},{16,48},{20,52},{24,56},{28,60},{32,6... | collective-permute-start | bytes 98312 | tf_op jit(solution)/shard_map/ppermute | solution.py:149
  212.6 5.4 %collective-permute-start.11 = (f32[64,128]{1,0:T(8,128)S(1)}, f32[64,128]{1,0:T(8,128)S(1)}, u32[]{:S(2)}, u32[]{:S(2)}) collective-permute-start(f32[64,128]{1,0:T(8,128)S(1)} %select_add_fusion.4), channel_id=1, source_target_pairs={{0,64},{4,68},{8,72},{12,76},{16,80},{20,84},{24,88},{28,92},{32,9... | collective-permute-start | bytes 98312 | tf_op jit(solution)/shard_map/ppermute | solution.py:149
  215.2 3.9 %collective-permute-start.10 = (f32[64,128]{1,0:T(8,128)S(1)}, f32[64,128]{1,0:T(8,128)S(1)}, u32[]{:S(2)}, u32[]{:S(2)}) collective-permute-start(f32[64,128]{1,0:T(8,128)S(1)} %select_add_fusion.4), channel_id=1, source_target_pairs={{0,96},{4,100},{8,104},{12,108},{16,112},{20,116},{24,120},{28,124... | collective-permute-start | bytes 98312 | tf_op jit(solution)/shard_map/ppermute | solution.py:149
  219.1 7.1 %collective-permute-start.15 = (f32[64,128]{1,0:T(8,128)S(1)}, f32[64,128]{1,0:T(8,128)S(1)}, u32[]{:S(2)}, u32[]{:S(2)}) collective-permute-start(f32[64,128]{1,0:T(8,128)S(1)} %select_add_fusion.3), channel_id=1, source_target_pairs={{0,1},{1,2},{2,3},{3,0},{4,5},{5,6},{6,7},{7,4},{8,9},{9,10},{10,1... | collective-permute-start | bytes 98312 | tf_op jit(solution)/shard_map/ppermute | solution.py:149
  219.8 6.4 %collective-permute-start.14 = (f32[64,128]{1,0:T(8,128)S(1)}, f32[64,128]{1,0:T(8,128)S(1)}, u32[]{:S(2)}, u32[]{:S(2)}) collective-permute-start(f32[64,128]{1,0:T(8,128)S(1)} %select_add_fusion.3), channel_id=1, source_target_pairs={{0,2},{1,3},{2,0},{3,1},{4,6},{5,7},{6,4},{7,5},{8,10},{9,11},{10,... | collective-permute-start | bytes 98312 | tf_op jit(solution)/shard_map/ppermute | solution.py:149
  221.8 4.4 %collective-permute-start.13 = (f32[64,128]{1,0:T(8,128)S(1)}, f32[64,128]{1,0:T(8,128)S(1)}, u32[]{:S(2)}, u32[]{:S(2)}) collective-permute-start(f32[64,128]{1,0:T(8,128)S(1)} %select_add_fusion.3), channel_id=1, source_target_pairs={{0,3},{1,0},{2,1},{3,2},{4,7},{5,4},{6,5},{7,6},{8,11},{9,8},{10,9... | collective-permute-start | bytes 98312 | tf_op jit(solution)/shard_map/ppermute | solution.py:149
  239.8 1.3 collective-permute-start.16
  241.0 5.8 %collective-permute-start.19 = (f32[64,64]{1,0:T(8,128)S(1)}, f32[64,64]{1,0:T(8,128)S(1)}, u32[]{:S(2)}, u32[]{:S(2)}) collective-permute-start(f32[64,64]{1,0:T(8,128)S(1)} %select_add_fusion.2), channel_id=1, source_target_pairs={{0,8},{4,12},{8,16},{12,20},{16,24},{20,28},{24,0},{28,4},{32,40},... | collective-permute-start | bytes 49160 | tf_op jit(solution)/shard_map/ppermute | solution.py:149
  241.6 5.9 %collective-permute-start.18 = (f32[64,64]{1,0:T(8,128)S(1)}, f32[64,64]{1,0:T(8,128)S(1)}, u32[]{:S(2)}, u32[]{:S(2)}) collective-permute-start(f32[64,64]{1,0:T(8,128)S(1)} %select_add_fusion.2), channel_id=1, source_target_pairs={{0,16},{4,20},{8,24},{12,28},{16,0},{20,4},{24,8},{28,12},{32,48},... | collective-permute-start | bytes 49160 | tf_op jit(solution)/shard_map/ppermute | solution.py:149
  245.3 3.9 %collective-permute-start.17 = (f32[64,64]{1,0:T(8,128)S(1)}, f32[64,64]{1,0:T(8,128)S(1)}, u32[]{:S(2)}, u32[]{:S(2)}) collective-permute-start(f32[64,64]{1,0:T(8,128)S(1)} %select_add_fusion.2), channel_id=1, source_target_pairs={{0,24},{4,28},{8,0},{12,4},{16,8},{20,12},{24,16},{28,20},{32,56},... | collective-permute-start | bytes 49160 | tf_op jit(solution)/shard_map/ppermute | solution.py:149
  249.2 5.2 %collective-permute-start.22 = (f32[64,64]{1,0:T(8,128)S(1)}, f32[64,64]{1,0:T(8,128)S(1)}, u32[]{:S(2)}, u32[]{:S(2)}) collective-permute-start(f32[64,64]{1,0:T(8,128)S(1)} %select_add_fusion.1), channel_id=1, source_target_pairs={{0,32},{4,36},{8,40},{12,44},{16,48},{20,52},{24,56},{28,60},{32,6... | collective-permute-start | bytes 49160 | tf_op jit(solution)/shard_map/ppermute | solution.py:149
  249.3 5.5 %collective-permute-start.21 = (f32[64,64]{1,0:T(8,128)S(1)}, f32[64,64]{1,0:T(8,128)S(1)}, u32[]{:S(2)}, u32[]{:S(2)}) collective-permute-start(f32[64,64]{1,0:T(8,128)S(1)} %select_add_fusion.1), channel_id=1, source_target_pairs={{0,64},{4,68},{8,72},{12,76},{16,80},{20,84},{24,88},{28,92},{32,9... | collective-permute-start | bytes 49160 | tf_op jit(solution)/shard_map/ppermute | solution.py:149
  252.3 3.9 %collective-permute-start.20 = (f32[64,64]{1,0:T(8,128)S(1)}, f32[64,64]{1,0:T(8,128)S(1)}, u32[]{:S(2)}, u32[]{:S(2)}) collective-permute-start(f32[64,64]{1,0:T(8,128)S(1)} %select_add_fusion.1), channel_id=1, source_target_pairs={{0,96},{4,100},{8,104},{12,108},{16,112},{20,116},{24,120},{28,124... | collective-permute-start | bytes 49160 | tf_op jit(solution)/shard_map/ppermute | solution.py:149
  256.3 5.4 %collective-permute-start.25 = (f32[64,64]{1,0:T(8,128)S(1)}, f32[64,64]{1,0:T(8,128)S(1)}, u32[]{:S(2)}, u32[]{:S(2)}) collective-permute-start(f32[64,64]{1,0:T(8,128)S(1)} %select_add_fusion), channel_id=1, source_target_pairs={{0,1},{1,2},{2,3},{3,0},{4,5},{5,6},{6,7},{7,4},{8,9},{9,10},{10,1... | collective-permute-start | bytes 49160 | tf_op jit(solution)/shard_map/ppermute | solution.py:149
  257.5 5.4 %collective-permute-start.24 = (f32[64,64]{1,0:T(8,128)S(1)}, f32[64,64]{1,0:T(8,128)S(1)}, u32[]{:S(2)}, u32[]{:S(2)}) collective-permute-start(f32[64,64]{1,0:T(8,128)S(1)} %select_add_fusion), channel_id=1, source_target_pairs={{0,2},{1,3},{2,0},{3,1},{4,6},{5,7},{6,4},{7,5},{8,10},{9,11},{10,... | collective-permute-start | bytes 49160 | tf_op jit(solution)/shard_map/ppermute | solution.py:149
  259.7 3.9 %collective-permute-start.23 = (f32[64,64]{1,0:T(8,128)S(1)}, f32[64,64]{1,0:T(8,128)S(1)}, u32[]{:S(2)}, u32[]{:S(2)}) collective-permute-start(f32[64,64]{1,0:T(8,128)S(1)} %select_add_fusion), channel_id=1, source_target_pairs={{0,3},{1,0},{2,1},{3,2},{4,7},{5,4},{6,5},{7,6},{8,11},{9,8},{10,9... | collective-permute-start | bytes 49160 | tf_op jit(solution)/shard_map/ppermute | solution.py:149
  279.9 5.1 %slice-start = ((f32[64,192]{1,0:T(8,128)}), f32[64,128]{1,0:T(8,128)S(1)}, s32[]{:S(2)}) async-start(f32[64,192]{1,0:T(8,128)} %shard_map.45), calls=%async_computation.3 | async-start | bytes 65536 | tf_op jit(solution)/shard_map/concatenate | solution.py:222
  279.9 5.1 %copy-start.6 = (f32[64,128]{1,0:T(8,128)S(1)}, f32[64,128]{1,0:T(8,128)}, u32[]{:S(2)}) copy-start(f32[64,128]{1,0:T(8,128)} %shard_map.46) | copy-start | bytes 98308
  279.9 55.3 %all-to-all-start.2 = ((f32[128,1,72,128]{3,2,1,0:T(8,128)}), f32[128,1,72,128]{3,2,1,0:T(8,128)}, u32[]{:S(2)}, u32[]{:S(2)}) async-start(f32[128,1,72,128]{3,2,1,0:T(8,128)} %copy.15), calls=%async_computation.2 | async-start | bytes 9437184 | tf_op jit(solution)/shard_map/all_to_all | solution.py:257
  (4 other events, 7.5 us)
where the time goes:
time: 341 us; the launch traced here: 340 us
  other arithmetic  99.8 us (29%)
  waiting for transfers between devices  78.6 us (23%)
  starting transfers between devices  55 us (16%)
  Pallas kernels  42.3 us (12%)
  blocking collectives  33.2 us (10%)
  local copies, waits for them, and re-layouts  21.4 us (6%)
  matrix products  9.05 us (3%)
    add x3, other arithmetic, local_terms(): return -2.0 * total + potential[None] * orbital_field  91.7 us
    all_to_all x1, waiting for transfers between devices, local(): orbitals = lax.all_to_all(orbitals, 'orb', 0, 1, tiled=True)  49.5 us
    all_to_all x1, blocking collectives, spread_cells(): lax.all_to_all(chunks, 'orb', 1, 0, tiled=True)  33.2 us
    ppermute x20, starting transfers between devices, group_round(): received.append(lax.ppermute(value, axis, pairs))  28.1 us
    pallas_call x4, Pallas kernels, filter_step(): pl.pallas_call(functools.partial(combine_kernel, scale, base is not None)...  25.9 us
    ppermute x20, waiting for transfers between devices, group_round(): received.append(lax.ppermute(value, axis, pairs))  17 us
    pallas_call x2, Pallas kernels, eliminate(): pl.pallas_call(eliminate_kernel, out_shape=jax.ShapeDtypeStruct(source.sh...  16.4 us
    ppermute x3, starting transfers between devices, halo_planes(): before = lax.ppermute(last, axis, up)  12.5 us
  transfers between devices with their start and end apart: 28, of which 17 were waited for; matrix products, arithmetic and copies ran while one was open for 30% of the time, Pallas kernels for 6%

commit v1 on v0

--- a/solution.py
+++ b/solution.py
@@ -77,7 +77,7 @@
 
 def filter_step(local, orbital_field, before, after, scale, base=None, start=0, count=None, base_start=0):
     count = orbital_field.shape[0] if count is None else count
-    block_rows = 4 if count % 4 == 0 and start % 4 == 0 and base_start % 4 == 0 else 1
+    block_rows = 8 if count % 8 == 0 and start % 8 == 0 and base_start % 8 == 0 else 1
     offset = start // block_rows
     base_offset = base_start // block_rows
     block = (block_rows,) + orbital_field.shape[1:]
@@ -185,10 +185,10 @@
     def column_step(column, carry):
         current = result_ref[pl.ds(column, 1), :]
         pivot_value = jnp.sum(jnp.where(lanes == column, current, 0.0), axis=1, keepdims=True)
-        root = jnp.sqrt(pivot_value)
-        scaled = jnp.where(lanes >= column, current, 0.0) / root
+        inv_root = 1.0 / jnp.sqrt(pivot_value)
+        scaled = jnp.where(lanes >= column, current, 0.0) * inv_root
         whole = result_ref[...]
-        below = jnp.sum(jnp.where(cols == column, whole, 0.0), axis=1, keepdims=True) / root
+        below = jnp.sum(jnp.where(cols == column, whole, 0.0), axis=1, keepdims=True) * inv_root
         below = jnp.where(row_ids > column, below, 0.0)
         whole = whole - below * scaled
         result_ref[...] = jnp.where(row_ids == column, scaled, whole)

time: 341 us -> 340 us (level)
  transfers between devices with their start and end apart: 28 -> 28, of which waited for: 17 -> 17; matrix products, arithmetic and copies ran while one was open for 30% -> 30% of each run, Pallas kernels for 6% -> 5%
where the time goes in v1:
time: 340 us; the launch traced here: 339 us
  other arithmetic  99.8 us (29%)
  waiting for transfers between devices  78.9 us (23%)
  starting transfers between devices  54.8 us (16%)
  Pallas kernels  40.4 us (12%)
  blocking collectives  33.3 us (10%)
  local copies, waits for them, and re-layouts  21.4 us (6%)
  matrix products  9.06 us (3%)
    add x3, other arithmetic, local_terms(): return -2.0 * total + potential[None] * orbital_field  91.7 us
    all_to_all x1, waiting for transfers between devices, local(): orbitals = lax.all_to_all(orbitals, 'orb', 0, 1, tiled=True)  49.5 us
    all_to_all x1, blocking collectives, spread_cells(): lax.all_to_all(chunks, 'orb', 1, 0, tiled=True)  33.3 us
    ppermute x20, starting transfers between devices, group_round(): received.append(lax.ppermute(value, axis, pairs))  28 us
    pallas_call x4, Pallas kernels, filter_step(): pl.pallas_call(functools.partial(combine_kernel, scale, base is not None)...  24 us
    ppermute x20, waiting for transfers between devices, group_round(): received.append(lax.ppermute(value, axis, pairs))  17 us
    pallas_call x2, Pallas kernels, eliminate(): pl.pallas_call(eliminate_kernel, out_shape=jax.ShapeDtypeStruct(source.sh...  16.4 us
    ppermute x3, starting transfers between devices, halo_planes(): before = lax.ppermute(last, axis, up)  12.5 us
  transfers between devices with their start and end apart: 28, of which 17 were waited for; matrix products, arithmetic and copies ran while one was open for 30% of the time, Pallas kernels for 5%

profile of v1, /device:TPU:0, one launch (start us, length us, event | category | flops | bytes accessed | tf_op | source)
XLA Modules:
  0.0 338.7 jit_solution(4930010687015633277)
XLA Ops:
  1.9 5.2 %collective-permute-start = (f32[32,6,48,128]{3,2,1,0:T(8,128)}, f32[32,6,48,128]{3,2,1,0:T(8,128)}, u32[]{:S(2)}, u32[]{:S(2)}) collective-permute-start(f32[32,6,48,128]{3,2,1,0:T(8,128)} %refs_4_.3), channel_id=1, source_target_pairs={{0,4},{4,8},{8,12},{12,16},{16,20},{20,24},{24,28},{28,32},{32,36}... | collective-permute-start | bytes 14155784 | tf_op jit(solution)/shard_map/ppermute | solution.py:30
  7.1 52.5 %multiply_add_fusion.refs_0_ = f32[32,6,48,128]{3,2,1,0:T(8,128)} fusion(f32[32,6,48,128]{3,2,1,0:T(8,128)} %refs_4_.3, f32[6,48,128]{2,1,0:T(8,128)} %param.3), kind=kLoop, calls=%fused_computation.114 | loop fusion | flops 47185920 | bytes 9584640 | tf_op jit(solution)/shard_map/add | solution.py:49
  59.6 5.6 %shard_map.41.refs_1_ = f32[16,6,48,128]{3,2,1,0:T(8,128)} custom-call(f32[32,6,48,128]{3,2,1,0:T(8,128)} %multiply_add_fusion.refs_0_, f32[32,6,48,128]{3,2,1,0:T(8,128)} %refs_4_.3, f32[32,6,48,128]{3,2,1,0:T(8,128)} %collective-permute-done.refs_2_, f32[32,6,48,128]{3,2,1,0:T(8,128)} %collective-permute-done.1.refs_3_), custom_call_target="tpu_custom_call" | custom-call | tf_op jit(solution)/shard_map/pallas_call | solution.py:92
  65.3 2.8 collective-permute-start.2
  69.4 5.6 %shard_map.42.refs_1_ = f32[16,6,48,128]{3,2,1,0:T(8,128)} custom-call(f32[32,6,48,128]{3,2,1,0:T(8,128)} %multiply_add_fusion.refs_0_, f32[32,6,48,128]{3,2,1,0:T(8,128)} %refs_4_.3, f32[32,6,48,128]{3,2,1,0:T(8,128)} %collective-permute-done.refs_2_, f32[32,6,48,128]{3,2,1,0:T(8,128)} %collective-permute-done.1.refs_3_), custom_call_target="tpu_custom_call" | custom-call | tf_op jit(solution)/shard_map/pallas_call | solution.py:92
  75.0 30.7 %multiply_add_fusion.2.refs_0_ = f32[16,6,48,128]{3,2,1,0:T(8,128)} fusion(f32[16,6,48,128]{3,2,1,0:T(8,128)} %shard_map.41.refs_1_, f32[6,48,128]{2,1,0:T(8,128)S(1)} %copy-done.4), kind=kLoop, calls=%fused_computation.191 | loop fusion | flops 23592960 | bytes 4866048 | tf_op jit(solution)/shard_map/add | solution.py:49
  105.7 4.5 %collective-permute-start.4 = (f32[16,6,48,128]{3,2,1,0:T(8,128)S(1)}, f32[16,6,48,128]{3,2,1,0:T(8,128)}, u32[]{:S(2)}, u32[]{:S(2)}) collective-permute-start(f32[16,6,48,128]{3,2,1,0:T(8,128)S(1)} %copy-done.2), channel_id=1, source_target_pairs={{0,4},{4,8},{8,12},{12,16},{16,20},{20,24},{24,28},{28,32},{32,36}... | collective-permute-start | bytes 7077896 | tf_op jit(solution)/shard_map/ppermute | solution.py:30
  111.5 6.4 %shard_map.43 = f32[16,6,48,128]{3,2,1,0:T(8,128)} custom-call(f32[16,6,48,128]{3,2,1,0:T(8,128)} %multiply_add_fusion.2.refs_0_, f32[16,6,48,128]{3,2,1,0:T(8,128)} %shard_map.41.refs_1_, f32[16,6,48,128]{3,2,1,0:T(8,128)} %collective-permute-done.2.refs_2_, f32[16,6,48,128]{3,2,1,0:T(8,128)} %collective-permute-done.3.refs_3_, f32[32,6,48,128]{3,2,1,0:T(8,128)} %refs_4_.3), custom_call_target="tpu_custom_call" | custom-call | tf_op jit(solution)/shard_map/pallas_call | solution.py:92
  117.8 3.2 copy.9
  121.0 5.4 %all-to-all-start = ((f32[16,4,72,128]{3,2,0,1:T(8,128)}), f32[16,4,72,128]{3,2,0,1:T(8,128)}, u32[]{:S(2)}, u32[]{:S(2)}) async-start(f32[16,4,72,128]{3,2,0,1:T(8,128)} %copy.9), calls=%async_computation | async-start | bytes 4718592 | tf_op jit(solution)/shard_map/all_to_all | solution.py:107
  126.5 8.5 %multiply_add_fusion.1.refs_0_ = f32[16,6,48,128]{3,2,1,0:T(8,128)} fusion(f32[16,6,48,128]{3,2,1,0:T(8,128)S(1)} %copy-done.2, f32[6,48,128]{2,1,0:T(8,128)S(1)} %copy-done.4), kind=kLoop, calls=%fused_computation.190 | loop fusion | flops 23592960 | bytes 4866048 | tf_op jit(solution)/shard_map/add | solution.py:49
  135.0 6.4 %shard_map.44 = f32[16,6,48,128]{3,2,1,0:T(8,128)} custom-call(f32[16,6,48,128]{3,2,1,0:T(8,128)} %multiply_add_fusion.1.refs_0_, f32[16,6,48,128]{3,2,1,0:T(8,128)} %shard_map.42.refs_1_, f32[16,6,48,128]{3,2,1,0:T(8,128)} %collective-permute-done.4.refs_2_, f32[16,6,48,128]{3,2,1,0:T(8,128)} %collective-permute-done.5.refs_3_, f32[32,6,48,128]{3,2,1,0:T(8,128)} %refs_4_.3), custom_call_target="tpu_custom_call" | custom-call | tf_op jit(solution)/shard_map/pallas_call | solution.py:92
  141.4 3.2 copy.10
  144.6 12.4 %all-to-all-done = f32[16,4,72,128]{3,2,0,1:T(8,128)} async-done(((f32[16,4,72,128]{3,2,0,1:T(8,128)}), f32[16,4,72,128]{3,2,0,1:T(8,128)}, u32[]{:S(2)}, u32[]{:S(2)}) %all-to-all-start) | async-done | bytes 2359328 | tf_op jit(solution)/shard_map/all_to_all | solution.py:107
  157.0 33.3 %all_to_all.45 = f32[16,4,72,128]{3,2,0,1:T(8,128)S(1)} all-to-all(f32[16,4,72,128]{3,2,0,1:T(8,128)} %copy.10), channel_id=1, replica_groups=mesh['grid'=32,'orb'=4] {'orb'}, dimensions={1} | all-to-all | bytes 4718592 | tf_op jit(solution)/shard_map/all_to_all | solution.py:107
  190.3 2.0 pad_maximum_fusion
  192.3 3.4 fusion.36
  197.1 2.6 convolution_bitcast_fusion.1
  201.0 4.4 %collective-permute-start.8 = (f32[64,128]{1,0:T(8,128)S(1)}, f32[64,128]{1,0:T(8,128)S(1)}, u32[]{:S(2)}, u32[]{:S(2)}) collective-permute-start(f32[64,128]{1,0:T(8,128)S(1)} %select_add_fusion.5), channel_id=1, source_target_pairs={{0,16},{4,20},{8,24},{12,28},{16,0},{20,4},{24,8},{28,12},{32,48},... | collective-permute-start | bytes 98312 | tf_op jit(solution)/shard_map/ppermute | solution.py:149
  210.9 3.1 collective-permute-start.11
  218.6 2.1 collective-permute-start.14
  221.5 3.5 %copy.13 = f32[2,2,16,72,128]{4,2,1,0,3:T(8,128)} copy(f32[2,2,16,72,128]{4,3,2,0,1:T(8,128)} %get-tuple-element.23) | data formatting | bytes 4718592 | tf_op jit(solution)/shard_map/slice | solution.py:217
  225.7 8.4 %shard_map.45 = f32[64,192]{1,0:T(8,128)} custom-call(f32[64,192]{1,0:T(8,128)} %pad_maximum_fusion.1.source_ref), custom_call_target="tpu_custom_call" | custom-call | tf_op jit(solution)/shard_map/pallas_call | solution.py:202
  240.2 3.6 %collective-permute-start.18 = (f32[64,64]{1,0:T(8,128)S(1)}, f32[64,64]{1,0:T(8,128)S(1)}, u32[]{:S(2)}, u32[]{:S(2)}) collective-permute-start(f32[64,64]{1,0:T(8,128)S(1)} %select_add_fusion.2), channel_id=1, source_target_pairs={{0,16},{4,20},{8,24},{12,28},{16,0},{20,4},{24,8},{28,12},{32,48},... | collective-permute-start | bytes 49160 | tf_op jit(solution)/shard_map/ppermute | solution.py:149
  247.9 2.8 collective-permute-start.21
  255.9 2.2 collective-permute-start.24
  262.7 8.0 %shard_map.46 = f32[64,128]{1,0:T(8,128)} custom-call(f32[64,128]{1,0:T(8,128)} %pad_maximum_fusion.2.source_ref), custom_call_target="tpu_custom_call" | custom-call | tf_op jit(solution)/shard_map/pallas_call | solution.py:202
  270.7 2.1 fusion.110
  273.4 4.9 %copy.15 = f32[128,1,72,128]{3,2,1,0:T(8,128)} copy(f32[128,1,72,128]{3,0,2,1:T(8,128)S(1)} %maximum_bitcast_fusion) | data formatting | bytes 9437184 | tf_op jit(solution)/shard_map/reshape | solution.py:256
  278.3 5.1 %all-to-all-start.2 = ((f32[128,1,72,128]{3,2,1,0:T(8,128)}), f32[128,1,72,128]{3,2,1,0:T(8,128)}, u32[]{:S(2)}, u32[]{:S(2)}) async-start(f32[128,1,72,128]{3,2,1,0:T(8,128)} %copy.15), calls=%async_computation.2 | async-start | bytes 9437184 | tf_op jit(solution)/shard_map/all_to_all | solution.py:257
  284.1 49.5 %all-to-all-done.2 = f32[128,1,72,128]{3,2,1,0:T(8,128)} async-done(((f32[128,1,72,128]{3,2,1,0:T(8,128)}), f32[128,1,72,128]{3,2,1,0:T(8,128)}, u32[]{:S(2)}, u32[]{:S(2)}) %all-to-all-start.2) | async-done | bytes 4718624 | tf_op jit(solution)/shard_map/all_to_all | solution.py:257
  333.6 5.1 %copy.16 = f32[32,4,1,72,128]{4,3,1,0,2:T(8,128)} copy(f32[32,4,1,72,128]{4,3,0,1,2:T(8,128)} %bitcast.18) | data formatting | bytes 9437184 | tf_op jit(solution)/shard_map/all_to_all | solution.py:257
  (77 shorter events, 39.4 us)
Async XLA Ops:
  0.6 59.0 %collective-permute-start.1 = (f32[32,6,48,128]{3,2,1,0:T(8,128)}, f32[32,6,48,128]{3,2,1,0:T(8,128)}, u32[]{:S(2)}, u32[]{:S(2)}) collective-permute-start(f32[32,6,48,128]{3,2,1,0:T(8,128)} %refs_4_.3), channel_id=1, source_target_pairs={{4,0},{8,4},{12,8},{16,12},{20,16},{24,20},{28,24},{32,28},{36,32}... | collective-permute-start | bytes 14155784 | tf_op jit(solution)/shard_map/ppermute | solution.py:31
  1.9 57.7 %collective-permute-start = (f32[32,6,48,128]{3,2,1,0:T(8,128)}, f32[32,6,48,128]{3,2,1,0:T(8,128)}, u32[]{:S(2)}, u32[]{:S(2)}) collective-permute-start(f32[32,6,48,128]{3,2,1,0:T(8,128)} %refs_4_.3), channel_id=1, source_target_pairs={{0,4},{4,8},{8,12},{12,16},{16,20},{20,24},{24,28},{28,32},{32,36}... | collective-permute-start | bytes 14155784 | tf_op jit(solution)/shard_map/ppermute | solution.py:30
  65.3 9.7 %copy-start.4 = (f32[6,48,128]{2,1,0:T(8,128)S(1)}, f32[6,48,128]{2,1,0:T(8,128)}, u32[]{:S(2)}) copy-start(f32[6,48,128]{2,1,0:T(8,128)} %param.3) | copy-start | bytes 442372
  65.3 40.4 %collective-permute-start.2 = (f32[16,6,48,128]{3,2,1,0:T(8,128)}, f32[16,6,48,128]{3,2,1,0:T(8,128)}, u32[]{:S(2)}, u32[]{:S(2)}) collective-permute-start(f32[16,6,48,128]{3,2,1,0:T(8,128)} %shard_map.41.refs_1_), channel_id=1, source_target_pairs={{0,4},{4,8},{8,12},{12,16},{16,20},{20,24},{24,28},{28,32},{32,36}... | collective-permute-start | bytes 7077896 | tf_op jit(solution)/shard_map/ppermute | solution.py:30
  68.1 37.6 %collective-permute-start.3 = (f32[16,6,48,128]{3,2,1,0:T(8,128)}, f32[16,6,48,128]{3,2,1,0:T(8,128)}, u32[]{:S(2)}, u32[]{:S(2)}) collective-permute-start(f32[16,6,48,128]{3,2,1,0:T(8,128)} %shard_map.41.refs_1_), channel_id=1, source_target_pairs={{4,0},{8,4},{12,8},{16,12},{20,16},{24,20},{28,24},{32,28},{36,32}... | collective-permute-start | bytes 7077896 | tf_op jit(solution)/shard_map/ppermute | solution.py:31
  75.0 30.7 %copy-start.2 = (f32[16,6,48,128]{3,2,1,0:T(8,128)S(1)}, f32[16,6,48,128]{3,2,1,0:T(8,128)}, u32[]{:S(2)}) copy-start(f32[16,6,48,128]{3,2,1,0:T(8,128)} %shard_map.42.refs_1_) | copy-start | bytes 7077892
  105.7 29.2 %collective-permute-start.4 = (f32[16,6,48,128]{3,2,1,0:T(8,128)S(1)}, f32[16,6,48,128]{3,2,1,0:T(8,128)}, u32[]{:S(2)}, u32[]{:S(2)}) collective-permute-start(f32[16,6,48,128]{3,2,1,0:T(8,128)S(1)} %copy-done.2), channel_id=1, source_target_pairs={{0,4},{4,8},{8,12},{12,16},{16,20},{20,24},{24,28},{28,32},{32,36}... | collective-permute-start | bytes 7077896 | tf_op jit(solution)/shard_map/ppermute | solution.py:30
  110.2 24.8 %collective-permute-start.5 = (f32[16,6,48,128]{3,2,1,0:T(8,128)S(1)}, f32[16,6,48,128]{3,2,1,0:T(8,128)}, u32[]{:S(2)}, u32[]{:S(2)}) collective-permute-start(f32[16,6,48,128]{3,2,1,0:T(8,128)S(1)} %copy-done.2), channel_id=1, source_target_pairs={{4,0},{8,4},{12,8},{16,12},{20,16},{24,20},{28,24},{32,28},{36,32}... | collective-permute-start | bytes 7077896 | tf_op jit(solution)/shard_map/ppermute | solution.py:31
  121.0 36.0 %all-to-all-start = ((f32[16,4,72,128]{3,2,0,1:T(8,128)}), f32[16,4,72,128]{3,2,0,1:T(8,128)}, u32[]{:S(2)}, u32[]{:S(2)}) async-start(f32[16,4,72,128]{3,2,0,1:T(8,128)} %copy.9), calls=%async_computation | async-start | bytes 4718592 | tf_op jit(solution)/shard_map/all_to_all | solution.py:107
  199.6 1.3 collective-permute-start.6
  200.9 5.2 %collective-permute-start.9 = (f32[64,128]{1,0:T(8,128)S(1)}, f32[64,128]{1,0:T(8,128)S(1)}, u32[]{:S(2)}, u32[]{:S(2)}) collective-permute-start(f32[64,128]{1,0:T(8,128)S(1)} %select_add_fusion.5), channel_id=1, source_target_pairs={{0,8},{4,12},{8,16},{12,20},{16,24},{20,28},{24,0},{28,4},{32,40},... | collective-permute-start | bytes 98312 | tf_op jit(solution)/shard_map/ppermute | solution.py:149
  201.0 6.8 %collective-permute-start.8 = (f32[64,128]{1,0:T(8,128)S(1)}, f32[64,128]{1,0:T(8,128)S(1)}, u32[]{:S(2)}, u32[]{:S(2)}) collective-permute-start(f32[64,128]{1,0:T(8,128)S(1)} %select_add_fusion.5), channel_id=1, source_target_pairs={{0,16},{4,20},{8,24},{12,28},{16,0},{20,4},{24,8},{28,12},{32,48},... | collective-permute-start | bytes 98312 | tf_op jit(solution)/shard_map/ppermute | solution.py:149
  205.4 3.9 %collective-permute-start.7 = (f32[64,128]{1,0:T(8,128)S(1)}, f32[64,128]{1,0:T(8,128)S(1)}, u32[]{:S(2)}, u32[]{:S(2)}) collective-permute-start(f32[64,128]{1,0:T(8,128)S(1)} %select_add_fusion.5), channel_id=1, source_target_pairs={{0,24},{4,28},{8,0},{12,4},{16,8},{20,12},{24,16},{28,20},{32,56},... | collective-permute-start | bytes 98312 | tf_op jit(solution)/shard_map/ppermute | solution.py:149
  209.4 5.7 %collective-permute-start.12 = (f32[64,128]{1,0:T(8,128)S(1)}, f32[64,128]{1,0:T(8,128)S(1)}, u32[]{:S(2)}, u32[]{:S(2)}) collective-permute-start(f32[64,128]{1,0:T(8,128)S(1)} %select_add_fusion.4), channel_id=1, source_target_pairs={{0,32},{4,36},{8,40},{12,44},{16,48},{20,52},{24,56},{28,60},{32,6... | collective-permute-start | bytes 98312 | tf_op jit(solution)/shard_map/ppermute | solution.py:149
  210.9 5.4 %collective-permute-start.11 = (f32[64,128]{1,0:T(8,128)S(1)}, f32[64,128]{1,0:T(8,128)S(1)}, u32[]{:S(2)}, u32[]{:S(2)}) collective-permute-start(f32[64,128]{1,0:T(8,128)S(1)} %select_add_fusion.4), channel_id=1, source_target_pairs={{0,64},{4,68},{8,72},{12,76},{16,80},{20,84},{24,88},{28,92},{32,9... | collective-permute-start | bytes 98312 | tf_op jit(solution)/shard_map/ppermute | solution.py:149
  214.0 3.9 %collective-permute-start.10 = (f32[64,128]{1,0:T(8,128)S(1)}, f32[64,128]{1,0:T(8,128)S(1)}, u32[]{:S(2)}, u32[]{:S(2)}) collective-permute-start(f32[64,128]{1,0:T(8,128)S(1)} %select_add_fusion.4), channel_id=1, source_target_pairs={{0,96},{4,100},{8,104},{12,108},{16,112},{20,116},{24,120},{28,124... | collective-permute-start | bytes 98312 | tf_op jit(solution)/shard_map/ppermute | solution.py:149
  217.9 7.1 %collective-permute-start.15 = (f32[64,128]{1,0:T(8,128)S(1)}, f32[64,128]{1,0:T(8,128)S(1)}, u32[]{:S(2)}, u32[]{:S(2)}) collective-permute-start(f32[64,128]{1,0:T(8,128)S(1)} %select_add_fusion.3), channel_id=1, source_target_pairs={{0,1},{1,2},{2,3},{3,0},{4,5},{5,6},{6,7},{7,4},{8,9},{9,10},{10,1... | collective-permute-start | bytes 98312 | tf_op jit(solution)/shard_map/ppermute | solution.py:149
  218.6 6.4 %collective-permute-start.14 = (f32[64,128]{1,0:T(8,128)S(1)}, f32[64,128]{1,0:T(8,128)S(1)}, u32[]{:S(2)}, u32[]{:S(2)}) collective-permute-start(f32[64,128]{1,0:T(8,128)S(1)} %select_add_fusion.3), channel_id=1, source_target_pairs={{0,2},{1,3},{2,0},{3,1},{4,6},{5,7},{6,4},{7,5},{8,10},{9,11},{10,... | collective-permute-start | bytes 98312 | tf_op jit(solution)/shard_map/ppermute | solution.py:149
  220.6 4.4 %collective-permute-start.13 = (f32[64,128]{1,0:T(8,128)S(1)}, f32[64,128]{1,0:T(8,128)S(1)}, u32[]{:S(2)}, u32[]{:S(2)}) collective-permute-start(f32[64,128]{1,0:T(8,128)S(1)} %select_add_fusion.3), channel_id=1, source_target_pairs={{0,3},{1,0},{2,1},{3,2},{4,7},{5,4},{6,5},{7,6},{8,11},{9,8},{10,9... | collective-permute-start | bytes 98312 | tf_op jit(solution)/shard_map/ppermute | solution.py:149
  238.6 1.3 collective-permute-start.16
  239.9 5.5 %collective-permute-start.19 = (f32[64,64]{1,0:T(8,128)S(1)}, f32[64,64]{1,0:T(8,128)S(1)}, u32[]{:S(2)}, u32[]{:S(2)}) collective-permute-start(f32[64,64]{1,0:T(8,128)S(1)} %select_add_fusion.2), channel_id=1, source_target_pairs={{0,8},{4,12},{8,16},{12,20},{16,24},{20,28},{24,0},{28,4},{32,40},... | collective-permute-start | bytes 49160 | tf_op jit(solution)/shard_map/ppermute | solution.py:149
  240.2 5.9 %collective-permute-start.18 = (f32[64,64]{1,0:T(8,128)S(1)}, f32[64,64]{1,0:T(8,128)S(1)}, u32[]{:S(2)}, u32[]{:S(2)}) collective-permute-start(f32[64,64]{1,0:T(8,128)S(1)} %select_add_fusion.2), channel_id=1, source_target_pairs={{0,16},{4,20},{8,24},{12,28},{16,0},{20,4},{24,8},{28,12},{32,48},... | collective-permute-start | bytes 49160 | tf_op jit(solution)/shard_map/ppermute | solution.py:149
  243.8 3.9 %collective-permute-start.17 = (f32[64,64]{1,0:T(8,128)S(1)}, f32[64,64]{1,0:T(8,128)S(1)}, u32[]{:S(2)}, u32[]{:S(2)}) collective-permute-start(f32[64,64]{1,0:T(8,128)S(1)} %select_add_fusion.2), channel_id=1, source_target_pairs={{0,24},{4,28},{8,0},{12,4},{16,8},{20,12},{24,16},{28,20},{32,56},... | collective-permute-start | bytes 49160 | tf_op jit(solution)/shard_map/ppermute | solution.py:149
  247.8 5.2 %collective-permute-start.22 = (f32[64,64]{1,0:T(8,128)S(1)}, f32[64,64]{1,0:T(8,128)S(1)}, u32[]{:S(2)}, u32[]{:S(2)}) collective-permute-start(f32[64,64]{1,0:T(8,128)S(1)} %select_add_fusion.1), channel_id=1, source_target_pairs={{0,32},{4,36},{8,40},{12,44},{16,48},{20,52},{24,56},{28,60},{32,6... | collective-permute-start | bytes 49160 | tf_op jit(solution)/shard_map/ppermute | solution.py:149
  247.9 5.5 %collective-permute-start.21 = (f32[64,64]{1,0:T(8,128)S(1)}, f32[64,64]{1,0:T(8,128)S(1)}, u32[]{:S(2)}, u32[]{:S(2)}) collective-permute-start(f32[64,64]{1,0:T(8,128)S(1)} %select_add_fusion.1), channel_id=1, source_target_pairs={{0,64},{4,68},{8,72},{12,76},{16,80},{20,84},{24,88},{28,92},{32,9... | collective-permute-start | bytes 49160 | tf_op jit(solution)/shard_map/ppermute | solution.py:149
  250.7 3.9 %collective-permute-start.20 = (f32[64,64]{1,0:T(8,128)S(1)}, f32[64,64]{1,0:T(8,128)S(1)}, u32[]{:S(2)}, u32[]{:S(2)}) collective-permute-start(f32[64,64]{1,0:T(8,128)S(1)} %select_add_fusion.1), channel_id=1, source_target_pairs={{0,96},{4,100},{8,104},{12,108},{16,112},{20,116},{24,120},{28,124... | collective-permute-start | bytes 49160 | tf_op jit(solution)/shard_map/ppermute | solution.py:149
  254.6 5.4 %collective-permute-start.25 = (f32[64,64]{1,0:T(8,128)S(1)}, f32[64,64]{1,0:T(8,128)S(1)}, u32[]{:S(2)}, u32[]{:S(2)}) collective-permute-start(f32[64,64]{1,0:T(8,128)S(1)} %select_add_fusion), channel_id=1, source_target_pairs={{0,1},{1,2},{2,3},{3,0},{4,5},{5,6},{6,7},{7,4},{8,9},{9,10},{10,1... | collective-permute-start | bytes 49160 | tf_op jit(solution)/shard_map/ppermute | solution.py:149
  255.9 5.4 %collective-permute-start.24 = (f32[64,64]{1,0:T(8,128)S(1)}, f32[64,64]{1,0:T(8,128)S(1)}, u32[]{:S(2)}, u32[]{:S(2)}) collective-permute-start(f32[64,64]{1,0:T(8,128)S(1)} %select_add_fusion), channel_id=1, source_target_pairs={{0,2},{1,3},{2,0},{3,1},{4,6},{5,7},{6,4},{7,5},{8,10},{9,11},{10,... | collective-permute-start | bytes 49160 | tf_op jit(solution)/shard_map/ppermute | solution.py:149
  258.1 3.9 %collective-permute-start.23 = (f32[64,64]{1,0:T(8,128)S(1)}, f32[64,64]{1,0:T(8,128)S(1)}, u32[]{:S(2)}, u32[]{:S(2)}) collective-permute-start(f32[64,64]{1,0:T(8,128)S(1)} %select_add_fusion), channel_id=1, source_target_pairs={{0,3},{1,0},{2,1},{3,2},{4,7},{5,4},{6,5},{7,6},{8,11},{9,8},{10,9... | collective-permute-start | bytes 49160 | tf_op jit(solution)/shard_map/ppermute | solution.py:149
  278.3 5.1 %slice-start = ((f32[64,192]{1,0:T(8,128)}), f32[64,128]{1,0:T(8,128)S(1)}, s32[]{:S(2)}) async-start(f32[64,192]{1,0:T(8,128)} %shard_map.45), calls=%async_computation.3 | async-start | bytes 65536 | tf_op jit(solution)/shard_map/concatenate | solution.py:222
  278.3 5.1 %copy-start.6 = (f32[64,128]{1,0:T(8,128)S(1)}, f32[64,128]{1,0:T(8,128)}, u32[]{:S(2)}) copy-start(f32[64,128]{1,0:T(8,128)} %shard_map.46) | copy-start | bytes 98308
  278.3 55.3 %all-to-all-start.2 = ((f32[128,1,72,128]{3,2,1,0:T(8,128)}), f32[128,1,72,128]{3,2,1,0:T(8,128)}, u32[]{:S(2)}, u32[]{:S(2)}) async-start(f32[128,1,72,128]{3,2,1,0:T(8,128)} %copy.15), calls=%async_computation.2 | async-start | bytes 9437184 | tf_op jit(solution)/shard_map/all_to_all | solution.py:257
  (4 other events, 7.5 us)

commit v2 on v1

--- a/solution.py
+++ b/solution.py
@@ -214,17 +214,25 @@
     coupling = first[:, panel_rows : 2 * panel_rows]
     first_lower_inv = first[:, 2 * panel_rows :]
     first_q = mix_rows(first_lower_inv, rows_block[:panel_rows])
-    remainder = rows_block[panel_rows:] - apply_rows(coupling, first_q)
+    zeros = jnp.zeros((panel_rows, panel_rows), jnp.float32)
+    lift = jnp.concatenate([zeros, coupling.T], axis=0)
+    adjusted = rows_block - mix_rows(lift, first_q)
+    remainder = adjusted[panel_rows:]
     trailing = cell_sum(gram_matrix(remainder, remainder)) * inv_cells
     second = eliminate(trailing, eye)
     second_r = second[:, :panel_rows]
     second_lower_inv = second[:, panel_rows:]
     upper_rows = jnp.concatenate([first_r, coupling], axis=1)
-    lower_rows = jnp.concatenate(
-        [jnp.zeros((second_r.shape[0], panel_rows), jnp.float32), second_r], axis=1
-    )
+    lower_rows = jnp.concatenate([zeros, second_r], axis=1)
     triangle = jnp.concatenate([upper_rows, lower_rows], axis=0)
-    return triangle, first_q, second_lower_inv, remainder
+    weights = jnp.concatenate(
+        [
+            jnp.concatenate([first_lower_inv, zeros], axis=1),
+            jnp.concatenate([zeros, second_lower_inv], axis=1),
+        ],
+        axis=0,
+    )
+    return triangle, mix_rows(weights, adjusted)
 
 
 def local(orbital_block, potential):
@@ -250,9 +258,7 @@
     parts, _, rows_per_part, lanes = spread_a.shape
     spread = jnp.stack([spread_a, spread_b], axis=1).reshape(-1, rows_per_part, lanes)
     inv_cells = 1.0 / (lax.axis_size("grid") * parts * rows_per_part * lanes)
-    triangle, first_q, second_lower_inv, remainder = factorize(spread, inv_cells)
-    second_q = mix_rows(second_lower_inv, remainder)
-    orbitals = jnp.concatenate([first_q, second_q], axis=0)
+    triangle, orbitals = factorize(spread, inv_cells)
     orbitals = orbitals.reshape(orbitals.shape[0], 1, rows_per_part, lanes)
     orbitals = lax.all_to_all(orbitals, "orb", 0, 1, tiled=True)
     return (orbitals.reshape(orbital_block.shape), triangle)

time: 340 us -> 348 us (1.024)
  starting transfers between devices: 54.8 us -> 72.7 us
  waiting for transfers between devices: 78.9 us -> 70.4 us
  other arithmetic: 99.8 us -> 92.2 us
    ppermute x3, starting transfers between devices: 12.5 us -> 26.1 us  [halo_planes(): before = lax.ppermute(last, axis, up)]
    all_to_all x1, waiting for transfers between devices: 12.4 us -> 0.01 us  [spread_cells(): lax.all_to_all(chunks, 'orb', 1, 0, tiled=True)]
    another operation x2, other arithmetic: 5.37 us -> 0.46 us  [local(): jnp.stack([spread_a, spread_b], axis=1).reshape(-1, rows_per_part, lanes)]
    dot_general x2 -> x3, matrix products: 4.05 us -> 8.77 us  [mix_rows(): lax.dot_general(weights, source_rows, (((1,), (0,)), ((), ())), precision...]
    ppermute x20, starting transfers between devices: 28 us -> 32.3 us  [group_round(): received.append(lax.ppermute(value, axis, pairs))]
    unnamed x14 -> x10, local copies, waits for them, and re-layouts: 0.06 us -> 3.91 us
    ppermute x20, waiting for transfers between devices: 17 us -> 20.8 us  [group_round(): received.append(lax.ppermute(value, axis, pairs))]
  transfers between devices with their start and end apart: 28 -> 28, of which waited for: 17 -> 19; matrix products, arithmetic and copies ran while one was open for 30% -> 28% of each run, Pallas kernels for 5% -> 5%
where the time goes in v2:
time: 348 us; the launch traced here: 347 us
  other arithmetic  92.2 us (26%)
  starting transfers between devices  72.7 us (21%)
  waiting for transfers between devices  70.4 us (20%)
  Pallas kernels  40.5 us (12%)
  blocking collectives  34.7 us (10%)
  local copies, waits for them, and re-layouts  23.5 us (7%)
  matrix products  12.5 us (4%)
    add x3, other arithmetic, local_terms(): return -2.0 * total + potential[None] * orbital_field  89.5 us
    all_to_all x1, waiting for transfers between devices, local(): orbitals = lax.all_to_all(orbitals, 'orb', 0, 1, tiled=True)  49.6 us
    all_to_all x1, blocking collectives, spread_cells(): lax.all_to_all(chunks, 'orb', 1, 0, tiled=True)  34.7 us
    ppermute x20, starting transfers between devices, group_round(): received.append(lax.ppermute(value, axis, pairs))  32.3 us
    ppermute x3, starting transfers between devices, halo_planes(): before = lax.ppermute(last, axis, up)  26.1 us
    pallas_call x4, Pallas kernels, filter_step(): pl.pallas_call(functools.partial(combine_kernel, scale, base is not None)...  24.1 us
    ppermute x20, waiting for transfers between devices, group_round(): received.append(lax.ppermute(value, axis, pairs))  20.8 us
    pallas_call x2, Pallas kernels, eliminate(): pl.pallas_call(eliminate_kernel, out_shape=jax.ShapeDtypeStruct(source.sh...  16.4 us
  transfers between devices with their start and end apart: 28, of which 19 were waited for; matrix products, arithmetic and copies ran while one was open for 28% of the time, Pallas kernels for 5%

profile of v2, /device:TPU:0, one launch (start us, length us, event | category | flops | bytes accessed | tf_op | source)
XLA Modules:
  0.0 347.5 jit_solution(11211788839350431199)
XLA Ops:
  1.9 5.2 %collective-permute-start = (f32[32,6,48,128]{3,2,1,0:T(8,128)}, f32[32,6,48,128]{3,2,1,0:T(8,128)}, u32[]{:S(2)}, u32[]{:S(2)}) collective-permute-start(f32[32,6,48,128]{3,2,1,0:T(8,128)} %refs_4_.3), channel_id=1, source_target_pairs={{0,4},{4,8},{8,12},{12,16},{16,20},{20,24},{24,28},{28,32},{32,36}... | collective-permute-start | bytes 14155784 | tf_op jit(solution)/shard_map/ppermute | solution.py:30
  7.1 52.5 %multiply_add_fusion.refs_0_ = f32[32,6,48,128]{3,2,1,0:T(8,128)} fusion(f32[32,6,48,128]{3,2,1,0:T(8,128)} %refs_4_.3, f32[6,48,128]{2,1,0:T(8,128)} %param.3), kind=kLoop, calls=%fused_computation.111 | loop fusion | flops 47185920 | bytes 9584640 | tf_op jit(solution)/shard_map/add | solution.py:49
  59.7 5.6 %shard_map.41.refs_1_ = f32[16,6,48,128]{3,2,1,0:T(8,128)} custom-call(f32[32,6,48,128]{3,2,1,0:T(8,128)} %multiply_add_fusion.refs_0_, f32[32,6,48,128]{3,2,1,0:T(8,128)} %refs_4_.3, f32[32,6,48,128]{3,2,1,0:T(8,128)} %collective-permute-done.refs_2_, f32[32,6,48,128]{3,2,1,0:T(8,128)} %collective-permute-done.1.refs_3_), custom_call_target="tpu_custom_call" | custom-call | tf_op jit(solution)/shard_map/pallas_call | solution.py:92
  65.3 2.8 collective-permute-start.2
  69.4 5.6 %shard_map.42.refs_1_ = f32[16,6,48,128]{3,2,1,0:T(8,128)} custom-call(f32[32,6,48,128]{3,2,1,0:T(8,128)} %multiply_add_fusion.refs_0_, f32[32,6,48,128]{3,2,1,0:T(8,128)} %refs_4_.3, f32[32,6,48,128]{3,2,1,0:T(8,128)} %collective-permute-done.refs_2_, f32[32,6,48,128]{3,2,1,0:T(8,128)} %collective-permute-done.1.refs_3_), custom_call_target="tpu_custom_call" | custom-call | tf_op jit(solution)/shard_map/pallas_call | solution.py:92
  75.0 8.4 %multiply_add_fusion.2.refs_0_ = f32[16,6,48,128]{3,2,1,0:T(8,128)} fusion(f32[16,6,48,128]{3,2,1,0:T(8,128)S(1)} %copy-done.3, f32[6,48,128]{2,1,0:T(8,128)S(1)} %copy-done.4), kind=kLoop, calls=%fused_computation.188 | loop fusion | flops 23592960 | bytes 4866048 | tf_op jit(solution)/shard_map/add | solution.py:49
  83.4 18.1 %collective-permute-start.4 = (f32[16,6,48,128]{3,2,1,0:T(8,128)}, f32[16,6,48,128]{3,2,1,0:T(8,128)}, u32[]{:S(2)}, u32[]{:S(2)}) collective-permute-start(f32[16,6,48,128]{3,2,1,0:T(8,128)} %shard_map.42.refs_1_), channel_id=1, source_target_pairs={{0,4},{4,8},{8,12},{12,16},{16,20},{20,24},{24,28},{28,32},{32,36}... | collective-permute-start | bytes 7077896 | tf_op jit(solution)/shard_map/ppermute | solution.py:30
  102.9 6.4 %shard_map.43 = f32[16,6,48,128]{3,2,1,0:T(8,128)} custom-call(f32[16,6,48,128]{3,2,1,0:T(8,128)} %multiply_add_fusion.2.refs_0_, f32[16,6,48,128]{3,2,1,0:T(8,128)} %shard_map.41.refs_1_, f32[16,6,48,128]{3,2,1,0:T(8,128)} %collective-permute-done.2.refs_2_, f32[16,6,48,128]{3,2,1,0:T(8,128)} %collective-permute-done.3.refs_3_, f32[32,6,48,128]{3,2,1,0:T(8,128)} %refs_4_.3), custom_call_target="tpu_custom_call" | custom-call | tf_op jit(solution)/shard_map/pallas_call | solution.py:92
  109.3 3.3 copy.7
  112.6 5.3 %all-to-all-start = ((f32[16,4,72,128]{3,2,0,1:T(8,128)}), f32[16,4,72,128]{3,2,0,1:T(8,128)S(1)}, u32[]{:S(2)}, u32[]{:S(2)}) async-start(f32[16,4,72,128]{3,2,0,1:T(8,128)} %copy.7), calls=%async_computation | async-start | bytes 4718592 | tf_op jit(solution)/shard_map/all_to_all | solution.py:107
  117.9 28.6 %multiply_add_fusion.1.refs_0_ = f32[16,6,48,128]{3,2,1,0:T(8,128)} fusion(f32[16,6,48,128]{3,2,1,0:T(8,128)} %shard_map.42.refs_1_, f32[6,48,128]{2,1,0:T(8,128)S(1)} %copy-done.4), kind=kLoop, calls=%fused_computation.187 | loop fusion | flops 23592960 | bytes 4866048 | tf_op jit(solution)/shard_map/add | solution.py:49
  146.5 6.4 %shard_map.44 = f32[16,6,48,128]{3,2,1,0:T(8,128)} custom-call(f32[16,6,48,128]{3,2,1,0:T(8,128)} %multiply_add_fusion.1.refs_0_, f32[16,6,48,128]{3,2,1,0:T(8,128)} %shard_map.42.refs_1_, f32[16,6,48,128]{3,2,1,0:T(8,128)} %collective-permute-done.4.refs_2_, f32[16,6,48,128]{3,2,1,0:T(8,128)} %collective-permute-done.5.refs_3_, f32[32,6,48,128]{3,2,1,0:T(8,128)} %refs_4_.3), custom_call_target="tpu_custom_call" | custom-call | tf_op jit(solution)/shard_map/pallas_call | solution.py:92
  152.9 3.2 copy.8
  156.1 34.7 %all_to_all.45 = f32[16,4,72,128]{3,2,0,1:T(8,128)S(1)} all-to-all(f32[16,4,72,128]{3,2,0,1:T(8,128)} %copy.8), channel_id=1, replica_groups=mesh['grid'=32,'orb'=4] {'orb'}, dimensions={1} | all-to-all | bytes 4718592 | tf_op jit(solution)/shard_map/all_to_all | solution.py:107
  194.4 2.6 convolution_bitcast_fusion.1
  198.5 9.1 %collective-permute-start.8 = (f32[64,128]{1,0:T(8,128)S(1)}, f32[64,128]{1,0:T(8,128)S(1)}, u32[]{:S(2)}, u32[]{:S(2)}) collective-permute-start(f32[64,128]{1,0:T(8,128)S(1)} %select_add_fusion.5), channel_id=1, source_target_pairs={{0,16},{4,20},{8,24},{12,28},{16,0},{20,4},{24,8},{28,12},{32,48},... | collective-permute-start | bytes 98312 | tf_op jit(solution)/shard_map/ppermute | solution.py:149
  208.0 1.8 collective-permute-done.8
  214.7 2.5 collective-permute-start.10
  219.5 2.1 collective-permute-start.14
  226.2 8.4 %shard_map.45 = f32[64,192]{1,0:T(8,128)} custom-call(f32[64,192]{1,0:T(8,128)} %pad_maximum_fusion.1.source_ref), custom_call_target="tpu_custom_call" | custom-call | tf_op jit(solution)/shard_map/pallas_call | solution.py:202
  234.5 2.0 fusion.121
  237.4 2.3 convolution_subtract_fusion
  239.7 2.2 copy-done.2
  244.4 2.7 collective-permute-start.18
  252.2 3.8 %collective-permute-start.21 = (f32[64,64]{1,0:T(8,128)S(1)}, f32[64,64]{1,0:T(8,128)S(1)}, u32[]{:S(2)}, u32[]{:S(2)}) collective-permute-start(f32[64,64]{1,0:T(8,128)S(1)} %select_add_fusion.1), channel_id=1, source_target_pairs={{0,64},{4,68},{8,72},{12,76},{16,80},{20,84},{24,88},{28,92},{32,9... | collective-permute-start | bytes 49160 | tf_op jit(solution)/shard_map/ppermute | solution.py:149
  261.5 2.4 collective-permute-start.24
  268.6 8.0 %shard_map.46 = f32[64,128]{1,0:T(8,128)} custom-call(f32[64,128]{1,0:T(8,128)} %pad_maximum_fusion.2.source_ref), custom_call_target="tpu_custom_call" | custom-call | tf_op jit(solution)/shard_map/pallas_call | solution.py:202
  277.5 4.5 %convolution_bitcast_fusion = f32[128,1,72,128]{3,0,2,1:T(8,128)S(1)} fusion(f32[128,72,128]{2,0,1:T(8,128)} %copy-done.2, f32[64,64]{1,0:T(8,128)S(1)} %get-tuple-element.25, f32[64,64]{1,0:T(8,128)S(1)} %get-tuple-element.22), kind=kOutput, calls=%fused_computation.189 | convolution fusion | flops 906051584 | bytes 9469952 | tf_op jit(solution)/shard_map/dot_general | solution.py:131
  282.0 4.9 %copy.11 = f32[128,1,72,128]{3,2,1,0:T(8,128)} copy(f32[128,1,72,128]{3,0,2,1:T(8,128)S(1)} %convolution_bitcast_fusion) | data formatting | bytes 9437184 | tf_op jit(solution)/shard_map/reshape | solution.py:262
  287.0 5.1 %all-to-all-start.2 = ((f32[128,1,72,128]{3,2,1,0:T(8,128)}), f32[128,1,72,128]{3,2,1,0:T(8,128)}, u32[]{:S(2)}, u32[]{:S(2)}) async-start(f32[128,1,72,128]{3,2,1,0:T(8,128)} %copy.11), calls=%async_computation.2 | async-start | bytes 9437184 | tf_op jit(solution)/shard_map/all_to_all | solution.py:263
  292.8 49.6 %all-to-all-done.2 = f32[128,1,72,128]{3,2,1,0:T(8,128)} async-done(((f32[128,1,72,128]{3,2,1,0:T(8,128)}), f32[128,1,72,128]{3,2,1,0:T(8,128)}, u32[]{:S(2)}, u32[]{:S(2)}) %all-to-all-start.2) | async-done | bytes 4718624 | tf_op jit(solution)/shard_map/all_to_all | solution.py:263
  342.4 5.1 %copy.12 = f32[32,4,1,72,128]{4,3,1,0,2:T(8,128)} copy(f32[32,4,1,72,128]{4,3,0,1,2:T(8,128)} %bitcast.18) | data formatting | bytes 9437184 | tf_op jit(solution)/shard_map/all_to_all | solution.py:263
  (73 shorter events, 41.3 us)
Async XLA Ops:
  0.6 59.0 %collective-permute-start.1 = (f32[32,6,48,128]{3,2,1,0:T(8,128)}, f32[32,6,48,128]{3,2,1,0:T(8,128)}, u32[]{:S(2)}, u32[]{:S(2)}) collective-permute-start(f32[32,6,48,128]{3,2,1,0:T(8,128)} %refs_4_.3), channel_id=1, source_target_pairs={{4,0},{8,4},{12,8},{16,12},{20,16},{24,20},{28,24},{32,28},{36,32}... | collective-permute-start | bytes 14155784 | tf_op jit(solution)/shard_map/ppermute | solution.py:31
  1.9 57.7 %collective-permute-start = (f32[32,6,48,128]{3,2,1,0:T(8,128)}, f32[32,6,48,128]{3,2,1,0:T(8,128)}, u32[]{:S(2)}, u32[]{:S(2)}) collective-permute-start(f32[32,6,48,128]{3,2,1,0:T(8,128)} %refs_4_.3), channel_id=1, source_target_pairs={{0,4},{4,8},{8,12},{12,16},{16,20},{20,24},{24,28},{28,32},{32,36}... | collective-permute-start | bytes 14155784 | tf_op jit(solution)/shard_map/ppermute | solution.py:30
  65.3 9.7 %copy-start.3 = (f32[16,6,48,128]{3,2,1,0:T(8,128)S(1)}, f32[16,6,48,128]{3,2,1,0:T(8,128)}, u32[]{:S(2)}) copy-start(f32[16,6,48,128]{3,2,1,0:T(8,128)} %shard_map.41.refs_1_) | copy-start | bytes 7077892
  65.3 9.7 %copy-start.4 = (f32[6,48,128]{2,1,0:T(8,128)S(1)}, f32[6,48,128]{2,1,0:T(8,128)}, u32[]{:S(2)}) copy-start(f32[6,48,128]{2,1,0:T(8,128)} %param.3) | copy-start | bytes 442372
  65.3 18.2 %collective-permute-start.2 = (f32[16,6,48,128]{3,2,1,0:T(8,128)}, f32[16,6,48,128]{3,2,1,0:T(8,128)}, u32[]{:S(2)}, u32[]{:S(2)}) collective-permute-start(f32[16,6,48,128]{3,2,1,0:T(8,128)} %shard_map.41.refs_1_), channel_id=1, source_target_pairs={{0,4},{4,8},{8,12},{12,16},{16,20},{20,24},{24,28},{28,32},{32,36}... | collective-permute-start | bytes 7077896 | tf_op jit(solution)/shard_map/ppermute | solution.py:30
  68.1 15.4 %collective-permute-start.3 = (f32[16,6,48,128]{3,2,1,0:T(8,128)}, f32[16,6,48,128]{3,2,1,0:T(8,128)}, u32[]{:S(2)}, u32[]{:S(2)}) collective-permute-start(f32[16,6,48,128]{3,2,1,0:T(8,128)} %shard_map.41.refs_1_), channel_id=1, source_target_pairs={{4,0},{8,4},{12,8},{16,12},{20,16},{24,20},{28,24},{32,28},{36,32}... | collective-permute-start | bytes 7077896 | tf_op jit(solution)/shard_map/ppermute | solution.py:31
  83.4 63.0 %collective-permute-start.4 = (f32[16,6,48,128]{3,2,1,0:T(8,128)}, f32[16,6,48,128]{3,2,1,0:T(8,128)}, u32[]{:S(2)}, u32[]{:S(2)}) collective-permute-start(f32[16,6,48,128]{3,2,1,0:T(8,128)} %shard_map.42.refs_1_), channel_id=1, source_target_pairs={{0,4},{4,8},{8,12},{12,16},{16,20},{20,24},{24,28},{28,32},{32,36}... | collective-permute-start | bytes 7077896 | tf_op jit(solution)/shard_map/ppermute | solution.py:30
  101.6 44.9 %collective-permute-start.5 = (f32[16,6,48,128]{3,2,1,0:T(8,128)}, f32[16,6,48,128]{3,2,1,0:T(8,128)}, u32[]{:S(2)}, u32[]{:S(2)}) collective-permute-start(f32[16,6,48,128]{3,2,1,0:T(8,128)} %shard_map.42.refs_1_), channel_id=1, source_target_pairs={{4,0},{8,4},{12,8},{16,12},{20,16},{24,20},{28,24},{32,28},{36,32}... | collective-permute-start | bytes 7077896 | tf_op jit(solution)/shard_map/ppermute | solution.py:31
  112.6 43.6 %all-to-all-start = ((f32[16,4,72,128]{3,2,0,1:T(8,128)}), f32[16,4,72,128]{3,2,0,1:T(8,128)S(1)}, u32[]{:S(2)}, u32[]{:S(2)}) async-start(f32[16,4,72,128]{3,2,0,1:T(8,128)} %copy.7), calls=%async_computation | async-start | bytes 4718592 | tf_op jit(solution)/shard_map/all_to_all | solution.py:107
  197.0 1.3 collective-permute-start.6
  198.2 9.8 %collective-permute-start.9 = (f32[64,128]{1,0:T(8,128)S(1)}, f32[64,128]{1,0:T(8,128)S(1)}, u32[]{:S(2)}, u32[]{:S(2)}) collective-permute-start(f32[64,128]{1,0:T(8,128)S(1)} %select_add_fusion.5), channel_id=1, source_target_pairs={{0,8},{4,12},{8,16},{12,20},{16,24},{20,28},{24,0},{28,4},{32,40},... | collective-permute-start | bytes 98312 | tf_op jit(solution)/shard_map/ppermute | solution.py:149
  198.5 11.3 %collective-permute-start.8 = (f32[64,128]{1,0:T(8,128)S(1)}, f32[64,128]{1,0:T(8,128)S(1)}, u32[]{:S(2)}, u32[]{:S(2)}) collective-permute-start(f32[64,128]{1,0:T(8,128)S(1)} %select_add_fusion.5), channel_id=1, source_target_pairs={{0,16},{4,20},{8,24},{12,28},{16,0},{20,4},{24,8},{28,12},{32,48},... | collective-permute-start | bytes 98312 | tf_op jit(solution)/shard_map/ppermute | solution.py:149
  207.6 3.9 %collective-permute-start.7 = (f32[64,128]{1,0:T(8,128)S(1)}, f32[64,128]{1,0:T(8,128)S(1)}, u32[]{:S(2)}, u32[]{:S(2)}) collective-permute-start(f32[64,128]{1,0:T(8,128)S(1)} %select_add_fusion.5), channel_id=1, source_target_pairs={{0,24},{4,28},{8,0},{12,4},{16,8},{20,12},{24,16},{28,20},{32,56},... | collective-permute-start | bytes 98312 | tf_op jit(solution)/shard_map/ppermute | solution.py:149
  211.5 5.7 %collective-permute-start.12 = (f32[64,128]{1,0:T(8,128)S(1)}, f32[64,128]{1,0:T(8,128)S(1)}, u32[]{:S(2)}, u32[]{:S(2)}) collective-permute-start(f32[64,128]{1,0:T(8,128)S(1)} %select_add_fusion.4), channel_id=1, source_target_pairs={{0,32},{4,36},{8,40},{12,44},{16,48},{20,52},{24,56},{28,60},{32,6... | collective-permute-start | bytes 98312 | tf_op jit(solution)/shard_map/ppermute | solution.py:149
  213.1 5.4 %collective-permute-start.11 = (f32[64,128]{1,0:T(8,128)S(1)}, f32[64,128]{1,0:T(8,128)S(1)}, u32[]{:S(2)}, u32[]{:S(2)}) collective-permute-start(f32[64,128]{1,0:T(8,128)S(1)} %select_add_fusion.4), channel_id=1, source_target_pairs={{0,64},{4,68},{8,72},{12,76},{16,80},{20,84},{24,88},{28,92},{32,9... | collective-permute-start | bytes 98312 | tf_op jit(solution)/shard_map/ppermute | solution.py:149
  214.7 4.1 %collective-permute-start.10 = (f32[64,128]{1,0:T(8,128)S(1)}, f32[64,128]{1,0:T(8,128)S(1)}, u32[]{:S(2)}, u32[]{:S(2)}) collective-permute-start(f32[64,128]{1,0:T(8,128)S(1)} %select_add_fusion.4), channel_id=1, source_target_pairs={{0,96},{4,100},{8,104},{12,108},{16,112},{20,116},{24,120},{28,124... | collective-permute-start | bytes 98312 | tf_op jit(solution)/shard_map/ppermute | solution.py:149
  218.9 5.2 %collective-permute-start.15 = (f32[64,128]{1,0:T(8,128)S(1)}, f32[64,128]{1,0:T(8,128)S(1)}, u32[]{:S(2)}, u32[]{:S(2)}) collective-permute-start(f32[64,128]{1,0:T(8,128)S(1)} %select_add_fusion.3), channel_id=1, source_target_pairs={{0,1},{1,2},{2,3},{3,0},{4,5},{5,6},{6,7},{7,4},{8,9},{9,10},{10,1... | collective-permute-start | bytes 98312 | tf_op jit(solution)/shard_map/ppermute | solution.py:149
  219.5 5.4 %collective-permute-start.14 = (f32[64,128]{1,0:T(8,128)S(1)}, f32[64,128]{1,0:T(8,128)S(1)}, u32[]{:S(2)}, u32[]{:S(2)}) collective-permute-start(f32[64,128]{1,0:T(8,128)S(1)} %select_add_fusion.3), channel_id=1, source_target_pairs={{0,2},{1,3},{2,0},{3,1},{4,6},{5,7},{6,4},{7,5},{8,10},{9,11},{10,... | collective-permute-start | bytes 98312 | tf_op jit(solution)/shard_map/ppermute | solution.py:149
  221.6 3.9 %collective-permute-start.13 = (f32[64,128]{1,0:T(8,128)S(1)}, f32[64,128]{1,0:T(8,128)S(1)}, u32[]{:S(2)}, u32[]{:S(2)}) collective-permute-start(f32[64,128]{1,0:T(8,128)S(1)} %select_add_fusion.3), channel_id=1, source_target_pairs={{0,3},{1,0},{2,1},{3,2},{4,7},{5,4},{6,5},{7,6},{8,11},{9,8},{10,9... | collective-permute-start | bytes 98312 | tf_op jit(solution)/shard_map/ppermute | solution.py:149
  234.5 2.8 copy-start.1
  243.0 1.3 collective-permute-start.16
  244.3 5.7 %collective-permute-start.19 = (f32[64,64]{1,0:T(8,128)S(1)}, f32[64,64]{1,0:T(8,128)S(1)}, u32[]{:S(2)}, u32[]{:S(2)}) collective-permute-start(f32[64,64]{1,0:T(8,128)S(1)} %select_add_fusion.2), channel_id=1, source_target_pairs={{0,8},{4,12},{8,16},{12,20},{16,24},{20,28},{24,0},{28,4},{32,40},... | collective-permute-start | bytes 49160 | tf_op jit(solution)/shard_map/ppermute | solution.py:149
  244.4 5.6 %collective-permute-start.18 = (f32[64,64]{1,0:T(8,128)S(1)}, f32[64,64]{1,0:T(8,128)S(1)}, u32[]{:S(2)}, u32[]{:S(2)}) collective-permute-start(f32[64,64]{1,0:T(8,128)S(1)} %select_add_fusion.2), channel_id=1, source_target_pairs={{0,16},{4,20},{8,24},{12,28},{16,0},{20,4},{24,8},{28,12},{32,48},... | collective-permute-start | bytes 49160 | tf_op jit(solution)/shard_map/ppermute | solution.py:149
  247.1 3.9 %collective-permute-start.17 = (f32[64,64]{1,0:T(8,128)S(1)}, f32[64,64]{1,0:T(8,128)S(1)}, u32[]{:S(2)}, u32[]{:S(2)}) collective-permute-start(f32[64,64]{1,0:T(8,128)S(1)} %select_add_fusion.2), channel_id=1, source_target_pairs={{0,24},{4,28},{8,0},{12,4},{16,8},{20,12},{24,16},{28,20},{32,56},... | collective-permute-start | bytes 49160 | tf_op jit(solution)/shard_map/ppermute | solution.py:149
  251.0 5.5 %collective-permute-start.22 = (f32[64,64]{1,0:T(8,128)S(1)}, f32[64,64]{1,0:T(8,128)S(1)}, u32[]{:S(2)}, u32[]{:S(2)}) collective-permute-start(f32[64,64]{1,0:T(8,128)S(1)} %select_add_fusion.1), channel_id=1, source_target_pairs={{0,32},{4,36},{8,40},{12,44},{16,48},{20,52},{24,56},{28,60},{32,6... | collective-permute-start | bytes 49160 | tf_op jit(solution)/shard_map/ppermute | solution.py:149
  252.2 6.1 %collective-permute-start.21 = (f32[64,64]{1,0:T(8,128)S(1)}, f32[64,64]{1,0:T(8,128)S(1)}, u32[]{:S(2)}, u32[]{:S(2)}) collective-permute-start(f32[64,64]{1,0:T(8,128)S(1)} %select_add_fusion.1), channel_id=1, source_target_pairs={{0,64},{4,68},{8,72},{12,76},{16,80},{20,84},{24,88},{28,92},{32,9... | collective-permute-start | bytes 49160 | tf_op jit(solution)/shard_map/ppermute | solution.py:149
  256.1 3.9 %collective-permute-start.20 = (f32[64,64]{1,0:T(8,128)S(1)}, f32[64,64]{1,0:T(8,128)S(1)}, u32[]{:S(2)}, u32[]{:S(2)}) collective-permute-start(f32[64,64]{1,0:T(8,128)S(1)} %select_add_fusion.1), channel_id=1, source_target_pairs={{0,96},{4,100},{8,104},{12,108},{16,112},{20,116},{24,120},{28,124... | collective-permute-start | bytes 49160 | tf_op jit(solution)/shard_map/ppermute | solution.py:149
  260.0 5.2 %collective-permute-start.25 = (f32[64,64]{1,0:T(8,128)S(1)}, f32[64,64]{1,0:T(8,128)S(1)}, u32[]{:S(2)}, u32[]{:S(2)}) collective-permute-start(f32[64,64]{1,0:T(8,128)S(1)} %select_add_fusion), channel_id=1, source_target_pairs={{0,1},{1,2},{2,3},{3,0},{4,5},{5,6},{6,7},{7,4},{8,9},{9,10},{10,1... | collective-permute-start | bytes 49160 | tf_op jit(solution)/shard_map/ppermute | solution.py:149
  261.5 5.4 %collective-permute-start.24 = (f32[64,64]{1,0:T(8,128)S(1)}, f32[64,64]{1,0:T(8,128)S(1)}, u32[]{:S(2)}, u32[]{:S(2)}) collective-permute-start(f32[64,64]{1,0:T(8,128)S(1)} %select_add_fusion), channel_id=1, source_target_pairs={{0,2},{1,3},{2,0},{3,1},{4,6},{5,7},{6,4},{7,5},{8,10},{9,11},{10,... | collective-permute-start | bytes 49160 | tf_op jit(solution)/shard_map/ppermute | solution.py:149
  263.9 3.9 %collective-permute-start.23 = (f32[64,64]{1,0:T(8,128)S(1)}, f32[64,64]{1,0:T(8,128)S(1)}, u32[]{:S(2)}, u32[]{:S(2)}) collective-permute-start(f32[64,64]{1,0:T(8,128)S(1)} %select_add_fusion), channel_id=1, source_target_pairs={{0,3},{1,0},{2,1},{3,2},{4,7},{5,4},{6,5},{7,6},{8,11},{9,8},{10,9... | collective-permute-start | bytes 49160 | tf_op jit(solution)/shard_map/ppermute | solution.py:149
  286.9 5.1 %slice-start = ((f32[64,192]{1,0:T(8,128)}), f32[64,128]{1,0:T(8,128)S(1)}, s32[]{:S(2)}) async-start(f32[64,192]{1,0:T(8,128)} %shard_map.45), calls=%async_computation.3 | async-start | bytes 65536 | tf_op jit(solution)/shard_map/concatenate | solution.py:225
  287.0 55.4 %all-to-all-start.2 = ((f32[128,1,72,128]{3,2,1,0:T(8,128)}), f32[128,1,72,128]{3,2,1,0:T(8,128)}, u32[]{:S(2)}, u32[]{:S(2)}) async-start(f32[128,1,72,128]{3,2,1,0:T(8,128)} %copy.11), calls=%async_computation.2 | async-start | bytes 9437184 | tf_op jit(solution)/shard_map/all_to_all | solution.py:263
  (2 other events, 4.4 us)

commit v3 on v1

--- a/solution.py
+++ b/solution.py
@@ -75,15 +75,20 @@
         out_ref[:, p] = value
 
 
-def filter_step(local, orbital_field, before, after, scale, base=None, start=0, count=None, base_start=0):
+def filter_step(
+    local, orbital_field, before, after, scale, base=None, start=0, count=None, base_start=0, halo_start=None
+):
     count = orbital_field.shape[0] if count is None else count
-    block_rows = 8 if count % 8 == 0 and start % 8 == 0 and base_start % 8 == 0 else 1
+    halo_start = start if halo_start is None else halo_start
+    aligned = all(value % 8 == 0 for value in (count, start, base_start, halo_start))
+    block_rows = 8 if aligned else 1
     offset = start // block_rows
+    halo_offset = halo_start // block_rows
     base_offset = base_start // block_rows
     block = (block_rows,) + orbital_field.shape[1:]
     halo_block = (block_rows,) + before.shape[1:]
     spec = pl.BlockSpec(block, lambda i: (i + offset, 0, 0, 0))
-    halo_spec = pl.BlockSpec(halo_block, lambda i: (i + offset, 0, 0, 0))
+    halo_spec = pl.BlockSpec(halo_block, lambda i: (i + halo_offset, 0, 0, 0))
     operands = [local, orbital_field, before, after]
     specs = [spec, spec, halo_spec, halo_spec]
     if base is not None:
@@ -230,11 +235,16 @@
 def local(orbital_block, potential):
     orb_rows = orbital_block.shape[0]
     half = orb_rows // 2
-    before, after = halo_planes(orbital_block, "grid", 6)
     local_part = local_terms(orbital_block, potential)
-    local_part, before, after = lax.optimization_barrier((local_part, before, after))
-    first_a = filter_step(local_part, orbital_block, before, after, 1.0, start=0, count=half)
-    first_b = filter_step(local_part, orbital_block, before, after, 1.0, start=half, count=orb_rows - half)
+    before_0, after_0 = halo_planes(orbital_block[:half], "grid", 6)
+    local_part, before_0, after_0 = lax.optimization_barrier((local_part, before_0, after_0))
+    second_rows, before_0, after_0 = lax.optimization_barrier((orbital_block[half:], before_0, after_0))
+    before_1, after_1 = halo_planes(second_rows, "grid", 6)
+    first_a = filter_step(local_part, orbital_block, before_0, after_0, 1.0, start=0, count=half)
+    before_1, after_1 = lax.optimization_barrier((before_1, after_1))
+    first_b = filter_step(
+        local_part, orbital_block, before_1, after_1, 1.0, start=half, count=orb_rows - half, halo_start=0
+    )
     before_a, after_a = halo_planes(first_a, "grid", 6)
     local_a = local_terms(first_a, potential)
     local_a, before_a, after_a, first_b = lax.optimization_barrier((local_a, before_a, after_a, first_b))

time: 340 us -> 332 us (0.976)
  other arithmetic: 99.8 us -> 62.3 us
  starting transfers between devices: 54.8 us -> 69.6 us
  waiting for transfers between devices: 78.9 us -> 88.1 us
  local copies, waits for them, and re-layouts: 21.4 us -> 27.2 us
    add x3, other arithmetic: 91.7 us -> 54.2 us  [local_terms(): return -2.0 * total + potential[None] * orbital_field]
    ppermute x3 -> x4, starting transfers between devices: 12.5 us -> 32.7 us  [halo_planes(): before = lax.ppermute(last, axis, up)]
    ppermute x20, waiting for transfers between devices: 17 us -> 26 us  [group_round(): received.append(lax.ppermute(value, axis, pairs))]
    ppermute x20, starting transfers between devices: 28 us -> 21.2 us  [group_round(): received.append(lax.ppermute(value, axis, pairs))]
    slice x0 -> x1, local copies, waits for them, and re-layouts: none -> 4.31 us  [local(): orbital_block[half:]]
  transfers between devices with their start and end apart: 28 -> 30, of which waited for: 17 -> 19; matrix products, arithmetic and copies ran while one was open for 30% -> 20% of each run, Pallas kernels for 5% -> 7%
where the time goes in v3:
time: 332 us; the launch traced here: 331 us
  waiting for transfers between devices  88.1 us (27%)
  starting transfers between devices  69.6 us (21%)
  other arithmetic  62.3 us (19%)
  Pallas kernels  40.3 us (12%)
  blocking collectives  33.3 us (10%)
  local copies, waits for them, and re-layouts  27.2 us (8%)
  matrix products  9.06 us (3%)
    add x3, other arithmetic, local_terms(): return -2.0 * total + potential[None] * orbital_field  54.2 us
    all_to_all x1, waiting for transfers between devices, local(): orbitals = lax.all_to_all(orbitals, 'orb', 0, 1, tiled=True)  49.6 us
    all_to_all x1, blocking collectives, spread_cells(): lax.all_to_all(chunks, 'orb', 1, 0, tiled=True)  33.3 us
    ppermute x4, starting transfers between devices, halo_planes(): before = lax.ppermute(last, axis, up)  32.7 us
    ppermute x20, waiting for transfers between devices, group_round(): received.append(lax.ppermute(value, axis, pairs))  26 us
    pallas_call x4, Pallas kernels, filter_step(): pl.pallas_call(functools.partial(combine_kernel, scale, base is not None)...  23.9 us
    ppermute x20, starting transfers between devices, group_round(): received.append(lax.ppermute(value, axis, pairs))  21.2 us
    pallas_call x2, Pallas kernels, eliminate(): pl.pallas_call(eliminate_kernel, out_shape=jax.ShapeDtypeStruct(source.sh...  16.4 us
  transfers between devices with their start and end apart: 30, of which 19 were waited for; matrix products, arithmetic and copies ran while one was open for 20% of the time, Pallas kernels for 7%

profile of v3, /device:TPU:0, one launch (start us, length us, event | category | flops | bytes accessed | tf_op | source)
XLA Modules:
  0.0 330.9 jit_solution(1176862676495258825)
XLA Ops:
  0.7 4.3 %fusion.113 = (f32[16,6,48,128]{3,2,1,0:T(8,128)S(1)}, f32[16,6,48,128]{3,2,1,0:T(8,128)}) fusion(f32[32,6,48,128]{3,2,1,0:T(8,128)} %refs_4_.3), kind=kLoop, calls=%fused_computation.213 | loop fusion | bytes 9437184 | tf_op jit(solution)/shard_map/slice | solution.py:241
  7.7 16.0 %multiply_add_fusion.refs_0_ = f32[32,6,48,128]{3,2,1,0:T(8,128)} fusion(f32[32,6,48,128]{3,2,1,0:T(8,128)S(1)} %copy-done, f32[6,48,128]{2,1,0:T(8,128)S(1)} %copy-done.6), kind=kLoop, calls=%fused_computation.114 | loop fusion | flops 47185920 | bytes 9584640 | tf_op jit(solution)/shard_map/add | solution.py:49
  25.1 17.4 %collective-permute-start.4 = (f32[16,6,48,128]{3,2,1,0:T(8,128)S(1)}, f32[16,6,48,128]{3,2,1,0:T(8,128)}, u32[]{:S(2)}, u32[]{:S(2)}) collective-permute-start(f32[16,6,48,128]{3,2,1,0:T(8,128)S(1)} %get-tuple-element.22), channel_id=1, source_target_pairs={{0,4},{4,8},{8,12},{12,16},{16,20},{20,24},{24,28},{28,32},{32,36}... | collective-permute-start | bytes 7077896 | tf_op jit(solution)/shard_map/ppermute | solution.py:30
  43.8 5.6 %shard_map.41.refs_1_ = f32[16,6,48,128]{3,2,1,0:T(8,128)} custom-call(f32[32,6,48,128]{3,2,1,0:T(8,128)} %multiply_add_fusion.refs_0_, f32[32,6,48,128]{3,2,1,0:T(8,128)} %refs_4_.3, f32[16,6,48,128]{3,2,1,0:T(8,128)} %copy-done.5, f32[16,6,48,128]{3,2,1,0:T(8,128)} %collective-permute-done.1.refs_3_), custom_call_target="tpu_custom_call" | custom-call | tf_op jit(solution)/shard_map/pallas_call | solution.py:97
  49.4 4.4 %collective-permute-start.2 = (f32[16,6,48,128]{3,2,1,0:T(8,128)}, f32[16,6,48,128]{3,2,1,0:T(8,128)}, u32[]{:S(2)}, u32[]{:S(2)}) collective-permute-start(f32[16,6,48,128]{3,2,1,0:T(8,128)} %shard_map.41.refs_1_), channel_id=1, source_target_pairs={{0,4},{4,8},{8,12},{12,16},{16,20},{20,24},{24,28},{28,32},{32,36}... | collective-permute-start | bytes 7077896 | tf_op jit(solution)/shard_map/ppermute | solution.py:30
  55.1 29.8 %multiply_add_fusion.2.refs_0_ = f32[16,6,48,128]{3,2,1,0:T(8,128)} fusion(f32[16,6,48,128]{3,2,1,0:T(8,128)} %shard_map.41.refs_1_, f32[6,48,128]{2,1,0:T(8,128)S(1)} %copy-done.6), kind=kLoop, calls=%fused_computation.191 | loop fusion | flops 23592960 | bytes 4866048 | tf_op jit(solution)/shard_map/add | solution.py:49
  84.9 5.6 %shard_map.42.refs_1_ = f32[16,6,48,128]{3,2,1,0:T(8,128)} custom-call(f32[32,6,48,128]{3,2,1,0:T(8,128)} %multiply_add_fusion.refs_0_, f32[32,6,48,128]{3,2,1,0:T(8,128)} %refs_4_.3, f32[16,6,48,128]{3,2,1,0:T(8,128)} %collective-permute-done.4.refs_2_, f32[16,6,48,128]{3,2,1,0:T(8,128)} %collective-permute-done.5.refs_3_), custom_call_target="tpu_custom_call" | custom-call | tf_op jit(solution)/shard_map/pallas_call | solution.py:97
  90.5 9.4 %collective-permute-start.6 = (f32[16,6,48,128]{3,2,1,0:T(8,128)}, f32[16,6,48,128]{3,2,1,0:T(8,128)}, u32[]{:S(2)}, u32[]{:S(2)}) collective-permute-start(f32[16,6,48,128]{3,2,1,0:T(8,128)} %shard_map.42.refs_1_), channel_id=1, source_target_pairs={{0,4},{4,8},{8,12},{12,16},{16,20},{20,24},{24,28},{28,32},{32,36}... | collective-permute-start | bytes 7077896 | tf_op jit(solution)/shard_map/ppermute | solution.py:30
  101.2 6.4 %shard_map.43 = f32[16,6,48,128]{3,2,1,0:T(8,128)} custom-call(f32[16,6,48,128]{3,2,1,0:T(8,128)} %multiply_add_fusion.2.refs_0_, f32[16,6,48,128]{3,2,1,0:T(8,128)} %shard_map.41.refs_1_, f32[16,6,48,128]{3,2,1,0:T(8,128)} %collective-permute-done.2.refs_2_, f32[16,6,48,128]{3,2,1,0:T(8,128)} %collective-permute-done.3.refs_3_, f32[32,6,48,128]{3,2,1,0:T(8,128)} %refs_4_.3), custom_call_target="tpu_custom_call" | custom-call | tf_op jit(solution)/shard_map/pallas_call | solution.py:97
  107.6 3.2 copy.9
  110.8 5.4 %all-to-all-start = ((f32[16,4,72,128]{3,2,0,1:T(8,128)}), f32[16,4,72,128]{3,2,0,1:T(8,128)}, u32[]{:S(2)}, u32[]{:S(2)}) async-start(f32[16,4,72,128]{3,2,0,1:T(8,128)} %copy.9), calls=%async_computation | async-start | bytes 4718592 | tf_op jit(solution)/shard_map/all_to_all | solution.py:112
  116.2 8.4 %multiply_add_fusion.1.refs_0_ = f32[16,6,48,128]{3,2,1,0:T(8,128)} fusion(f32[16,6,48,128]{3,2,1,0:T(8,128)S(1)} %copy-done.3, f32[6,48,128]{2,1,0:T(8,128)S(1)} %copy-done.6), kind=kLoop, calls=%fused_computation.190 | loop fusion | flops 23592960 | bytes 4866048 | tf_op jit(solution)/shard_map/add | solution.py:49
  124.7 6.4 %shard_map.44 = f32[16,6,48,128]{3,2,1,0:T(8,128)} custom-call(f32[16,6,48,128]{3,2,1,0:T(8,128)} %multiply_add_fusion.1.refs_0_, f32[16,6,48,128]{3,2,1,0:T(8,128)} %shard_map.42.refs_1_, f32[16,6,48,128]{3,2,1,0:T(8,128)} %collective-permute-done.6.refs_2_, f32[16,6,48,128]{3,2,1,0:T(8,128)} %collective-permute-done.7.refs_3_, f32[32,6,48,128]{3,2,1,0:T(8,128)} %refs_4_.3), custom_call_target="tpu_custom_call" | custom-call | tf_op jit(solution)/shard_map/pallas_call | solution.py:97
  131.0 3.2 copy.10
  134.3 12.5 %all-to-all-done = f32[16,4,72,128]{3,2,0,1:T(8,128)} async-done(((f32[16,4,72,128]{3,2,0,1:T(8,128)}), f32[16,4,72,128]{3,2,0,1:T(8,128)}, u32[]{:S(2)}, u32[]{:S(2)}) %all-to-all-start) | async-done | bytes 2359328 | tf_op jit(solution)/shard_map/all_to_all | solution.py:112
  146.8 33.3 %all_to_all.45 = f32[16,4,72,128]{3,2,0,1:T(8,128)S(1)} all-to-all(f32[16,4,72,128]{3,2,0,1:T(8,128)} %copy.10), channel_id=1, replica_groups=mesh['grid'=32,'orb'=4] {'orb'}, dimensions={1} | all-to-all | bytes 4718592 | tf_op jit(solution)/shard_map/all_to_all | solution.py:112
  182.1 3.4 %fusion.36 = (f32[2,2,16,72,128]{4,3,2,0,1:T(8,128)S(1)}, f32[2,2,16,72,128]{4,3,2,0,1:T(8,128)}) fusion(f32[4,1,16,72,128]{4,3,2,0,1:T(8,128)} %bitcast.3, f32[4,1,16,72,128]{4,3,2,0,1:T(8,128)S(1)} %bitcast.46), kind=kLoop, calls=%fused_computation.115 | loop fusion | flops 1179648 | bytes 9437184 | tf_op jit(solution)/shard_map/stack | solution.py:261
  186.8 2.6 convolution_bitcast_fusion.1
  190.7 3.0 collective-permute-start.10
  193.7 3.1 collective-permute-start.11
  200.9 3.5 %collective-permute-start.13 = (f32[64,128]{1,0:T(8,128)S(1)}, f32[64,128]{1,0:T(8,128)S(1)}, u32[]{:S(2)}, u32[]{:S(2)}) collective-permute-start(f32[64,128]{1,0:T(8,128)S(1)} %select_add_fusion.4), channel_id=1, source_target_pairs={{0,64},{4,68},{8,72},{12,76},{16,80},{20,84},{24,88},{28,92},{32,9... | collective-permute-start | bytes 98312 | tf_op jit(solution)/shard_map/ppermute | solution.py:154
  206.4 3.1 collective-permute-done.14
  212.4 3.6 %copy.13 = f32[2,2,16,72,128]{4,2,1,0,3:T(8,128)} copy(f32[2,2,16,72,128]{4,3,2,0,1:T(8,128)} %get-tuple-element.33) | data formatting | bytes 4718592 | tf_op jit(solution)/shard_map/slice | solution.py:222
  218.1 8.4 %shard_map.45 = f32[64,192]{1,0:T(8,128)} custom-call(f32[64,192]{1,0:T(8,128)} %pad_maximum_fusion.1.source_ref), custom_call_target="tpu_custom_call" | custom-call | tf_op jit(solution)/shard_map/pallas_call | solution.py:207
  236.2 3.1 collective-permute-done.20
  250.3 3.2 collective-permute-done.26
  254.8 8.0 %shard_map.46 = f32[64,128]{1,0:T(8,128)} custom-call(f32[64,128]{1,0:T(8,128)} %pad_maximum_fusion.2.source_ref), custom_call_target="tpu_custom_call" | custom-call | tf_op jit(solution)/shard_map/pallas_call | solution.py:207
  262.8 2.1 fusion.110
  265.5 4.9 %copy.15 = f32[128,1,72,128]{3,2,1,0:T(8,128)} copy(f32[128,1,72,128]{3,0,2,1:T(8,128)S(1)} %maximum_bitcast_fusion) | data formatting | bytes 9437184 | tf_op jit(solution)/shard_map/reshape | solution.py:266
  270.4 5.1 %all-to-all-start.2 = ((f32[128,1,72,128]{3,2,1,0:T(8,128)}), f32[128,1,72,128]{3,2,1,0:T(8,128)}, u32[]{:S(2)}, u32[]{:S(2)}) async-start(f32[128,1,72,128]{3,2,1,0:T(8,128)} %copy.15), calls=%async_computation.2 | async-start | bytes 9437184 | tf_op jit(solution)/shard_map/all_to_all | solution.py:267
  276.2 49.6 %all-to-all-done.2 = f32[128,1,72,128]{3,2,1,0:T(8,128)} async-done(((f32[128,1,72,128]{3,2,1,0:T(8,128)}), f32[128,1,72,128]{3,2,1,0:T(8,128)}, u32[]{:S(2)}, u32[]{:S(2)}) %all-to-all-start.2) | async-done | bytes 4718624 | tf_op jit(solution)/shard_map/all_to_all | solution.py:267
  325.8 5.1 %copy.16 = f32[32,4,1,72,128]{4,3,1,0,2:T(8,128)} copy(f32[32,4,1,72,128]{4,3,0,1,2:T(8,128)} %bitcast.18) | data formatting | bytes 9437184 | tf_op jit(solution)/shard_map/all_to_all | solution.py:267
  (86 shorter events, 46.8 us)
Async XLA Ops:
  0.6 7.1 %copy-start = (f32[32,6,48,128]{3,2,1,0:T(8,128)S(1)}, f32[32,6,48,128]{3,2,1,0:T(8,128)}, u32[]{:S(2)}) copy-start(f32[32,6,48,128]{3,2,1,0:T(8,128)} %refs_4_.3) | copy-start | bytes 14155780
  0.6 7.1 %copy-start.6 = (f32[6,48,128]{2,1,0:T(8,128)S(1)}, f32[6,48,128]{2,1,0:T(8,128)}, u32[]{:S(2)}) copy-start(f32[6,48,128]{2,1,0:T(8,128)} %param.3) | copy-start | bytes 442372
  5.0 18.7 %collective-permute-start = (f32[16,6,48,128]{3,2,1,0:T(8,128)}, f32[16,6,48,128]{3,2,1,0:T(8,128)S(1)}, u32[]{:S(2)}, u32[]{:S(2)}) collective-permute-start(f32[16,6,48,128]{3,2,1,0:T(8,128)} %get-tuple-element.35), channel_id=1, source_target_pairs={{0,4},{4,8},{8,12},{12,16},{16,20},{20,24},{24,28},{28,32},{32,36}... | collective-permute-start | bytes 7077896 | tf_op jit(solution)/shard_map/ppermute | solution.py:30
  6.4 17.3 %collective-permute-start.1 = (f32[16,6,48,128]{3,2,1,0:T(8,128)}, f32[16,6,48,128]{3,2,1,0:T(8,128)}, u32[]{:S(2)}, u32[]{:S(2)}) collective-permute-start(f32[16,6,48,128]{3,2,1,0:T(8,128)} %get-tuple-element.35), channel_id=1, source_target_pairs={{4,0},{8,4},{12,8},{16,12},{20,16},{24,20},{28,24},{32,28},{36,32}... | collective-permute-start | bytes 7077896 | tf_op jit(solution)/shard_map/ppermute | solution.py:31
  25.1 59.7 %collective-permute-start.4 = (f32[16,6,48,128]{3,2,1,0:T(8,128)S(1)}, f32[16,6,48,128]{3,2,1,0:T(8,128)}, u32[]{:S(2)}, u32[]{:S(2)}) collective-permute-start(f32[16,6,48,128]{3,2,1,0:T(8,128)S(1)} %get-tuple-element.22), channel_id=1, source_target_pairs={{0,4},{4,8},{8,12},{12,16},{16,20},{20,24},{24,28},{28,32},{32,36}... | collective-permute-start | bytes 7077896 | tf_op jit(solution)/shard_map/ppermute | solution.py:30
  42.5 42.4 %collective-permute-start.5 = (f32[16,6,48,128]{3,2,1,0:T(8,128)S(1)}, f32[16,6,48,128]{3,2,1,0:T(8,128)}, u32[]{:S(2)}, u32[]{:S(2)}) collective-permute-start(f32[16,6,48,128]{3,2,1,0:T(8,128)S(1)} %get-tuple-element.22), channel_id=1, source_target_pairs={{4,0},{8,4},{12,8},{16,12},{20,16},{24,20},{28,24},{32,28},{36,32}... | collective-permute-start | bytes 7077896 | tf_op jit(solution)/shard_map/ppermute | solution.py:31
  49.4 41.1 %collective-permute-start.2 = (f32[16,6,48,128]{3,2,1,0:T(8,128)}, f32[16,6,48,128]{3,2,1,0:T(8,128)}, u32[]{:S(2)}, u32[]{:S(2)}) collective-permute-start(f32[16,6,48,128]{3,2,1,0:T(8,128)} %shard_map.41.refs_1_), channel_id=1, source_target_pairs={{0,4},{4,8},{8,12},{12,16},{16,20},{20,24},{24,28},{28,32},{32,36}... | collective-permute-start | bytes 7077896 | tf_op jit(solution)/shard_map/ppermute | solution.py:30
  53.8 36.7 %collective-permute-start.3 = (f32[16,6,48,128]{3,2,1,0:T(8,128)}, f32[16,6,48,128]{3,2,1,0:T(8,128)}, u32[]{:S(2)}, u32[]{:S(2)}) collective-permute-start(f32[16,6,48,128]{3,2,1,0:T(8,128)} %shard_map.41.refs_1_), channel_id=1, source_target_pairs={{4,0},{8,4},{12,8},{16,12},{20,16},{24,20},{28,24},{32,28},{36,32}... | collective-permute-start | bytes 7077896 | tf_op jit(solution)/shard_map/ppermute | solution.py:31
  90.5 34.2 %collective-permute-start.6 = (f32[16,6,48,128]{3,2,1,0:T(8,128)}, f32[16,6,48,128]{3,2,1,0:T(8,128)}, u32[]{:S(2)}, u32[]{:S(2)}) collective-permute-start(f32[16,6,48,128]{3,2,1,0:T(8,128)} %shard_map.42.refs_1_), channel_id=1, source_target_pairs={{0,4},{4,8},{8,12},{12,16},{16,20},{20,24},{24,28},{28,32},{32,36}... | collective-permute-start | bytes 7077896 | tf_op jit(solution)/shard_map/ppermute | solution.py:30
  100.0 24.7 %collective-permute-start.7 = (f32[16,6,48,128]{3,2,1,0:T(8,128)}, f32[16,6,48,128]{3,2,1,0:T(8,128)}, u32[]{:S(2)}, u32[]{:S(2)}) collective-permute-start(f32[16,6,48,128]{3,2,1,0:T(8,128)} %shard_map.42.refs_1_), channel_id=1, source_target_pairs={{4,0},{8,4},{12,8},{16,12},{20,16},{24,20},{28,24},{32,28},{36,32}... | collective-permute-start | bytes 7077896 | tf_op jit(solution)/shard_map/ppermute | solution.py:31
  110.8 36.0 %all-to-all-start = ((f32[16,4,72,128]{3,2,0,1:T(8,128)}), f32[16,4,72,128]{3,2,0,1:T(8,128)}, u32[]{:S(2)}, u32[]{:S(2)}) async-start(f32[16,4,72,128]{3,2,0,1:T(8,128)} %copy.9), calls=%async_computation | async-start | bytes 4718592 | tf_op jit(solution)/shard_map/all_to_all | solution.py:112
  189.4 1.3 collective-permute-start.8
  190.7 6.3 %collective-permute-start.10 = (f32[64,128]{1,0:T(8,128)S(1)}, f32[64,128]{1,0:T(8,128)S(1)}, u32[]{:S(2)}, u32[]{:S(2)}) collective-permute-start(f32[64,128]{1,0:T(8,128)S(1)} %select_add_fusion.5), channel_id=1, source_target_pairs={{0,16},{4,20},{8,24},{12,28},{16,0},{20,4},{24,8},{28,12},{32,48},... | collective-permute-start | bytes 98312 | tf_op jit(solution)/shard_map/ppermute | solution.py:154
  193.7 5.1 %collective-permute-start.11 = (f32[64,128]{1,0:T(8,128)S(1)}, f32[64,128]{1,0:T(8,128)S(1)}, u32[]{:S(2)}, u32[]{:S(2)}) collective-permute-start(f32[64,128]{1,0:T(8,128)S(1)} %select_add_fusion.5), channel_id=1, source_target_pairs={{0,8},{4,12},{8,16},{12,20},{16,24},{20,28},{24,0},{28,4},{32,40},... | collective-permute-start | bytes 98312 | tf_op jit(solution)/shard_map/ppermute | solution.py:154
  196.8 3.9 %collective-permute-start.9 = (f32[64,128]{1,0:T(8,128)S(1)}, f32[64,128]{1,0:T(8,128)S(1)}, u32[]{:S(2)}, u32[]{:S(2)}) collective-permute-start(f32[64,128]{1,0:T(8,128)S(1)} %select_add_fusion.5), channel_id=1, source_target_pairs={{0,24},{4,28},{8,0},{12,4},{16,8},{20,12},{24,16},{28,20},{32,56},... | collective-permute-start | bytes 98312 | tf_op jit(solution)/shard_map/ppermute | solution.py:154
  200.8 4.2 %collective-permute-start.12 = (f32[64,128]{1,0:T(8,128)S(1)}, f32[64,128]{1,0:T(8,128)S(1)}, u32[]{:S(2)}, u32[]{:S(2)}) collective-permute-start(f32[64,128]{1,0:T(8,128)S(1)} %select_add_fusion.4), channel_id=1, source_target_pairs={{0,96},{4,100},{8,104},{12,108},{16,112},{20,116},{24,120},{28,124... | collective-permute-start | bytes 98312 | tf_op jit(solution)/shard_map/ppermute | solution.py:154
  200.9 5.5 %collective-permute-start.13 = (f32[64,128]{1,0:T(8,128)S(1)}, f32[64,128]{1,0:T(8,128)S(1)}, u32[]{:S(2)}, u32[]{:S(2)}) collective-permute-start(f32[64,128]{1,0:T(8,128)S(1)} %select_add_fusion.4), channel_id=1, source_target_pairs={{0,64},{4,68},{8,72},{12,76},{16,80},{20,84},{24,88},{28,92},{32,9... | collective-permute-start | bytes 98312 | tf_op jit(solution)/shard_map/ppermute | solution.py:154
  204.4 5.1 %collective-permute-start.14 = (f32[64,128]{1,0:T(8,128)S(1)}, f32[64,128]{1,0:T(8,128)S(1)}, u32[]{:S(2)}, u32[]{:S(2)}) collective-permute-start(f32[64,128]{1,0:T(8,128)S(1)} %select_add_fusion.4), channel_id=1, source_target_pairs={{0,32},{4,36},{8,40},{12,44},{16,48},{20,52},{24,56},{28,60},{32,6... | collective-permute-start | bytes 98312 | tf_op jit(solution)/shard_map/ppermute | solution.py:154
  209.6 6.4 %collective-permute-start.15 = (f32[64,128]{1,0:T(8,128)S(1)}, f32[64,128]{1,0:T(8,128)S(1)}, u32[]{:S(2)}, u32[]{:S(2)}) collective-permute-start(f32[64,128]{1,0:T(8,128)S(1)} %select_add_fusion.3), channel_id=1, source_target_pairs={{0,3},{1,0},{2,1},{3,2},{4,7},{5,4},{6,5},{7,6},{8,11},{9,8},{10,9... | collective-permute-start | bytes 98312 | tf_op jit(solution)/shard_map/ppermute | solution.py:154
  210.8 5.4 %collective-permute-start.16 = (f32[64,128]{1,0:T(8,128)S(1)}, f32[64,128]{1,0:T(8,128)S(1)}, u32[]{:S(2)}, u32[]{:S(2)}) collective-permute-start(f32[64,128]{1,0:T(8,128)S(1)} %select_add_fusion.3), channel_id=1, source_target_pairs={{0,2},{1,3},{2,0},{3,1},{4,6},{5,7},{6,4},{7,5},{8,10},{9,11},{10,... | collective-permute-start | bytes 98312 | tf_op jit(solution)/shard_map/ppermute | solution.py:154
  212.3 5.1 %collective-permute-start.17 = (f32[64,128]{1,0:T(8,128)S(1)}, f32[64,128]{1,0:T(8,128)S(1)}, u32[]{:S(2)}, u32[]{:S(2)}) collective-permute-start(f32[64,128]{1,0:T(8,128)S(1)} %select_add_fusion.3), channel_id=1, source_target_pairs={{0,1},{1,2},{2,3},{3,0},{4,5},{5,6},{6,7},{7,4},{8,9},{9,10},{10,1... | collective-permute-start | bytes 98312 | tf_op jit(solution)/shard_map/ppermute | solution.py:154
  231.0 1.3 collective-permute-start.18
  232.3 4.0 %collective-permute-start.19 = (f32[64,64]{1,0:T(8,128)S(1)}, f32[64,64]{1,0:T(8,128)S(1)}, u32[]{:S(2)}, u32[]{:S(2)}) collective-permute-start(f32[64,64]{1,0:T(8,128)S(1)} %select_add_fusion.2), channel_id=1, source_target_pairs={{0,24},{4,28},{8,0},{12,4},{16,8},{20,12},{24,16},{28,20},{32,56},... | collective-permute-start | bytes 49160 | tf_op jit(solution)/shard_map/ppermute | solution.py:154
  233.6 5.7 %collective-permute-start.20 = (f32[64,64]{1,0:T(8,128)S(1)}, f32[64,64]{1,0:T(8,128)S(1)}, u32[]{:S(2)}, u32[]{:S(2)}) collective-permute-start(f32[64,64]{1,0:T(8,128)S(1)} %select_add_fusion.2), channel_id=1, source_target_pairs={{0,16},{4,20},{8,24},{12,28},{16,0},{20,4},{24,8},{28,12},{32,48},... | collective-permute-start | bytes 49160 | tf_op jit(solution)/shard_map/ppermute | solution.py:154
  234.4 5.2 %collective-permute-start.21 = (f32[64,64]{1,0:T(8,128)S(1)}, f32[64,64]{1,0:T(8,128)S(1)}, u32[]{:S(2)}, u32[]{:S(2)}) collective-permute-start(f32[64,64]{1,0:T(8,128)S(1)} %select_add_fusion.2), channel_id=1, source_target_pairs={{0,8},{4,12},{8,16},{12,20},{16,24},{20,28},{24,0},{28,4},{32,40},... | collective-permute-start | bytes 49160 | tf_op jit(solution)/shard_map/ppermute | solution.py:154
  239.7 4.0 %collective-permute-start.22 = (f32[64,64]{1,0:T(8,128)S(1)}, f32[64,64]{1,0:T(8,128)S(1)}, u32[]{:S(2)}, u32[]{:S(2)}) collective-permute-start(f32[64,64]{1,0:T(8,128)S(1)} %select_add_fusion.1), channel_id=1, source_target_pairs={{0,96},{4,100},{8,104},{12,108},{16,112},{20,116},{24,120},{28,124... | collective-permute-start | bytes 49160 | tf_op jit(solution)/shard_map/ppermute | solution.py:154
  239.8 5.5 %collective-permute-start.23 = (f32[64,64]{1,0:T(8,128)S(1)}, f32[64,64]{1,0:T(8,128)S(1)}, u32[]{:S(2)}, u32[]{:S(2)}) collective-permute-start(f32[64,64]{1,0:T(8,128)S(1)} %select_add_fusion.1), channel_id=1, source_target_pairs={{0,64},{4,68},{8,72},{12,76},{16,80},{20,84},{24,88},{28,92},{32,9... | collective-permute-start | bytes 49160 | tf_op jit(solution)/shard_map/ppermute | solution.py:154
  241.2 5.1 %collective-permute-start.24 = (f32[64,64]{1,0:T(8,128)S(1)}, f32[64,64]{1,0:T(8,128)S(1)}, u32[]{:S(2)}, u32[]{:S(2)}) collective-permute-start(f32[64,64]{1,0:T(8,128)S(1)} %select_add_fusion.1), channel_id=1, source_target_pairs={{0,32},{4,36},{8,40},{12,44},{16,48},{20,52},{24,56},{28,60},{32,6... | collective-permute-start | bytes 49160 | tf_op jit(solution)/shard_map/ppermute | solution.py:154
  246.4 4.0 %collective-permute-start.25 = (f32[64,64]{1,0:T(8,128)S(1)}, f32[64,64]{1,0:T(8,128)S(1)}, u32[]{:S(2)}, u32[]{:S(2)}) collective-permute-start(f32[64,64]{1,0:T(8,128)S(1)} %select_add_fusion), channel_id=1, source_target_pairs={{0,3},{1,0},{2,1},{3,2},{4,7},{5,4},{6,5},{7,6},{8,11},{9,8},{10,9... | collective-permute-start | bytes 49160 | tf_op jit(solution)/shard_map/ppermute | solution.py:154
  248.1 5.4 %collective-permute-start.26 = (f32[64,64]{1,0:T(8,128)S(1)}, f32[64,64]{1,0:T(8,128)S(1)}, u32[]{:S(2)}, u32[]{:S(2)}) collective-permute-start(f32[64,64]{1,0:T(8,128)S(1)} %select_add_fusion), channel_id=1, source_target_pairs={{0,2},{1,3},{2,0},{3,1},{4,6},{5,7},{6,4},{7,5},{8,10},{9,11},{10,... | collective-permute-start | bytes 49160 | tf_op jit(solution)/shard_map/ppermute | solution.py:154
  249.0 5.1 %collective-permute-start.27 = (f32[64,64]{1,0:T(8,128)S(1)}, f32[64,64]{1,0:T(8,128)S(1)}, u32[]{:S(2)}, u32[]{:S(2)}) collective-permute-start(f32[64,64]{1,0:T(8,128)S(1)} %select_add_fusion), channel_id=1, source_target_pairs={{0,1},{1,2},{2,3},{3,0},{4,5},{5,6},{6,7},{7,4},{8,9},{9,10},{10,1... | collective-permute-start | bytes 49160 | tf_op jit(solution)/shard_map/ppermute | solution.py:154
  270.4 55.4 %all-to-all-start.2 = ((f32[128,1,72,128]{3,2,1,0:T(8,128)}), f32[128,1,72,128]{3,2,1,0:T(8,128)}, u32[]{:S(2)}, u32[]{:S(2)}) async-start(f32[128,1,72,128]{3,2,1,0:T(8,128)} %copy.15), calls=%async_computation.2 | async-start | bytes 9437184 | tf_op jit(solution)/shard_map/all_to_all | solution.py:267
  (8 other events, 24.6 us)

commit v4 on v3

--- a/solution.py
+++ b/solution.py
@@ -103,6 +103,23 @@
     )(*operands)
 
 
+def copy_kernel(source_ref, result_ref):
+    result_ref[...] = source_ref[...]
+
+
+def take_rows(value, start, count):
+    block_rows = 8 if count % 8 == 0 and start % 8 == 0 else 1
+    offset = start // block_rows
+    block = (block_rows,) + value.shape[1:]
+    return pl.pallas_call(
+        copy_kernel,
+        grid=(count // block_rows,),
+        in_specs=[pl.BlockSpec(block, lambda i: (i + offset, 0, 0, 0))],
+        out_specs=pl.BlockSpec(block, lambda i: (i, 0, 0, 0)),
+        out_shape=jax.ShapeDtypeStruct((count,) + value.shape[1:], value.dtype),
+    )(value)
+
+
 def spread_cells(filtered):
     rows = filtered.shape[0]
     parts = lax.axis_size("orb")
@@ -236,9 +253,9 @@
     orb_rows = orbital_block.shape[0]
     half = orb_rows // 2
     local_part = local_terms(orbital_block, potential)
-    before_0, after_0 = halo_planes(orbital_block[:half], "grid", 6)
+    before_0, after_0 = halo_planes(take_rows(orbital_block, 0, half), "grid", 6)
     local_part, before_0, after_0 = lax.optimization_barrier((local_part, before_0, after_0))
-    second_rows, before_0, after_0 = lax.optimization_barrier((orbital_block[half:], before_0, after_0))
+    second_rows, before_0, after_0 = lax.optimization_barrier((take_rows(orbital_block, half, orb_rows - half), before_0, after_0))
     before_1, after_1 = halo_planes(second_rows, "grid", 6)
     first_a = filter_step(local_part, orbital_block, before_0, after_0, 1.0, start=0, count=half)
     before_1, after_1 = lax.optimization_barrier((before_1, after_1))

time: 332 us -> 359 us (1.081)
  other arithmetic: 62.3 us -> 98.5 us
  starting transfers between devices: 69.6 us -> 60.4 us
  local copies, waits for them, and re-layouts: 27.2 us -> 21.4 us
  Pallas kernels: 40.3 us -> 45.9 us
    add x3, other arithmetic: 54.2 us -> 90.4 us  [local_terms(): return -2.0 * total + potential[None] * orbital_field]
    ppermute x4, starting transfers between devices: 32.7 us -> 23.7 us  [halo_planes(): before = lax.ppermute(last, axis, up)]
    pallas_call x0 -> x2, Pallas kernels: none -> 5.58 us  [take_rows(): pl.pallas_call(copy_kernel, grid=(count // block_rows,), in_specs=[pl.Blo...]
    slice x1 -> x0, local copies, waits for them, and re-layouts: 4.31 us -> none  [local(): orbital_block[half:]]
  transfers between devices with their start and end apart: 30 -> 30, of which waited for: 19 -> 19; matrix products, arithmetic and copies ran while one was open for 20% -> 28% of each run, Pallas kernels for 7% -> 7%
where the time goes in v4:
time: 359 us; the launch traced here: 358 us
  other arithmetic  98.5 us (27%)
  waiting for transfers between devices  88.2 us (25%)
  starting transfers between devices  60.4 us (17%)
  Pallas kernels  45.9 us (13%)
  blocking collectives  33.3 us (9%)
  local copies, waits for them, and re-layouts  21.4 us (6%)
  matrix products  9.05 us (3%)
    add x3, other arithmetic, local_terms(): return -2.0 * total + potential[None] * orbital_field  90.4 us
    all_to_all x1, waiting for transfers between devices, local(): orbitals = lax.all_to_all(orbitals, 'orb', 0, 1, tiled=True)  49.5 us
    all_to_all x1, blocking collectives, spread_cells(): lax.all_to_all(chunks, 'orb', 1, 0, tiled=True)  33.3 us
    ppermute x20, waiting for transfers between devices, group_round(): received.append(lax.ppermute(value, axis, pairs))  26.2 us
    pallas_call x4, Pallas kernels, filter_step(): pl.pallas_call(functools.partial(combine_kernel, scale, base is not None)...  24 us
    ppermute x4, starting transfers between devices, halo_planes(): before = lax.ppermute(last, axis, up)  23.7 us
    ppermute x20, starting transfers between devices, group_round(): received.append(lax.ppermute(value, axis, pairs))  21 us
    pallas_call x2, Pallas kernels, eliminate(): pl.pallas_call(eliminate_kernel, out_shape=jax.ShapeDtypeStruct(source.sh...  16.4 us
  transfers between devices with their start and end apart: 30, of which 19 were waited for; matrix products, arithmetic and copies ran while one was open for 28% of the time, Pallas kernels for 7%

profile of v4, /device:TPU:0, one launch (start us, length us, event | category | flops | bytes accessed | tf_op | source)
XLA Modules:
  0.0 357.8 jit_solution(6837808200901373405)
XLA Ops:
  0.6 2.8 shard_map.41
  3.4 2.8 collective-permute-start
  7.5 2.8 shard_map.42
  10.3 52.4 %multiply_add_fusion.refs_0_ = f32[32,6,48,128]{3,2,1,0:T(8,128)} fusion(f32[32,6,48,128]{3,2,1,0:T(8,128)} %refs_4_.3, f32[6,48,128]{2,1,0:T(8,128)S(1)} %copy-done.5), kind=kLoop, calls=%fused_computation.114 | loop fusion | flops 47185920 | bytes 9584640 | tf_op jit(solution)/shard_map/add | solution.py:49
  62.8 5.0 %collective-permute-start.4 = (f32[16,6,48,128]{3,2,1,0:T(8,128)S(1)}, f32[16,6,48,128]{3,2,1,0:T(8,128)}, u32[]{:S(2)}, u32[]{:S(2)}) collective-permute-start(f32[16,6,48,128]{3,2,1,0:T(8,128)S(1)} %copy-done.4), channel_id=1, source_target_pairs={{0,4},{4,8},{8,12},{12,16},{16,20},{20,24},{24,28},{28,32},{32,36}... | collective-permute-start | bytes 7077896 | tf_op jit(solution)/shard_map/ppermute | solution.py:30
  69.1 5.6 %shard_map.43.refs_1_ = f32[16,6,48,128]{3,2,1,0:T(8,128)} custom-call(f32[32,6,48,128]{3,2,1,0:T(8,128)} %multiply_add_fusion.refs_0_, f32[32,6,48,128]{3,2,1,0:T(8,128)} %refs_4_.3, f32[16,6,48,128]{3,2,1,0:T(8,128)} %collective-permute-done.refs_2_, f32[16,6,48,128]{3,2,1,0:T(8,128)} %collective-permute-done.1.refs_3_), custom_call_target="tpu_custom_call" | custom-call | tf_op jit(solution)/shard_map/pallas_call | solution.py:97
  74.7 4.5 %collective-permute-start.2 = (f32[16,6,48,128]{3,2,1,0:T(8,128)}, f32[16,6,48,128]{3,2,1,0:T(8,128)}, u32[]{:S(2)}, u32[]{:S(2)}) collective-permute-start(f32[16,6,48,128]{3,2,1,0:T(8,128)} %shard_map.43.refs_1_), channel_id=1, source_target_pairs={{0,4},{4,8},{8,12},{12,16},{16,20},{20,24},{24,28},{28,32},{32,36}... | collective-permute-start | bytes 7077896 | tf_op jit(solution)/shard_map/ppermute | solution.py:30
  80.4 29.5 %multiply_add_fusion.2.refs_0_ = f32[16,6,48,128]{3,2,1,0:T(8,128)} fusion(f32[16,6,48,128]{3,2,1,0:T(8,128)} %shard_map.43.refs_1_, f32[6,48,128]{2,1,0:T(8,128)S(1)} %copy-done.5), kind=kLoop, calls=%fused_computation.191 | loop fusion | flops 23592960 | bytes 4866048 | tf_op jit(solution)/shard_map/add | solution.py:49
  109.9 5.6 %shard_map.44.refs_1_ = f32[16,6,48,128]{3,2,1,0:T(8,128)} custom-call(f32[32,6,48,128]{3,2,1,0:T(8,128)} %multiply_add_fusion.refs_0_, f32[32,6,48,128]{3,2,1,0:T(8,128)} %refs_4_.3, f32[16,6,48,128]{3,2,1,0:T(8,128)} %collective-permute-done.4.refs_2_, f32[16,6,48,128]{3,2,1,0:T(8,128)} %collective-permute-done.5.refs_3_), custom_call_target="tpu_custom_call" | custom-call | tf_op jit(solution)/shard_map/pallas_call | solution.py:97
  115.6 11.4 %collective-permute-start.6 = (f32[16,6,48,128]{3,2,1,0:T(8,128)}, f32[16,6,48,128]{3,2,1,0:T(8,128)}, u32[]{:S(2)}, u32[]{:S(2)}) collective-permute-start(f32[16,6,48,128]{3,2,1,0:T(8,128)} %shard_map.44.refs_1_), channel_id=1, source_target_pairs={{0,4},{4,8},{8,12},{12,16},{16,20},{20,24},{24,28},{28,32},{32,36}... | collective-permute-start | bytes 7077896 | tf_op jit(solution)/shard_map/ppermute | solution.py:30
  128.3 6.4 %shard_map.45 = f32[16,6,48,128]{3,2,1,0:T(8,128)} custom-call(f32[16,6,48,128]{3,2,1,0:T(8,128)} %multiply_add_fusion.2.refs_0_, f32[16,6,48,128]{3,2,1,0:T(8,128)} %shard_map.43.refs_1_, f32[16,6,48,128]{3,2,1,0:T(8,128)} %collective-permute-done.2.refs_2_, f32[16,6,48,128]{3,2,1,0:T(8,128)} %collective-permute-done.3.refs_3_, f32[32,6,48,128]{3,2,1,0:T(8,128)} %refs_4_.3), custom_call_target="tpu_custom_call" | custom-call | tf_op jit(solution)/shard_map/pallas_call | solution.py:97
  134.6 3.2 copy.9
  137.8 5.4 %all-to-all-start = ((f32[16,4,72,128]{3,2,0,1:T(8,128)}), f32[16,4,72,128]{3,2,0,1:T(8,128)}, u32[]{:S(2)}, u32[]{:S(2)}) async-start(f32[16,4,72,128]{3,2,0,1:T(8,128)} %copy.9), calls=%async_computation | async-start | bytes 4718592 | tf_op jit(solution)/shard_map/all_to_all | solution.py:129
  143.3 8.4 %multiply_add_fusion.1.refs_0_ = f32[16,6,48,128]{3,2,1,0:T(8,128)} fusion(f32[16,6,48,128]{3,2,1,0:T(8,128)S(1)} %copy-done.2, f32[6,48,128]{2,1,0:T(8,128)S(1)} %copy-done.5), kind=kLoop, calls=%fused_computation.190 | loop fusion | flops 23592960 | bytes 4866048 | tf_op jit(solution)/shard_map/add | solution.py:49
  151.7 6.4 %shard_map.46 = f32[16,6,48,128]{3,2,1,0:T(8,128)} custom-call(f32[16,6,48,128]{3,2,1,0:T(8,128)} %multiply_add_fusion.1.refs_0_, f32[16,6,48,128]{3,2,1,0:T(8,128)} %shard_map.44.refs_1_, f32[16,6,48,128]{3,2,1,0:T(8,128)} %collective-permute-done.6.refs_2_, f32[16,6,48,128]{3,2,1,0:T(8,128)} %collective-permute-done.7.refs_3_, f32[32,6,48,128]{3,2,1,0:T(8,128)} %refs_4_.3), custom_call_target="tpu_custom_call" | custom-call | tf_op jit(solution)/shard_map/pallas_call | solution.py:97
  158.1 3.2 copy.10
  161.3 12.5 %all-to-all-done = f32[16,4,72,128]{3,2,0,1:T(8,128)} async-done(((f32[16,4,72,128]{3,2,0,1:T(8,128)}), f32[16,4,72,128]{3,2,0,1:T(8,128)}, u32[]{:S(2)}, u32[]{:S(2)}) %all-to-all-start) | async-done | bytes 2359328 | tf_op jit(solution)/shard_map/all_to_all | solution.py:129
  173.8 33.3 %all_to_all.45 = f32[16,4,72,128]{3,2,0,1:T(8,128)S(1)} all-to-all(f32[16,4,72,128]{3,2,0,1:T(8,128)} %copy.10), channel_id=1, replica_groups=mesh['grid'=32,'orb'=4] {'orb'}, dimensions={1} | all-to-all | bytes 4718592 | tf_op jit(solution)/shard_map/all_to_all | solution.py:129
  209.1 3.4 fusion.36
  213.8 2.6 convolution_bitcast_fusion.1
  218.7 5.1 %collective-permute-start.11 = (f32[64,128]{1,0:T(8,128)S(1)}, f32[64,128]{1,0:T(8,128)S(1)}, u32[]{:S(2)}, u32[]{:S(2)}) collective-permute-start(f32[64,128]{1,0:T(8,128)S(1)} %select_add_fusion.5), channel_id=1, source_target_pairs={{0,8},{4,12},{8,16},{12,20},{16,24},{20,28},{24,0},{28,4},{32,40},... | collective-permute-start | bytes 98312 | tf_op jit(solution)/shard_map/ppermute | solution.py:171
  227.9 3.5 collective-permute-start.13
  233.4 3.1 collective-permute-done.14
  239.4 3.5 copy.13
  245.1 8.4 %shard_map.47 = f32[64,192]{1,0:T(8,128)} custom-call(f32[64,192]{1,0:T(8,128)} %pad_maximum_fusion.1.source_ref), custom_call_target="tpu_custom_call" | custom-call | tf_op jit(solution)/shard_map/pallas_call | solution.py:224
  263.2 3.1 collective-permute-done.20
  277.3 3.2 collective-permute-done.26
  281.7 8.0 %shard_map.48 = f32[64,128]{1,0:T(8,128)} custom-call(f32[64,128]{1,0:T(8,128)} %pad_maximum_fusion.2.source_ref), custom_call_target="tpu_custom_call" | custom-call | tf_op jit(solution)/shard_map/pallas_call | solution.py:224
  292.4 4.9 %copy.15 = f32[128,1,72,128]{3,2,1,0:T(8,128)} copy(f32[128,1,72,128]{3,0,2,1:T(8,128)S(1)} %maximum_bitcast_fusion) | data formatting | bytes 9437184 | tf_op jit(solution)/shard_map/reshape | solution.py:283
  297.4 5.1 %all-to-all-start.2 = ((f32[128,1,72,128]{3,2,1,0:T(8,128)}), f32[128,1,72,128]{3,2,1,0:T(8,128)}, u32[]{:S(2)}, u32[]{:S(2)}) async-start(f32[128,1,72,128]{3,2,1,0:T(8,128)} %copy.15), calls=%async_computation.2 | async-start | bytes 9437184 | tf_op jit(solution)/shard_map/all_to_all | solution.py:284
  303.2 49.5 %all-to-all-done.2 = f32[128,1,72,128]{3,2,1,0:T(8,128)} async-done(((f32[128,1,72,128]{3,2,1,0:T(8,128)}), f32[128,1,72,128]{3,2,1,0:T(8,128)}, u32[]{:S(2)}, u32[]{:S(2)}) %all-to-all-start.2) | async-done | bytes 4718624 | tf_op jit(solution)/shard_map/all_to_all | solution.py:284
  352.7 5.1 %copy.16 = f32[32,4,1,72,128]{4,3,1,0,2:T(8,128)} copy(f32[32,4,1,72,128]{4,3,0,1,2:T(8,128)} %bitcast.18) | data formatting | bytes 9437184 | tf_op jit(solution)/shard_map/all_to_all | solution.py:284
  (85 shorter events, 47.0 us)
Async XLA Ops:
  3.4 6.9 %copy-start.5 = (f32[6,48,128]{2,1,0:T(8,128)S(1)}, f32[6,48,128]{2,1,0:T(8,128)}, u32[]{:S(2)}) copy-start(f32[6,48,128]{2,1,0:T(8,128)} %param.3) | copy-start | bytes 442372
  3.4 59.4 %collective-permute-start = (f32[16,6,48,128]{3,2,1,0:T(8,128)}, f32[16,6,48,128]{3,2,1,0:T(8,128)}, u32[]{:S(2)}, u32[]{:S(2)}) collective-permute-start(f32[16,6,48,128]{3,2,1,0:T(8,128)} %shard_map.41), channel_id=1, source_target_pairs={{0,4},{4,8},{8,12},{12,16},{16,20},{20,24},{24,28},{28,32},{32,36}... | collective-permute-start | bytes 7077896 | tf_op jit(solution)/shard_map/ppermute | solution.py:30
  6.3 56.5 %collective-permute-start.1 = (f32[16,6,48,128]{3,2,1,0:T(8,128)}, f32[16,6,48,128]{3,2,1,0:T(8,128)}, u32[]{:S(2)}, u32[]{:S(2)}) collective-permute-start(f32[16,6,48,128]{3,2,1,0:T(8,128)} %shard_map.41), channel_id=1, source_target_pairs={{4,0},{8,4},{12,8},{16,12},{20,16},{24,20},{28,24},{32,28},{36,32}... | collective-permute-start | bytes 7077896 | tf_op jit(solution)/shard_map/ppermute | solution.py:31
  10.3 52.5 %copy-start.4 = (f32[16,6,48,128]{3,2,1,0:T(8,128)S(1)}, f32[16,6,48,128]{3,2,1,0:T(8,128)}, u32[]{:S(2)}) copy-start(f32[16,6,48,128]{3,2,1,0:T(8,128)} %shard_map.42) | copy-start | bytes 7077892
  62.8 47.1 %collective-permute-start.4 = (f32[16,6,48,128]{3,2,1,0:T(8,128)S(1)}, f32[16,6,48,128]{3,2,1,0:T(8,128)}, u32[]{:S(2)}, u32[]{:S(2)}) collective-permute-start(f32[16,6,48,128]{3,2,1,0:T(8,128)S(1)} %copy-done.4), channel_id=1, source_target_pairs={{0,4},{4,8},{8,12},{12,16},{16,20},{20,24},{24,28},{28,32},{32,36}... | collective-permute-start | bytes 7077896 | tf_op jit(solution)/shard_map/ppermute | solution.py:30
  67.8 42.2 %collective-permute-start.5 = (f32[16,6,48,128]{3,2,1,0:T(8,128)S(1)}, f32[16,6,48,128]{3,2,1,0:T(8,128)}, u32[]{:S(2)}, u32[]{:S(2)}) collective-permute-start(f32[16,6,48,128]{3,2,1,0:T(8,128)S(1)} %copy-done.4), channel_id=1, source_target_pairs={{4,0},{8,4},{12,8},{16,12},{20,16},{24,20},{28,24},{32,28},{36,32}... | collective-permute-start | bytes 7077896 | tf_op jit(solution)/shard_map/ppermute | solution.py:31
  74.7 40.9 %collective-permute-start.2 = (f32[16,6,48,128]{3,2,1,0:T(8,128)}, f32[16,6,48,128]{3,2,1,0:T(8,128)}, u32[]{:S(2)}, u32[]{:S(2)}) collective-permute-start(f32[16,6,48,128]{3,2,1,0:T(8,128)} %shard_map.43.refs_1_), channel_id=1, source_target_pairs={{0,4},{4,8},{8,12},{12,16},{16,20},{20,24},{24,28},{28,32},{32,36}... | collective-permute-start | bytes 7077896 | tf_op jit(solution)/shard_map/ppermute | solution.py:30
  79.1 36.4 %collective-permute-start.3 = (f32[16,6,48,128]{3,2,1,0:T(8,128)}, f32[16,6,48,128]{3,2,1,0:T(8,128)}, u32[]{:S(2)}, u32[]{:S(2)}) collective-permute-start(f32[16,6,48,128]{3,2,1,0:T(8,128)} %shard_map.43.refs_1_), channel_id=1, source_target_pairs={{4,0},{8,4},{12,8},{16,12},{20,16},{24,20},{28,24},{32,28},{36,32}... | collective-permute-start | bytes 7077896 | tf_op jit(solution)/shard_map/ppermute | solution.py:31
  115.6 36.1 %collective-permute-start.6 = (f32[16,6,48,128]{3,2,1,0:T(8,128)}, f32[16,6,48,128]{3,2,1,0:T(8,128)}, u32[]{:S(2)}, u32[]{:S(2)}) collective-permute-start(f32[16,6,48,128]{3,2,1,0:T(8,128)} %shard_map.44.refs_1_), channel_id=1, source_target_pairs={{0,4},{4,8},{8,12},{12,16},{16,20},{20,24},{24,28},{28,32},{32,36}... | collective-permute-start | bytes 7077896 | tf_op jit(solution)/shard_map/ppermute | solution.py:30
  127.0 24.7 %collective-permute-start.7 = (f32[16,6,48,128]{3,2,1,0:T(8,128)}, f32[16,6,48,128]{3,2,1,0:T(8,128)}, u32[]{:S(2)}, u32[]{:S(2)}) collective-permute-start(f32[16,6,48,128]{3,2,1,0:T(8,128)} %shard_map.44.refs_1_), channel_id=1, source_target_pairs={{4,0},{8,4},{12,8},{16,12},{20,16},{24,20},{28,24},{32,28},{36,32}... | collective-permute-start | bytes 7077896 | tf_op jit(solution)/shard_map/ppermute | solution.py:31
  137.8 36.0 %all-to-all-start = ((f32[16,4,72,128]{3,2,0,1:T(8,128)}), f32[16,4,72,128]{3,2,0,1:T(8,128)}, u32[]{:S(2)}, u32[]{:S(2)}) async-start(f32[16,4,72,128]{3,2,0,1:T(8,128)} %copy.9), calls=%async_computation | async-start | bytes 4718592 | tf_op jit(solution)/shard_map/all_to_all | solution.py:129
  216.4 1.3 collective-permute-start.8
  217.7 6.1 %collective-permute-start.10 = (f32[64,128]{1,0:T(8,128)S(1)}, f32[64,128]{1,0:T(8,128)S(1)}, u32[]{:S(2)}, u32[]{:S(2)}) collective-permute-start(f32[64,128]{1,0:T(8,128)S(1)} %select_add_fusion.5), channel_id=1, source_target_pairs={{0,16},{4,20},{8,24},{12,28},{16,0},{20,4},{24,8},{28,12},{32,48},... | collective-permute-start | bytes 98312 | tf_op jit(solution)/shard_map/ppermute | solution.py:171
  218.7 6.7 %collective-permute-start.11 = (f32[64,128]{1,0:T(8,128)S(1)}, f32[64,128]{1,0:T(8,128)S(1)}, u32[]{:S(2)}, u32[]{:S(2)}) collective-permute-start(f32[64,128]{1,0:T(8,128)S(1)} %select_add_fusion.5), channel_id=1, source_target_pairs={{0,8},{4,12},{8,16},{12,20},{16,24},{20,28},{24,0},{28,4},{32,40},... | collective-permute-start | bytes 98312 | tf_op jit(solution)/shard_map/ppermute | solution.py:171
  223.8 3.9 %collective-permute-start.9 = (f32[64,128]{1,0:T(8,128)S(1)}, f32[64,128]{1,0:T(8,128)S(1)}, u32[]{:S(2)}, u32[]{:S(2)}) collective-permute-start(f32[64,128]{1,0:T(8,128)S(1)} %select_add_fusion.5), channel_id=1, source_target_pairs={{0,24},{4,28},{8,0},{12,4},{16,8},{20,12},{24,16},{28,20},{32,56},... | collective-permute-start | bytes 98312 | tf_op jit(solution)/shard_map/ppermute | solution.py:171
  227.8 4.2 %collective-permute-start.12 = (f32[64,128]{1,0:T(8,128)S(1)}, f32[64,128]{1,0:T(8,128)S(1)}, u32[]{:S(2)}, u32[]{:S(2)}) collective-permute-start(f32[64,128]{1,0:T(8,128)S(1)} %select_add_fusion.4), channel_id=1, source_target_pairs={{0,96},{4,100},{8,104},{12,108},{16,112},{20,116},{24,120},{28,124... | collective-permute-start | bytes 98312 | tf_op jit(solution)/shard_map/ppermute | solution.py:171
  227.9 5.5 %collective-permute-start.13 = (f32[64,128]{1,0:T(8,128)S(1)}, f32[64,128]{1,0:T(8,128)S(1)}, u32[]{:S(2)}, u32[]{:S(2)}) collective-permute-start(f32[64,128]{1,0:T(8,128)S(1)} %select_add_fusion.4), channel_id=1, source_target_pairs={{0,64},{4,68},{8,72},{12,76},{16,80},{20,84},{24,88},{28,92},{32,9... | collective-permute-start | bytes 98312 | tf_op jit(solution)/shard_map/ppermute | solution.py:171
  231.4 5.1 %collective-permute-start.14 = (f32[64,128]{1,0:T(8,128)S(1)}, f32[64,128]{1,0:T(8,128)S(1)}, u32[]{:S(2)}, u32[]{:S(2)}) collective-permute-start(f32[64,128]{1,0:T(8,128)S(1)} %select_add_fusion.4), channel_id=1, source_target_pairs={{0,32},{4,36},{8,40},{12,44},{16,48},{20,52},{24,56},{28,60},{32,6... | collective-permute-start | bytes 98312 | tf_op jit(solution)/shard_map/ppermute | solution.py:171
  236.6 6.4 %collective-permute-start.15 = (f32[64,128]{1,0:T(8,128)S(1)}, f32[64,128]{1,0:T(8,128)S(1)}, u32[]{:S(2)}, u32[]{:S(2)}) collective-permute-start(f32[64,128]{1,0:T(8,128)S(1)} %select_add_fusion.3), channel_id=1, source_target_pairs={{0,3},{1,0},{2,1},{3,2},{4,7},{5,4},{6,5},{7,6},{8,11},{9,8},{10,9... | collective-permute-start | bytes 98312 | tf_op jit(solution)/shard_map/ppermute | solution.py:171
  237.8 5.4 %collective-permute-start.16 = (f32[64,128]{1,0:T(8,128)S(1)}, f32[64,128]{1,0:T(8,128)S(1)}, u32[]{:S(2)}, u32[]{:S(2)}) collective-permute-start(f32[64,128]{1,0:T(8,128)S(1)} %select_add_fusion.3), channel_id=1, source_target_pairs={{0,2},{1,3},{2,0},{3,1},{4,6},{5,7},{6,4},{7,5},{8,10},{9,11},{10,... | collective-permute-start | bytes 98312 | tf_op jit(solution)/shard_map/ppermute | solution.py:171
  239.3 5.1 %collective-permute-start.17 = (f32[64,128]{1,0:T(8,128)S(1)}, f32[64,128]{1,0:T(8,128)S(1)}, u32[]{:S(2)}, u32[]{:S(2)}) collective-permute-start(f32[64,128]{1,0:T(8,128)S(1)} %select_add_fusion.3), channel_id=1, source_target_pairs={{0,1},{1,2},{2,3},{3,0},{4,5},{5,6},{6,7},{7,4},{8,9},{9,10},{10,1... | collective-permute-start | bytes 98312 | tf_op jit(solution)/shard_map/ppermute | solution.py:171
  258.0 1.3 collective-permute-start.18
  259.3 4.0 %collective-permute-start.19 = (f32[64,64]{1,0:T(8,128)S(1)}, f32[64,64]{1,0:T(8,128)S(1)}, u32[]{:S(2)}, u32[]{:S(2)}) collective-permute-start(f32[64,64]{1,0:T(8,128)S(1)} %select_add_fusion.2), channel_id=1, source_target_pairs={{0,24},{4,28},{8,0},{12,4},{16,8},{20,12},{24,16},{28,20},{32,56},... | collective-permute-start | bytes 49160 | tf_op jit(solution)/shard_map/ppermute | solution.py:171
  260.5 5.8 %collective-permute-start.20 = (f32[64,64]{1,0:T(8,128)S(1)}, f32[64,64]{1,0:T(8,128)S(1)}, u32[]{:S(2)}, u32[]{:S(2)}) collective-permute-start(f32[64,64]{1,0:T(8,128)S(1)} %select_add_fusion.2), channel_id=1, source_target_pairs={{0,16},{4,20},{8,24},{12,28},{16,0},{20,4},{24,8},{28,12},{32,48},... | collective-permute-start | bytes 49160 | tf_op jit(solution)/shard_map/ppermute | solution.py:171
  261.4 5.2 %collective-permute-start.21 = (f32[64,64]{1,0:T(8,128)S(1)}, f32[64,64]{1,0:T(8,128)S(1)}, u32[]{:S(2)}, u32[]{:S(2)}) collective-permute-start(f32[64,64]{1,0:T(8,128)S(1)} %select_add_fusion.2), channel_id=1, source_target_pairs={{0,8},{4,12},{8,16},{12,20},{16,24},{20,28},{24,0},{28,4},{32,40},... | collective-permute-start | bytes 49160 | tf_op jit(solution)/shard_map/ppermute | solution.py:171
  266.6 4.0 %collective-permute-start.22 = (f32[64,64]{1,0:T(8,128)S(1)}, f32[64,64]{1,0:T(8,128)S(1)}, u32[]{:S(2)}, u32[]{:S(2)}) collective-permute-start(f32[64,64]{1,0:T(8,128)S(1)} %select_add_fusion.1), channel_id=1, source_target_pairs={{0,96},{4,100},{8,104},{12,108},{16,112},{20,116},{24,120},{28,124... | collective-permute-start | bytes 49160 | tf_op jit(solution)/shard_map/ppermute | solution.py:171
  266.7 5.5 %collective-permute-start.23 = (f32[64,64]{1,0:T(8,128)S(1)}, f32[64,64]{1,0:T(8,128)S(1)}, u32[]{:S(2)}, u32[]{:S(2)}) collective-permute-start(f32[64,64]{1,0:T(8,128)S(1)} %select_add_fusion.1), channel_id=1, source_target_pairs={{0,64},{4,68},{8,72},{12,76},{16,80},{20,84},{24,88},{28,92},{32,9... | collective-permute-start | bytes 49160 | tf_op jit(solution)/shard_map/ppermute | solution.py:171
  268.1 5.1 %collective-permute-start.24 = (f32[64,64]{1,0:T(8,128)S(1)}, f32[64,64]{1,0:T(8,128)S(1)}, u32[]{:S(2)}, u32[]{:S(2)}) collective-permute-start(f32[64,64]{1,0:T(8,128)S(1)} %select_add_fusion.1), channel_id=1, source_target_pairs={{0,32},{4,36},{8,40},{12,44},{16,48},{20,52},{24,56},{28,60},{32,6... | collective-permute-start | bytes 49160 | tf_op jit(solution)/shard_map/ppermute | solution.py:171
  273.3 4.0 %collective-permute-start.25 = (f32[64,64]{1,0:T(8,128)S(1)}, f32[64,64]{1,0:T(8,128)S(1)}, u32[]{:S(2)}, u32[]{:S(2)}) collective-permute-start(f32[64,64]{1,0:T(8,128)S(1)} %select_add_fusion), channel_id=1, source_target_pairs={{0,3},{1,0},{2,1},{3,2},{4,7},{5,4},{6,5},{7,6},{8,11},{9,8},{10,9... | collective-permute-start | bytes 49160 | tf_op jit(solution)/shard_map/ppermute | solution.py:171
  275.0 5.4 %collective-permute-start.26 = (f32[64,64]{1,0:T(8,128)S(1)}, f32[64,64]{1,0:T(8,128)S(1)}, u32[]{:S(2)}, u32[]{:S(2)}) collective-permute-start(f32[64,64]{1,0:T(8,128)S(1)} %select_add_fusion), channel_id=1, source_target_pairs={{0,2},{1,3},{2,0},{3,1},{4,6},{5,7},{6,4},{7,5},{8,10},{9,11},{10,... | collective-permute-start | bytes 49160 | tf_op jit(solution)/shard_map/ppermute | solution.py:171
  275.9 5.1 %collective-permute-start.27 = (f32[64,64]{1,0:T(8,128)S(1)}, f32[64,64]{1,0:T(8,128)S(1)}, u32[]{:S(2)}, u32[]{:S(2)}) collective-permute-start(f32[64,64]{1,0:T(8,128)S(1)} %select_add_fusion), channel_id=1, source_target_pairs={{0,1},{1,2},{2,3},{3,0},{4,5},{5,6},{6,7},{7,4},{8,9},{9,10},{10,1... | collective-permute-start | bytes 49160 | tf_op jit(solution)/shard_map/ppermute | solution.py:171
  297.4 55.4 %all-to-all-start.2 = ((f32[128,1,72,128]{3,2,1,0:T(8,128)}), f32[128,1,72,128]{3,2,1,0:T(8,128)}, u32[]{:S(2)}, u32[]{:S(2)}) async-start(f32[128,1,72,128]{3,2,1,0:T(8,128)} %copy.15), calls=%async_computation.2 | async-start | bytes 9437184 | tf_op jit(solution)/shard_map/all_to_all | solution.py:284
  (7 other events, 23.2 us)

commit v5 on v3

--- a/solution.py
+++ b/solution.py
@@ -142,37 +142,14 @@
     )
 
 
-def group_round(value, axis, stride, radix):
-    size = lax.axis_size(axis)
-    position = (lax.axis_index(axis) // stride) % radix
-    received = [value]
-    for shift in range(1, radix):
-        pairs = []
-        for i in range(size):
-            p = (i // stride) % radix
-            pairs.append((i, i + ((p + shift) % radix - p) * stride))
-        received.append(lax.ppermute(value, axis, pairs))
-    total = None
-    for q in range(radix):
-        choice = (position - q) % radix
-        term = received[0]
-        for shift in range(1, radix):
-            term = jnp.where(choice == shift, received[shift], term)
-        total = term if total is None else total + term
-    return total
-
-
 def exchange_sum(value, axis):
     size = lax.axis_size(axis)
     if size & (size - 1):
         return lax.psum(value, axis)
-    stride = 1
-    if size.bit_length() % 2 == 0:
-        value = group_round(value, axis, 1, 2)
-        stride = 2
-    while stride < size:
-        value = group_round(value, axis, stride, 4)
-        stride *= 4
+    step = 1
+    while step < size:
+        value = value + lax.ppermute(value, axis, [(i, i ^ step) for i in range(size)])
+        step *= 2
     return value
 
 

time: 332 us -> 337 us (1.015)
  waiting for transfers between devices: 88.1 us -> 99.2 us
    ppermute x20 -> x14, waiting for transfers between devices: 26 us -> 36.9 us  [exchange_sum(): lax.ppermute(value, axis, [(i, i ^ step) for i in range(size)])]
    ppermute x20 -> x14, starting transfers between devices: 21.2 us -> 21.2 us  [exchange_sum(): lax.ppermute(value, axis, [(i, i ^ step) for i in range(size)])]
  transfers between devices with their start and end apart: 30 -> 24, of which waited for: 19 -> 16; matrix products, arithmetic and copies ran while one was open for 20% -> 18% of each run, Pallas kernels for 7% -> 7%
where the time goes in v5:
time: 337 us; the launch traced here: 336 us
  waiting for transfers between devices  99.2 us (29%)
  starting transfers between devices  69.8 us (21%)
  other arithmetic  60.5 us (18%)
  Pallas kernels  40.3 us (12%)
  blocking collectives  32.2 us (10%)
  local copies, waits for them, and re-layouts  24 us (7%)
  matrix products  9.05 us (3%)
    add x3, other arithmetic, local_terms(): return -2.0 * total + potential[None] * orbital_field  53.9 us
    all_to_all x1, waiting for transfers between devices, local(): orbitals = lax.all_to_all(orbitals, 'orb', 0, 1, tiled=True)  48.3 us
    ppermute x14, waiting for transfers between devices, exchange_sum(): lax.ppermute(value, axis, [(i, i ^ step) for i in range(size)])  36.9 us
    ppermute x4, starting transfers between devices, halo_planes(): before = lax.ppermute(last, axis, up)  33 us
    all_to_all x1, blocking collectives, spread_cells(): lax.all_to_all(chunks, 'orb', 1, 0, tiled=True)  32.2 us
    pallas_call x4, Pallas kernels, filter_step(): pl.pallas_call(functools.partial(combine_kernel, scale, base is not None)...  23.9 us
    ppermute x14, starting transfers between devices, exchange_sum(): lax.ppermute(value, axis, [(i, i ^ step) for i in range(size)])  21.2 us
    pallas_call x2, Pallas kernels, eliminate(): pl.pallas_call(eliminate_kernel, out_shape=jax.ShapeDtypeStruct(source.sh...  16.4 us
  transfers between devices with their start and end apart: 24, of which 16 were waited for; matrix products, arithmetic and copies ran while one was open for 18% of the time, Pallas kernels for 7%

profile of v5, /device:TPU:0, one launch (start us, length us, event | category | flops | bytes accessed | tf_op | source)
XLA Modules:
  0.0 336.0 jit_solution(15672711265393780891)
XLA Ops:
  0.7 4.3 %fusion.113 = (f32[16,6,48,128]{3,2,1,0:T(8,128)S(1)}, f32[16,6,48,128]{3,2,1,0:T(8,128)}) fusion(f32[32,6,48,128]{3,2,1,0:T(8,128)} %refs_4_.3), kind=kLoop, calls=%fused_computation.207 | loop fusion | bytes 9437184 | tf_op jit(solution)/shard_map/slice | solution.py:218
  7.7 16.0 %multiply_add_fusion.refs_0_ = f32[32,6,48,128]{3,2,1,0:T(8,128)} fusion(f32[32,6,48,128]{3,2,1,0:T(8,128)S(1)} %copy-done, f32[6,48,128]{2,1,0:T(8,128)S(1)} %copy-done.6), kind=kLoop, calls=%fused_computation.114 | loop fusion | flops 47185920 | bytes 9584640 | tf_op jit(solution)/shard_map/add | solution.py:49
  25.1 17.4 %collective-permute-start.4 = (f32[16,6,48,128]{3,2,1,0:T(8,128)S(1)}, f32[16,6,48,128]{3,2,1,0:T(8,128)}, u32[]{:S(2)}, u32[]{:S(2)}) collective-permute-start(f32[16,6,48,128]{3,2,1,0:T(8,128)S(1)} %get-tuple-element.22), channel_id=1, source_target_pairs={{0,4},{4,8},{8,12},{12,16},{16,20},{20,24},{24,28},{28,32},{32,36}... | collective-permute-start | bytes 7077896 | tf_op jit(solution)/shard_map/ppermute | solution.py:30
  43.8 5.6 %shard_map.41.refs_1_ = f32[16,6,48,128]{3,2,1,0:T(8,128)} custom-call(f32[32,6,48,128]{3,2,1,0:T(8,128)} %multiply_add_fusion.refs_0_, f32[32,6,48,128]{3,2,1,0:T(8,128)} %refs_4_.3, f32[16,6,48,128]{3,2,1,0:T(8,128)} %copy-done.5, f32[16,6,48,128]{3,2,1,0:T(8,128)} %collective-permute-done.1.refs_3_), custom_call_target="tpu_custom_call" | custom-call | tf_op jit(solution)/shard_map/pallas_call | solution.py:97
  49.4 4.5 %collective-permute-start.2 = (f32[16,6,48,128]{3,2,1,0:T(8,128)}, f32[16,6,48,128]{3,2,1,0:T(8,128)}, u32[]{:S(2)}, u32[]{:S(2)}) collective-permute-start(f32[16,6,48,128]{3,2,1,0:T(8,128)} %shard_map.41.refs_1_), channel_id=1, source_target_pairs={{0,4},{4,8},{8,12},{12,16},{16,20},{20,24},{24,28},{28,32},{32,36}... | collective-permute-start | bytes 7077896 | tf_op jit(solution)/shard_map/ppermute | solution.py:30
  55.2 29.5 %multiply_add_fusion.2.refs_0_ = f32[16,6,48,128]{3,2,1,0:T(8,128)} fusion(f32[16,6,48,128]{3,2,1,0:T(8,128)} %shard_map.41.refs_1_, f32[6,48,128]{2,1,0:T(8,128)S(1)} %copy-done.6), kind=kLoop, calls=%fused_computation.191 | loop fusion | flops 23592960 | bytes 4866048 | tf_op jit(solution)/shard_map/add | solution.py:49
  84.7 5.6 %shard_map.42.refs_1_ = f32[16,6,48,128]{3,2,1,0:T(8,128)} custom-call(f32[32,6,48,128]{3,2,1,0:T(8,128)} %multiply_add_fusion.refs_0_, f32[32,6,48,128]{3,2,1,0:T(8,128)} %refs_4_.3, f32[16,6,48,128]{3,2,1,0:T(8,128)} %collective-permute-done.4.refs_2_, f32[16,6,48,128]{3,2,1,0:T(8,128)} %collective-permute-done.5.refs_3_), custom_call_target="tpu_custom_call" | custom-call | tf_op jit(solution)/shard_map/pallas_call | solution.py:97
  90.3 9.7 %collective-permute-start.6 = (f32[16,6,48,128]{3,2,1,0:T(8,128)}, f32[16,6,48,128]{3,2,1,0:T(8,128)}, u32[]{:S(2)}, u32[]{:S(2)}) collective-permute-start(f32[16,6,48,128]{3,2,1,0:T(8,128)} %shard_map.42.refs_1_), channel_id=1, source_target_pairs={{0,4},{4,8},{8,12},{12,16},{16,20},{20,24},{24,28},{28,32},{32,36}... | collective-permute-start | bytes 7077896 | tf_op jit(solution)/shard_map/ppermute | solution.py:30
  101.3 6.4 %shard_map.43 = f32[16,6,48,128]{3,2,1,0:T(8,128)} custom-call(f32[16,6,48,128]{3,2,1,0:T(8,128)} %multiply_add_fusion.2.refs_0_, f32[16,6,48,128]{3,2,1,0:T(8,128)} %shard_map.41.refs_1_, f32[16,6,48,128]{3,2,1,0:T(8,128)} %collective-permute-done.2.refs_2_, f32[16,6,48,128]{3,2,1,0:T(8,128)} %collective-permute-done.3.refs_3_, f32[32,6,48,128]{3,2,1,0:T(8,128)} %refs_4_.3), custom_call_target="tpu_custom_call" | custom-call | tf_op jit(solution)/shard_map/pallas_call | solution.py:97
  107.6 3.2 copy.9
  110.8 5.4 %all-to-all-start = ((f32[16,4,72,128]{3,2,0,1:T(8,128)}), f32[16,4,72,128]{3,2,0,1:T(8,128)}, u32[]{:S(2)}, u32[]{:S(2)}) async-start(f32[16,4,72,128]{3,2,0,1:T(8,128)} %copy.9), calls=%async_computation | async-start | bytes 4718592 | tf_op jit(solution)/shard_map/all_to_all | solution.py:112
  116.3 8.4 %multiply_add_fusion.1.refs_0_ = f32[16,6,48,128]{3,2,1,0:T(8,128)} fusion(f32[16,6,48,128]{3,2,1,0:T(8,128)S(1)} %copy-done.3, f32[6,48,128]{2,1,0:T(8,128)S(1)} %copy-done.6), kind=kLoop, calls=%fused_computation.190 | loop fusion | flops 23592960 | bytes 4866048 | tf_op jit(solution)/shard_map/add | solution.py:49
  124.7 6.4 %shard_map.44 = f32[16,6,48,128]{3,2,1,0:T(8,128)} custom-call(f32[16,6,48,128]{3,2,1,0:T(8,128)} %multiply_add_fusion.1.refs_0_, f32[16,6,48,128]{3,2,1,0:T(8,128)} %shard_map.42.refs_1_, f32[16,6,48,128]{3,2,1,0:T(8,128)} %collective-permute-done.6.refs_2_, f32[16,6,48,128]{3,2,1,0:T(8,128)} %collective-permute-done.7.refs_3_, f32[32,6,48,128]{3,2,1,0:T(8,128)} %refs_4_.3), custom_call_target="tpu_custom_call" | custom-call | tf_op jit(solution)/shard_map/pallas_call | solution.py:97
  132.9 13.9 %all-to-all-done = f32[16,4,72,128]{3,2,0,1:T(8,128)} async-done(((f32[16,4,72,128]{3,2,0,1:T(8,128)}), f32[16,4,72,128]{3,2,0,1:T(8,128)}, u32[]{:S(2)}, u32[]{:S(2)}) %all-to-all-start) | async-done | bytes 2359328 | tf_op jit(solution)/shard_map/all_to_all | solution.py:112
  146.8 32.2 %all_to_all.45 = f32[16,4,72,128]{3,2,0,1:T(8,128)S(1)} all-to-all(f32[16,4,72,128]{3,2,0,1:T(8,128)S(1)} %copy.10), channel_id=1, replica_groups=mesh['grid'=32,'orb'=4] {'orb'}, dimensions={1} | all-to-all | bytes 4718592 | tf_op jit(solution)/shard_map/all_to_all | solution.py:112
  184.3 2.6 convolution_bitcast_fusion.1
  188.2 3.9 %collective-permute-done.9 = f32[64,128]{1,0:T(8,128)S(1)} collective-permute-done((f32[64,128]{1,0:T(8,128)S(1)}, f32[64,128]{1,0:T(8,128)S(1)}, u32[]{:S(2)}, u32[]{:S(2)}) %collective-permute-start.9) | collective-permute-done | bytes 32800 | tf_op jit(solution)/shard_map/ppermute | solution.py:151
  192.1 4.6 %collective-permute-start.10 = (f32[64,128]{1,0:T(8,128)S(1)}, f32[64,128]{1,0:T(8,128)S(1)}, u32[]{:S(2)}, u32[]{:S(2)}) collective-permute-start(f32[64,128]{1,0:T(8,128)S(1)} %add.351), channel_id=1, source_target_pairs={{0,16},{4,20},{8,24},{12,28},{16,0},{20,4},{24,8},{28,12},{32,48},... | collective-permute-start | bytes 98312 | tf_op jit(solution)/shard_map/ppermute | solution.py:151
  202.5 2.7 collective-permute-start.12
  205.2 2.7 collective-permute-done.12
  208.5 3.3 collective-permute-done.13
  217.9 8.4 %shard_map.45 = f32[64,192]{1,0:T(8,128)} custom-call(f32[64,192]{1,0:T(8,128)} %pad_maximum_fusion.1.source_ref), custom_call_target="tpu_custom_call" | custom-call | tf_op jit(solution)/shard_map/pallas_call | solution.py:184
  236.0 3.8 %collective-permute-start.17 = (f32[64,64]{1,0:T(8,128)S(1)}, f32[64,64]{1,0:T(8,128)S(1)}, u32[]{:S(2)}, u32[]{:S(2)}) collective-permute-start(f32[64,64]{1,0:T(8,128)S(1)} %add.358), channel_id=1, source_target_pairs={{0,16},{4,20},{8,24},{12,28},{16,0},{20,4},{24,8},{28,12},{32,48},... | collective-permute-start | bytes 49160 | tf_op jit(solution)/shard_map/ppermute | solution.py:151
  242.9 2.8 collective-permute-done.18
  248.1 3.0 collective-permute-done.19
  251.7 3.3 collective-permute-done.20
  256.2 4.3 %collective-permute-done.21 = f32[64,64]{1,0:T(8,128)S(1)} collective-permute-done((f32[64,64]{1,0:T(8,128)S(1)}, f32[64,64]{1,0:T(8,128)S(1)}, u32[]{:S(2)}, u32[]{:S(2)}) %collective-permute-start.21) | collective-permute-done | bytes 16416 | tf_op jit(solution)/shard_map/ppermute | solution.py:151
  261.2 8.0 %shard_map.46 = f32[64,128]{1,0:T(8,128)} custom-call(f32[64,128]{1,0:T(8,128)} %pad_maximum_fusion.2.source_ref), custom_call_target="tpu_custom_call" | custom-call | tf_op jit(solution)/shard_map/pallas_call | solution.py:184
  271.9 4.9 %copy.15 = f32[128,1,72,128]{3,2,1,0:T(8,128)} copy(f32[128,1,72,128]{3,0,2,1:T(8,128)S(1)} %maximum_bitcast_fusion) | data formatting | bytes 9437184 | tf_op jit(solution)/shard_map/reshape | solution.py:243
  276.8 5.1 %all-to-all-start.2 = ((f32[128,1,72,128]{3,2,1,0:T(8,128)}), f32[128,1,72,128]{3,2,1,0:T(8,128)}, u32[]{:S(2)}, u32[]{:S(2)}) async-start(f32[128,1,72,128]{3,2,1,0:T(8,128)} %copy.15), calls=%async_computation.2 | async-start | bytes 9437184 | tf_op jit(solution)/shard_map/all_to_all | solution.py:244
  282.6 48.3 %all-to-all-done.2 = f32[128,1,72,128]{3,2,1,0:T(8,128)} async-done(((f32[128,1,72,128]{3,2,1,0:T(8,128)}), f32[128,1,72,128]{3,2,1,0:T(8,128)}, u32[]{:S(2)}, u32[]{:S(2)}) %all-to-all-start.2) | async-done | bytes 4718624 | tf_op jit(solution)/shard_map/all_to_all | solution.py:244
  330.9 5.1 %copy.16 = f32[32,4,1,72,128]{4,3,1,0,2:T(8,128)} copy(f32[32,4,1,72,128]{4,3,0,1,2:T(8,128)} %bitcast.18) | data formatting | bytes 9437184 | tf_op jit(solution)/shard_map/all_to_all | solution.py:244
  (80 shorter events, 49.8 us)
Async XLA Ops:
  0.6 7.1 %copy-start = (f32[32,6,48,128]{3,2,1,0:T(8,128)S(1)}, f32[32,6,48,128]{3,2,1,0:T(8,128)}, u32[]{:S(2)}) copy-start(f32[32,6,48,128]{3,2,1,0:T(8,128)} %refs_4_.3) | copy-start | bytes 14155780
  0.6 7.1 %copy-start.6 = (f32[6,48,128]{2,1,0:T(8,128)S(1)}, f32[6,48,128]{2,1,0:T(8,128)}, u32[]{:S(2)}) copy-start(f32[6,48,128]{2,1,0:T(8,128)} %param.3) | copy-start | bytes 442372
  5.0 18.7 %collective-permute-start = (f32[16,6,48,128]{3,2,1,0:T(8,128)}, f32[16,6,48,128]{3,2,1,0:T(8,128)S(1)}, u32[]{:S(2)}, u32[]{:S(2)}) collective-permute-start(f32[16,6,48,128]{3,2,1,0:T(8,128)} %get-tuple-element.35), channel_id=1, source_target_pairs={{0,4},{4,8},{8,12},{12,16},{16,20},{20,24},{24,28},{28,32},{32,36}... | collective-permute-start | bytes 7077896 | tf_op jit(solution)/shard_map/ppermute | solution.py:30
  6.4 17.3 %collective-permute-start.1 = (f32[16,6,48,128]{3,2,1,0:T(8,128)}, f32[16,6,48,128]{3,2,1,0:T(8,128)}, u32[]{:S(2)}, u32[]{:S(2)}) collective-permute-start(f32[16,6,48,128]{3,2,1,0:T(8,128)} %get-tuple-element.35), channel_id=1, source_target_pairs={{4,0},{8,4},{12,8},{16,12},{20,16},{24,20},{28,24},{32,28},{36,32}... | collective-permute-start | bytes 7077896 | tf_op jit(solution)/shard_map/ppermute | solution.py:31
  25.1 59.5 %collective-permute-start.4 = (f32[16,6,48,128]{3,2,1,0:T(8,128)S(1)}, f32[16,6,48,128]{3,2,1,0:T(8,128)}, u32[]{:S(2)}, u32[]{:S(2)}) collective-permute-start(f32[16,6,48,128]{3,2,1,0:T(8,128)S(1)} %get-tuple-element.22), channel_id=1, source_target_pairs={{0,4},{4,8},{8,12},{12,16},{16,20},{20,24},{24,28},{28,32},{32,36}... | collective-permute-start | bytes 7077896 | tf_op jit(solution)/shard_map/ppermute | solution.py:30
  42.5 42.1 %collective-permute-start.5 = (f32[16,6,48,128]{3,2,1,0:T(8,128)S(1)}, f32[16,6,48,128]{3,2,1,0:T(8,128)}, u32[]{:S(2)}, u32[]{:S(2)}) collective-permute-start(f32[16,6,48,128]{3,2,1,0:T(8,128)S(1)} %get-tuple-element.22), channel_id=1, source_target_pairs={{4,0},{8,4},{12,8},{16,12},{20,16},{24,20},{28,24},{32,28},{36,32}... | collective-permute-start | bytes 7077896 | tf_op jit(solution)/shard_map/ppermute | solution.py:31
  49.4 40.9 %collective-permute-start.2 = (f32[16,6,48,128]{3,2,1,0:T(8,128)}, f32[16,6,48,128]{3,2,1,0:T(8,128)}, u32[]{:S(2)}, u32[]{:S(2)}) collective-permute-start(f32[16,6,48,128]{3,2,1,0:T(8,128)} %shard_map.41.refs_1_), channel_id=1, source_target_pairs={{0,4},{4,8},{8,12},{12,16},{16,20},{20,24},{24,28},{28,32},{32,36}... | collective-permute-start | bytes 7077896 | tf_op jit(solution)/shard_map/ppermute | solution.py:30
  53.9 36.4 %collective-permute-start.3 = (f32[16,6,48,128]{3,2,1,0:T(8,128)}, f32[16,6,48,128]{3,2,1,0:T(8,128)}, u32[]{:S(2)}, u32[]{:S(2)}) collective-permute-start(f32[16,6,48,128]{3,2,1,0:T(8,128)} %shard_map.41.refs_1_), channel_id=1, source_target_pairs={{4,0},{8,4},{12,8},{16,12},{20,16},{24,20},{28,24},{32,28},{36,32}... | collective-permute-start | bytes 7077896 | tf_op jit(solution)/shard_map/ppermute | solution.py:31
  90.3 34.4 %collective-permute-start.6 = (f32[16,6,48,128]{3,2,1,0:T(8,128)}, f32[16,6,48,128]{3,2,1,0:T(8,128)}, u32[]{:S(2)}, u32[]{:S(2)}) collective-permute-start(f32[16,6,48,128]{3,2,1,0:T(8,128)} %shard_map.42.refs_1_), channel_id=1, source_target_pairs={{0,4},{4,8},{8,12},{12,16},{16,20},{20,24},{24,28},{28,32},{32,36}... | collective-permute-start | bytes 7077896 | tf_op jit(solution)/shard_map/ppermute | solution.py:30
  100.0 24.7 %collective-permute-start.7 = (f32[16,6,48,128]{3,2,1,0:T(8,128)}, f32[16,6,48,128]{3,2,1,0:T(8,128)}, u32[]{:S(2)}, u32[]{:S(2)}) collective-permute-start(f32[16,6,48,128]{3,2,1,0:T(8,128)} %shard_map.42.refs_1_), channel_id=1, source_target_pairs={{4,0},{8,4},{12,8},{16,12},{20,16},{24,20},{28,24},{32,28},{36,32}... | collective-permute-start | bytes 7077896 | tf_op jit(solution)/shard_map/ppermute | solution.py:31
  110.8 5.4 %copy-start.3 = (f32[16,6,48,128]{3,2,1,0:T(8,128)S(1)}, f32[16,6,48,128]{3,2,1,0:T(8,128)}, u32[]{:S(2)}) copy-start(f32[16,6,48,128]{3,2,1,0:T(8,128)} %shard_map.42.refs_1_) | copy-start | bytes 7077892
  110.8 36.0 %all-to-all-start = ((f32[16,4,72,128]{3,2,0,1:T(8,128)}), f32[16,4,72,128]{3,2,0,1:T(8,128)}, u32[]{:S(2)}, u32[]{:S(2)}) async-start(f32[16,4,72,128]{3,2,0,1:T(8,128)} %copy.9), calls=%async_computation | async-start | bytes 4718592 | tf_op jit(solution)/shard_map/all_to_all | solution.py:112
  186.9 1.3 collective-permute-start.8
  188.2 3.9 %collective-permute-start.9 = (f32[64,128]{1,0:T(8,128)S(1)}, f32[64,128]{1,0:T(8,128)S(1)}, u32[]{:S(2)}, u32[]{:S(2)}) collective-permute-start(f32[64,128]{1,0:T(8,128)S(1)} %add.350), channel_id=1, source_target_pairs={{0,8},{4,12},{8,0},{12,4},{16,24},{20,28},{24,16},{28,20},{32,40},... | collective-permute-start | bytes 98312 | tf_op jit(solution)/shard_map/ppermute | solution.py:151
  192.1 6.5 %collective-permute-start.10 = (f32[64,128]{1,0:T(8,128)S(1)}, f32[64,128]{1,0:T(8,128)S(1)}, u32[]{:S(2)}, u32[]{:S(2)}) collective-permute-start(f32[64,128]{1,0:T(8,128)S(1)} %add.351), channel_id=1, source_target_pairs={{0,16},{4,20},{8,24},{12,28},{16,0},{20,4},{24,8},{28,12},{32,48},... | collective-permute-start | bytes 98312 | tf_op jit(solution)/shard_map/ppermute | solution.py:151
  198.6 3.9 %collective-permute-start.11 = (f32[64,128]{1,0:T(8,128)S(1)}, f32[64,128]{1,0:T(8,128)S(1)}, u32[]{:S(2)}, u32[]{:S(2)}) collective-permute-start(f32[64,128]{1,0:T(8,128)S(1)} %add.352), channel_id=1, source_target_pairs={{0,32},{4,36},{8,40},{12,44},{16,48},{20,52},{24,56},{28,60},{32,0... | collective-permute-start | bytes 98312 | tf_op jit(solution)/shard_map/ppermute | solution.py:151
  202.5 5.4 %collective-permute-start.12 = (f32[64,128]{1,0:T(8,128)S(1)}, f32[64,128]{1,0:T(8,128)S(1)}, u32[]{:S(2)}, u32[]{:S(2)}) collective-permute-start(f32[64,128]{1,0:T(8,128)S(1)} %add.353), channel_id=1, source_target_pairs={{0,64},{4,68},{8,72},{12,76},{16,80},{20,84},{24,88},{28,92},{32,9... | collective-permute-start | bytes 98312 | tf_op jit(solution)/shard_map/ppermute | solution.py:151
  207.9 3.9 %collective-permute-start.13 = (f32[64,128]{1,0:T(8,128)S(1)}, f32[64,128]{1,0:T(8,128)S(1)}, u32[]{:S(2)}, u32[]{:S(2)}) collective-permute-start(f32[64,128]{1,0:T(8,128)S(1)} %add.354), channel_id=1, source_target_pairs={{0,1},{1,0},{2,3},{3,2},{4,5},{5,4},{6,7},{7,6},{8,9},{9,8},{10,11... | collective-permute-start | bytes 98312 | tf_op jit(solution)/shard_map/ppermute | solution.py:151
  211.9 5.4 %collective-permute-start.14 = (f32[64,128]{1,0:T(8,128)S(1)}, f32[64,128]{1,0:T(8,128)S(1)}, u32[]{:S(2)}, u32[]{:S(2)}) collective-permute-start(f32[64,128]{1,0:T(8,128)S(1)} %add.355), channel_id=1, source_target_pairs={{0,2},{1,3},{2,0},{3,1},{4,6},{5,7},{6,4},{7,5},{8,10},{9,11},{10,... | collective-permute-start | bytes 98312 | tf_op jit(solution)/shard_map/ppermute | solution.py:151
  226.3 2.0 copy-start.4
  226.3 2.0 copy-start.7
  230.8 1.3 collective-permute-start.15
  232.1 3.9 %collective-permute-start.16 = (f32[64,64]{1,0:T(8,128)S(1)}, f32[64,64]{1,0:T(8,128)S(1)}, u32[]{:S(2)}, u32[]{:S(2)}) collective-permute-start(f32[64,64]{1,0:T(8,128)S(1)} %add.357), channel_id=1, source_target_pairs={{0,8},{4,12},{8,0},{12,4},{16,24},{20,28},{24,16},{28,20},{32,40},... | collective-permute-start | bytes 49160 | tf_op jit(solution)/shard_map/ppermute | solution.py:151
  236.0 5.7 %collective-permute-start.17 = (f32[64,64]{1,0:T(8,128)S(1)}, f32[64,64]{1,0:T(8,128)S(1)}, u32[]{:S(2)}, u32[]{:S(2)}) collective-permute-start(f32[64,64]{1,0:T(8,128)S(1)} %add.358), channel_id=1, source_target_pairs={{0,16},{4,20},{8,24},{12,28},{16,0},{20,4},{24,8},{28,12},{32,48},... | collective-permute-start | bytes 49160 | tf_op jit(solution)/shard_map/ppermute | solution.py:151
  241.8 4.0 %collective-permute-start.18 = (f32[64,64]{1,0:T(8,128)S(1)}, f32[64,64]{1,0:T(8,128)S(1)}, u32[]{:S(2)}, u32[]{:S(2)}) collective-permute-start(f32[64,64]{1,0:T(8,128)S(1)} %add.359), channel_id=1, source_target_pairs={{0,32},{4,36},{8,40},{12,44},{16,48},{20,52},{24,56},{28,60},{32,0... | collective-permute-start | bytes 49160 | tf_op jit(solution)/shard_map/ppermute | solution.py:151
  245.7 5.4 %collective-permute-start.19 = (f32[64,64]{1,0:T(8,128)S(1)}, f32[64,64]{1,0:T(8,128)S(1)}, u32[]{:S(2)}, u32[]{:S(2)}) collective-permute-start(f32[64,64]{1,0:T(8,128)S(1)} %add.360), channel_id=1, source_target_pairs={{0,64},{4,68},{8,72},{12,76},{16,80},{20,84},{24,88},{28,92},{32,9... | collective-permute-start | bytes 49160 | tf_op jit(solution)/shard_map/ppermute | solution.py:151
  251.1 3.9 %collective-permute-start.20 = (f32[64,64]{1,0:T(8,128)S(1)}, f32[64,64]{1,0:T(8,128)S(1)}, u32[]{:S(2)}, u32[]{:S(2)}) collective-permute-start(f32[64,64]{1,0:T(8,128)S(1)} %add.361), channel_id=1, source_target_pairs={{0,1},{1,0},{2,3},{3,2},{4,5},{5,4},{6,7},{7,6},{8,9},{9,8},{10,11... | collective-permute-start | bytes 49160 | tf_op jit(solution)/shard_map/ppermute | solution.py:151
  255.1 5.4 %collective-permute-start.21 = (f32[64,64]{1,0:T(8,128)S(1)}, f32[64,64]{1,0:T(8,128)S(1)}, u32[]{:S(2)}, u32[]{:S(2)}) collective-permute-start(f32[64,64]{1,0:T(8,128)S(1)} %add.362), channel_id=1, source_target_pairs={{0,2},{1,3},{2,0},{3,1},{4,6},{5,7},{6,4},{7,5},{8,10},{9,11},{10,... | collective-permute-start | bytes 49160 | tf_op jit(solution)/shard_map/ppermute | solution.py:151
  269.2 2.1 copy-start.2
  276.8 5.1 %slice-start = ((f32[64,192]{1,0:T(8,128)}), f32[64,128]{1,0:T(8,128)S(1)}, s32[]{:S(2)}) async-start(f32[64,192]{1,0:T(8,128)} %shard_map.45), calls=%async_computation.3 | async-start | bytes 65536 | tf_op jit(solution)/shard_map/concatenate | solution.py:204
  276.8 5.1 %copy-start.8 = (f32[64,128]{1,0:T(8,128)S(1)}, f32[64,128]{1,0:T(8,128)}, u32[]{:S(2)}) copy-start(f32[64,128]{1,0:T(8,128)} %shard_map.46) | copy-start | bytes 98308
  276.8 54.1 %all-to-all-start.2 = ((f32[128,1,72,128]{3,2,1,0:T(8,128)}), f32[128,1,72,128]{3,2,1,0:T(8,128)}, u32[]{:S(2)}, u32[]{:S(2)}) async-start(f32[128,1,72,128]{3,2,1,0:T(8,128)} %copy.15), calls=%async_computation.2 | async-start | bytes 9437184 | tf_op jit(solution)/shard_map/all_to_all | solution.py:244
  (2 other events, 2.8 us)

commit v6 on v3

--- a/solution.py
+++ b/solution.py
@@ -80,8 +80,8 @@
 ):
     count = orbital_field.shape[0] if count is None else count
     halo_start = start if halo_start is None else halo_start
-    aligned = all(value % 8 == 0 for value in (count, start, base_start, halo_start))
-    block_rows = 8 if aligned else 1
+    aligned = all(value % 4 == 0 for value in (count, start, base_start, halo_start))
+    block_rows = 4 if aligned else 1
     offset = start // block_rows
     halo_offset = halo_start // block_rows
     base_offset = base_start // block_rows

time: 332 us -> 332 us (level)
  transfers between devices with their start and end apart: 30 -> 30, of which waited for: 19 -> 19; matrix products, arithmetic and copies ran while one was open for 20% -> 20% of each run, Pallas kernels for 7% -> 8%
where the time goes in v6:
time: 332 us; the launch traced here: 331 us
  waiting for transfers between devices  87.7 us (26%)
  starting transfers between devices  68.4 us (21%)
  other arithmetic  62.3 us (19%)
  Pallas kernels  42.3 us (13%)
  blocking collectives  33.3 us (10%)
  local copies, waits for them, and re-layouts  27.2 us (8%)
  matrix products  9.05 us (3%)
    add x3, other arithmetic, local_terms(): return -2.0 * total + potential[None] * orbital_field  54.2 us
    all_to_all x1, waiting for transfers between devices, local(): orbitals = lax.all_to_all(orbitals, 'orb', 0, 1, tiled=True)  49.6 us
    all_to_all x1, blocking collectives, spread_cells(): lax.all_to_all(chunks, 'orb', 1, 0, tiled=True)  33.3 us
    ppermute x4, starting transfers between devices, halo_planes(): before = lax.ppermute(last, axis, up)  31.5 us
    ppermute x20, waiting for transfers between devices, group_round(): received.append(lax.ppermute(value, axis, pairs))  26 us
    pallas_call x4, Pallas kernels, filter_step(): pl.pallas_call(functools.partial(combine_kernel, scale, base is not None)...  25.9 us
    ppermute x20, starting transfers between devices, group_round(): received.append(lax.ppermute(value, axis, pairs))  21.2 us
    pallas_call x2, Pallas kernels, eliminate(): pl.pallas_call(eliminate_kernel, out_shape=jax.ShapeDtypeStruct(source.sh...  16.4 us
  transfers between devices with their start and end apart: 30, of which 19 were waited for; matrix products, arithmetic and copies ran while one was open for 20% of the time, Pallas kernels for 8%

profile of v6, /device:TPU:0, one launch (start us, length us, event | category | flops | bytes accessed | tf_op | source)
XLA Modules:
  0.0 331.4 jit_solution(14949696164901226147)
XLA Ops:
  0.7 4.3 %fusion.113 = (f32[16,6,48,128]{3,2,1,0:T(8,128)S(1)}, f32[16,6,48,128]{3,2,1,0:T(8,128)}) fusion(f32[32,6,48,128]{3,2,1,0:T(8,128)} %refs_4_.3), kind=kLoop, calls=%fused_computation.213 | loop fusion | bytes 9437184 | tf_op jit(solution)/shard_map/slice | solution.py:241
  7.7 16.0 %multiply_add_fusion.refs_0_ = f32[32,6,48,128]{3,2,1,0:T(8,128)} fusion(f32[32,6,48,128]{3,2,1,0:T(8,128)S(1)} %copy-done, f32[6,48,128]{2,1,0:T(8,128)S(1)} %copy-done.6), kind=kLoop, calls=%fused_computation.114 | loop fusion | flops 47185920 | bytes 9584640 | tf_op jit(solution)/shard_map/add | solution.py:49
  25.1 17.4 %collective-permute-start.4 = (f32[16,6,48,128]{3,2,1,0:T(8,128)S(1)}, f32[16,6,48,128]{3,2,1,0:T(8,128)}, u32[]{:S(2)}, u32[]{:S(2)}) collective-permute-start(f32[16,6,48,128]{3,2,1,0:T(8,128)S(1)} %get-tuple-element.22), channel_id=1, source_target_pairs={{0,4},{4,8},{8,12},{12,16},{16,20},{20,24},{24,28},{28,32},{32,36}... | collective-permute-start | bytes 7077896 | tf_op jit(solution)/shard_map/ppermute | solution.py:30
  43.8 6.2 %shard_map.41.refs_1_ = f32[16,6,48,128]{3,2,1,0:T(8,128)} custom-call(f32[32,6,48,128]{3,2,1,0:T(8,128)} %multiply_add_fusion.refs_0_, f32[32,6,48,128]{3,2,1,0:T(8,128)} %refs_4_.3, f32[16,6,48,128]{3,2,1,0:T(8,128)} %copy-done.5, f32[16,6,48,128]{3,2,1,0:T(8,128)} %collective-permute-done.1.refs_3_), custom_call_target="tpu_custom_call" | custom-call | tf_op jit(solution)/shard_map/pallas_call | solution.py:97
  50.0 4.4 %collective-permute-start.2 = (f32[16,6,48,128]{3,2,1,0:T(8,128)}, f32[16,6,48,128]{3,2,1,0:T(8,128)}, u32[]{:S(2)}, u32[]{:S(2)}) collective-permute-start(f32[16,6,48,128]{3,2,1,0:T(8,128)} %shard_map.41.refs_1_), channel_id=1, source_target_pairs={{0,4},{4,8},{8,12},{12,16},{16,20},{20,24},{24,28},{28,32},{32,36}... | collective-permute-start | bytes 7077896 | tf_op jit(solution)/shard_map/ppermute | solution.py:30
  55.7 29.8 %multiply_add_fusion.2.refs_0_ = f32[16,6,48,128]{3,2,1,0:T(8,128)} fusion(f32[16,6,48,128]{3,2,1,0:T(8,128)} %shard_map.41.refs_1_, f32[6,48,128]{2,1,0:T(8,128)S(1)} %copy-done.6), kind=kLoop, calls=%fused_computation.191 | loop fusion | flops 23592960 | bytes 4866048 | tf_op jit(solution)/shard_map/add | solution.py:49
  85.5 6.2 %shard_map.42.refs_1_ = f32[16,6,48,128]{3,2,1,0:T(8,128)} custom-call(f32[32,6,48,128]{3,2,1,0:T(8,128)} %multiply_add_fusion.refs_0_, f32[32,6,48,128]{3,2,1,0:T(8,128)} %refs_4_.3, f32[16,6,48,128]{3,2,1,0:T(8,128)} %collective-permute-done.4.refs_2_, f32[16,6,48,128]{3,2,1,0:T(8,128)} %collective-permute-done.5.refs_3_), custom_call_target="tpu_custom_call" | custom-call | tf_op jit(solution)/shard_map/pallas_call | solution.py:97
  91.7 8.3 %collective-permute-start.6 = (f32[16,6,48,128]{3,2,1,0:T(8,128)}, f32[16,6,48,128]{3,2,1,0:T(8,128)}, u32[]{:S(2)}, u32[]{:S(2)}) collective-permute-start(f32[16,6,48,128]{3,2,1,0:T(8,128)} %shard_map.42.refs_1_), channel_id=1, source_target_pairs={{0,4},{4,8},{8,12},{12,16},{16,20},{20,24},{24,28},{28,32},{32,36}... | collective-permute-start | bytes 7077896 | tf_op jit(solution)/shard_map/ppermute | solution.py:30
  101.2 6.8 %shard_map.43 = f32[16,6,48,128]{3,2,1,0:T(8,128)} custom-call(f32[16,6,48,128]{3,2,1,0:T(8,128)} %multiply_add_fusion.2.refs_0_, f32[16,6,48,128]{3,2,1,0:T(8,128)} %shard_map.41.refs_1_, f32[16,6,48,128]{3,2,1,0:T(8,128)} %collective-permute-done.2.refs_2_, f32[16,6,48,128]{3,2,1,0:T(8,128)} %collective-permute-done.3.refs_3_, f32[32,6,48,128]{3,2,1,0:T(8,128)} %refs_4_.3), custom_call_target="tpu_custom_call" | custom-call | tf_op jit(solution)/shard_map/pallas_call | solution.py:97
  108.0 3.2 copy.9
  111.2 5.4 %all-to-all-start = ((f32[16,4,72,128]{3,2,0,1:T(8,128)}), f32[16,4,72,128]{3,2,0,1:T(8,128)}, u32[]{:S(2)}, u32[]{:S(2)}) async-start(f32[16,4,72,128]{3,2,0,1:T(8,128)} %copy.9), calls=%async_computation | async-start | bytes 4718592 | tf_op jit(solution)/shard_map/all_to_all | solution.py:112
  116.7 8.4 %multiply_add_fusion.1.refs_0_ = f32[16,6,48,128]{3,2,1,0:T(8,128)} fusion(f32[16,6,48,128]{3,2,1,0:T(8,128)S(1)} %copy-done.3, f32[6,48,128]{2,1,0:T(8,128)S(1)} %copy-done.6), kind=kLoop, calls=%fused_computation.190 | loop fusion | flops 23592960 | bytes 4866048 | tf_op jit(solution)/shard_map/add | solution.py:49
  125.1 6.8 %shard_map.44 = f32[16,6,48,128]{3,2,1,0:T(8,128)} custom-call(f32[16,6,48,128]{3,2,1,0:T(8,128)} %multiply_add_fusion.1.refs_0_, f32[16,6,48,128]{3,2,1,0:T(8,128)} %shard_map.42.refs_1_, f32[16,6,48,128]{3,2,1,0:T(8,128)} %collective-permute-done.6.refs_2_, f32[16,6,48,128]{3,2,1,0:T(8,128)} %collective-permute-done.7.refs_3_, f32[32,6,48,128]{3,2,1,0:T(8,128)} %refs_4_.3), custom_call_target="tpu_custom_call" | custom-call | tf_op jit(solution)/shard_map/pallas_call | solution.py:97
  131.9 3.2 copy.10
  135.1 12.1 %all-to-all-done = f32[16,4,72,128]{3,2,0,1:T(8,128)} async-done(((f32[16,4,72,128]{3,2,0,1:T(8,128)}), f32[16,4,72,128]{3,2,0,1:T(8,128)}, u32[]{:S(2)}, u32[]{:S(2)}) %all-to-all-start) | async-done | bytes 2359328 | tf_op jit(solution)/shard_map/all_to_all | solution.py:112
  147.2 33.3 %all_to_all.45 = f32[16,4,72,128]{3,2,0,1:T(8,128)S(1)} all-to-all(f32[16,4,72,128]{3,2,0,1:T(8,128)} %copy.10), channel_id=1, replica_groups=mesh['grid'=32,'orb'=4] {'orb'}, dimensions={1} | all-to-all | bytes 4718592 | tf_op jit(solution)/shard_map/all_to_all | solution.py:112
  182.5 3.4 %fusion.36 = (f32[2,2,16,72,128]{4,3,2,0,1:T(8,128)S(1)}, f32[2,2,16,72,128]{4,3,2,0,1:T(8,128)}) fusion(f32[4,1,16,72,128]{4,3,2,0,1:T(8,128)} %bitcast.3, f32[4,1,16,72,128]{4,3,2,0,1:T(8,128)S(1)} %bitcast.46), kind=kLoop, calls=%fused_computation.115 | loop fusion | flops 1179648 | bytes 9437184 | tf_op jit(solution)/shard_map/stack | solution.py:261
  187.2 2.6 convolution_bitcast_fusion.1
  191.1 3.0 collective-permute-start.10
  194.1 3.1 collective-permute-start.11
  201.3 3.5 %collective-permute-start.13 = (f32[64,128]{1,0:T(8,128)S(1)}, f32[64,128]{1,0:T(8,128)S(1)}, u32[]{:S(2)}, u32[]{:S(2)}) collective-permute-start(f32[64,128]{1,0:T(8,128)S(1)} %select_add_fusion.4), channel_id=1, source_target_pairs={{0,64},{4,68},{8,72},{12,76},{16,80},{20,84},{24,88},{28,92},{32,9... | collective-permute-start | bytes 98312 | tf_op jit(solution)/shard_map/ppermute | solution.py:154
  206.8 3.1 collective-permute-done.14
  212.8 3.6 %copy.13 = f32[2,2,16,72,128]{4,2,1,0,3:T(8,128)} copy(f32[2,2,16,72,128]{4,3,2,0,1:T(8,128)} %get-tuple-element.33) | data formatting | bytes 4718592 | tf_op jit(solution)/shard_map/slice | solution.py:222
  218.5 8.4 %shard_map.45 = f32[64,192]{1,0:T(8,128)} custom-call(f32[64,192]{1,0:T(8,128)} %pad_maximum_fusion.1.source_ref), custom_call_target="tpu_custom_call" | custom-call | tf_op jit(solution)/shard_map/pallas_call | solution.py:207
  236.7 3.1 collective-permute-done.20
  250.8 3.2 collective-permute-done.26
  255.2 8.0 %shard_map.46 = f32[64,128]{1,0:T(8,128)} custom-call(f32[64,128]{1,0:T(8,128)} %pad_maximum_fusion.2.source_ref), custom_call_target="tpu_custom_call" | custom-call | tf_op jit(solution)/shard_map/pallas_call | solution.py:207
  263.3 2.1 fusion.110
  265.9 4.9 %copy.15 = f32[128,1,72,128]{3,2,1,0:T(8,128)} copy(f32[128,1,72,128]{3,0,2,1:T(8,128)S(1)} %maximum_bitcast_fusion) | data formatting | bytes 9437184 | tf_op jit(solution)/shard_map/reshape | solution.py:266
  270.8 5.1 %all-to-all-start.2 = ((f32[128,1,72,128]{3,2,1,0:T(8,128)}), f32[128,1,72,128]{3,2,1,0:T(8,128)}, u32[]{:S(2)}, u32[]{:S(2)}) async-start(f32[128,1,72,128]{3,2,1,0:T(8,128)} %copy.15), calls=%async_computation.2 | async-start | bytes 9437184 | tf_op jit(solution)/shard_map/all_to_all | solution.py:267
  276.7 49.6 %all-to-all-done.2 = f32[128,1,72,128]{3,2,1,0:T(8,128)} async-done(((f32[128,1,72,128]{3,2,1,0:T(8,128)}), f32[128,1,72,128]{3,2,1,0:T(8,128)}, u32[]{:S(2)}, u32[]{:S(2)}) %all-to-all-start.2) | async-done | bytes 4718624 | tf_op jit(solution)/shard_map/all_to_all | solution.py:267
  326.3 5.1 %copy.16 = f32[32,4,1,72,128]{4,3,1,0,2:T(8,128)} copy(f32[32,4,1,72,128]{4,3,0,1,2:T(8,128)} %bitcast.18) | data formatting | bytes 9437184 | tf_op jit(solution)/shard_map/all_to_all | solution.py:267
  (86 shorter events, 46.8 us)
Async XLA Ops:
  0.6 7.1 %copy-start = (f32[32,6,48,128]{3,2,1,0:T(8,128)S(1)}, f32[32,6,48,128]{3,2,1,0:T(8,128)}, u32[]{:S(2)}) copy-start(f32[32,6,48,128]{3,2,1,0:T(8,128)} %refs_4_.3) | copy-start | bytes 14155780
  0.6 7.1 %copy-start.6 = (f32[6,48,128]{2,1,0:T(8,128)S(1)}, f32[6,48,128]{2,1,0:T(8,128)}, u32[]{:S(2)}) copy-start(f32[6,48,128]{2,1,0:T(8,128)} %param.3) | copy-start | bytes 442372
  5.0 18.7 %collective-permute-start = (f32[16,6,48,128]{3,2,1,0:T(8,128)}, f32[16,6,48,128]{3,2,1,0:T(8,128)S(1)}, u32[]{:S(2)}, u32[]{:S(2)}) collective-permute-start(f32[16,6,48,128]{3,2,1,0:T(8,128)} %get-tuple-element.35), channel_id=1, source_target_pairs={{0,4},{4,8},{8,12},{12,16},{16,20},{20,24},{24,28},{28,32},{32,36}... | collective-permute-start | bytes 7077896 | tf_op jit(solution)/shard_map/ppermute | solution.py:30
  6.4 17.3 %collective-permute-start.1 = (f32[16,6,48,128]{3,2,1,0:T(8,128)}, f32[16,6,48,128]{3,2,1,0:T(8,128)}, u32[]{:S(2)}, u32[]{:S(2)}) collective-permute-start(f32[16,6,48,128]{3,2,1,0:T(8,128)} %get-tuple-element.35), channel_id=1, source_target_pairs={{4,0},{8,4},{12,8},{16,12},{20,16},{24,20},{28,24},{32,28},{36,32}... | collective-permute-start | bytes 7077896 | tf_op jit(solution)/shard_map/ppermute | solution.py:31
  25.1 60.3 %collective-permute-start.4 = (f32[16,6,48,128]{3,2,1,0:T(8,128)S(1)}, f32[16,6,48,128]{3,2,1,0:T(8,128)}, u32[]{:S(2)}, u32[]{:S(2)}) collective-permute-start(f32[16,6,48,128]{3,2,1,0:T(8,128)S(1)} %get-tuple-element.22), channel_id=1, source_target_pairs={{0,4},{4,8},{8,12},{12,16},{16,20},{20,24},{24,28},{28,32},{32,36}... | collective-permute-start | bytes 7077896 | tf_op jit(solution)/shard_map/ppermute | solution.py:30
  42.5 43.0 %collective-permute-start.5 = (f32[16,6,48,128]{3,2,1,0:T(8,128)S(1)}, f32[16,6,48,128]{3,2,1,0:T(8,128)}, u32[]{:S(2)}, u32[]{:S(2)}) collective-permute-start(f32[16,6,48,128]{3,2,1,0:T(8,128)S(1)} %get-tuple-element.22), channel_id=1, source_target_pairs={{4,0},{8,4},{12,8},{16,12},{20,16},{24,20},{28,24},{32,28},{36,32}... | collective-permute-start | bytes 7077896 | tf_op jit(solution)/shard_map/ppermute | solution.py:31
  50.0 41.7 %collective-permute-start.2 = (f32[16,6,48,128]{3,2,1,0:T(8,128)}, f32[16,6,48,128]{3,2,1,0:T(8,128)}, u32[]{:S(2)}, u32[]{:S(2)}) collective-permute-start(f32[16,6,48,128]{3,2,1,0:T(8,128)} %shard_map.41.refs_1_), channel_id=1, source_target_pairs={{0,4},{4,8},{8,12},{12,16},{16,20},{20,24},{24,28},{28,32},{32,36}... | collective-permute-start | bytes 7077896 | tf_op jit(solution)/shard_map/ppermute | solution.py:30
  54.4 37.3 %collective-permute-start.3 = (f32[16,6,48,128]{3,2,1,0:T(8,128)}, f32[16,6,48,128]{3,2,1,0:T(8,128)}, u32[]{:S(2)}, u32[]{:S(2)}) collective-permute-start(f32[16,6,48,128]{3,2,1,0:T(8,128)} %shard_map.41.refs_1_), channel_id=1, source_target_pairs={{4,0},{8,4},{12,8},{16,12},{20,16},{24,20},{28,24},{32,28},{36,32}... | collective-permute-start | bytes 7077896 | tf_op jit(solution)/shard_map/ppermute | solution.py:31
  91.7 33.4 %collective-permute-start.6 = (f32[16,6,48,128]{3,2,1,0:T(8,128)}, f32[16,6,48,128]{3,2,1,0:T(8,128)}, u32[]{:S(2)}, u32[]{:S(2)}) collective-permute-start(f32[16,6,48,128]{3,2,1,0:T(8,128)} %shard_map.42.refs_1_), channel_id=1, source_target_pairs={{0,4},{4,8},{8,12},{12,16},{16,20},{20,24},{24,28},{28,32},{32,36}... | collective-permute-start | bytes 7077896 | tf_op jit(solution)/shard_map/ppermute | solution.py:30
  100.0 25.1 %collective-permute-start.7 = (f32[16,6,48,128]{3,2,1,0:T(8,128)}, f32[16,6,48,128]{3,2,1,0:T(8,128)}, u32[]{:S(2)}, u32[]{:S(2)}) collective-permute-start(f32[16,6,48,128]{3,2,1,0:T(8,128)} %shard_map.42.refs_1_), channel_id=1, source_target_pairs={{4,0},{8,4},{12,8},{16,12},{20,16},{24,20},{28,24},{32,28},{36,32}... | collective-permute-start | bytes 7077896 | tf_op jit(solution)/shard_map/ppermute | solution.py:31
  111.2 36.0 %all-to-all-start = ((f32[16,4,72,128]{3,2,0,1:T(8,128)}), f32[16,4,72,128]{3,2,0,1:T(8,128)}, u32[]{:S(2)}, u32[]{:S(2)}) async-start(f32[16,4,72,128]{3,2,0,1:T(8,128)} %copy.9), calls=%async_computation | async-start | bytes 4718592 | tf_op jit(solution)/shard_map/all_to_all | solution.py:112
  189.8 1.3 collective-permute-start.8
  191.1 6.3 %collective-permute-start.10 = (f32[64,128]{1,0:T(8,128)S(1)}, f32[64,128]{1,0:T(8,128)S(1)}, u32[]{:S(2)}, u32[]{:S(2)}) collective-permute-start(f32[64,128]{1,0:T(8,128)S(1)} %select_add_fusion.5), channel_id=1, source_target_pairs={{0,16},{4,20},{8,24},{12,28},{16,0},{20,4},{24,8},{28,12},{32,48},... | collective-permute-start | bytes 98312 | tf_op jit(solution)/shard_map/ppermute | solution.py:154
  194.1 5.1 %collective-permute-start.11 = (f32[64,128]{1,0:T(8,128)S(1)}, f32[64,128]{1,0:T(8,128)S(1)}, u32[]{:S(2)}, u32[]{:S(2)}) collective-permute-start(f32[64,128]{1,0:T(8,128)S(1)} %select_add_fusion.5), channel_id=1, source_target_pairs={{0,8},{4,12},{8,16},{12,20},{16,24},{20,28},{24,0},{28,4},{32,40},... | collective-permute-start | bytes 98312 | tf_op jit(solution)/shard_map/ppermute | solution.py:154
  197.3 3.9 %collective-permute-start.9 = (f32[64,128]{1,0:T(8,128)S(1)}, f32[64,128]{1,0:T(8,128)S(1)}, u32[]{:S(2)}, u32[]{:S(2)}) collective-permute-start(f32[64,128]{1,0:T(8,128)S(1)} %select_add_fusion.5), channel_id=1, source_target_pairs={{0,24},{4,28},{8,0},{12,4},{16,8},{20,12},{24,16},{28,20},{32,56},... | collective-permute-start | bytes 98312 | tf_op jit(solution)/shard_map/ppermute | solution.py:154
  201.2 4.2 %collective-permute-start.12 = (f32[64,128]{1,0:T(8,128)S(1)}, f32[64,128]{1,0:T(8,128)S(1)}, u32[]{:S(2)}, u32[]{:S(2)}) collective-permute-start(f32[64,128]{1,0:T(8,128)S(1)} %select_add_fusion.4), channel_id=1, source_target_pairs={{0,96},{4,100},{8,104},{12,108},{16,112},{20,116},{24,120},{28,124... | collective-permute-start | bytes 98312 | tf_op jit(solution)/shard_map/ppermute | solution.py:154
  201.3 5.5 %collective-permute-start.13 = (f32[64,128]{1,0:T(8,128)S(1)}, f32[64,128]{1,0:T(8,128)S(1)}, u32[]{:S(2)}, u32[]{:S(2)}) collective-permute-start(f32[64,128]{1,0:T(8,128)S(1)} %select_add_fusion.4), channel_id=1, source_target_pairs={{0,64},{4,68},{8,72},{12,76},{16,80},{20,84},{24,88},{28,92},{32,9... | collective-permute-start | bytes 98312 | tf_op jit(solution)/shard_map/ppermute | solution.py:154
  204.8 5.1 %collective-permute-start.14 = (f32[64,128]{1,0:T(8,128)S(1)}, f32[64,128]{1,0:T(8,128)S(1)}, u32[]{:S(2)}, u32[]{:S(2)}) collective-permute-start(f32[64,128]{1,0:T(8,128)S(1)} %select_add_fusion.4), channel_id=1, source_target_pairs={{0,32},{4,36},{8,40},{12,44},{16,48},{20,52},{24,56},{28,60},{32,6... | collective-permute-start | bytes 98312 | tf_op jit(solution)/shard_map/ppermute | solution.py:154
  210.0 6.4 %collective-permute-start.15 = (f32[64,128]{1,0:T(8,128)S(1)}, f32[64,128]{1,0:T(8,128)S(1)}, u32[]{:S(2)}, u32[]{:S(2)}) collective-permute-start(f32[64,128]{1,0:T(8,128)S(1)} %select_add_fusion.3), channel_id=1, source_target_pairs={{0,3},{1,0},{2,1},{3,2},{4,7},{5,4},{6,5},{7,6},{8,11},{9,8},{10,9... | collective-permute-start | bytes 98312 | tf_op jit(solution)/shard_map/ppermute | solution.py:154
  211.2 5.4 %collective-permute-start.16 = (f32[64,128]{1,0:T(8,128)S(1)}, f32[64,128]{1,0:T(8,128)S(1)}, u32[]{:S(2)}, u32[]{:S(2)}) collective-permute-start(f32[64,128]{1,0:T(8,128)S(1)} %select_add_fusion.3), channel_id=1, source_target_pairs={{0,2},{1,3},{2,0},{3,1},{4,6},{5,7},{6,4},{7,5},{8,10},{9,11},{10,... | collective-permute-start | bytes 98312 | tf_op jit(solution)/shard_map/ppermute | solution.py:154
  212.7 5.1 %collective-permute-start.17 = (f32[64,128]{1,0:T(8,128)S(1)}, f32[64,128]{1,0:T(8,128)S(1)}, u32[]{:S(2)}, u32[]{:S(2)}) collective-permute-start(f32[64,128]{1,0:T(8,128)S(1)} %select_add_fusion.3), channel_id=1, source_target_pairs={{0,1},{1,2},{2,3},{3,0},{4,5},{5,6},{6,7},{7,4},{8,9},{9,10},{10,1... | collective-permute-start | bytes 98312 | tf_op jit(solution)/shard_map/ppermute | solution.py:154
  231.4 1.3 collective-permute-start.18
  232.7 4.0 %collective-permute-start.19 = (f32[64,64]{1,0:T(8,128)S(1)}, f32[64,64]{1,0:T(8,128)S(1)}, u32[]{:S(2)}, u32[]{:S(2)}) collective-permute-start(f32[64,64]{1,0:T(8,128)S(1)} %select_add_fusion.2), channel_id=1, source_target_pairs={{0,24},{4,28},{8,0},{12,4},{16,8},{20,12},{24,16},{28,20},{32,56},... | collective-permute-start | bytes 49160 | tf_op jit(solution)/shard_map/ppermute | solution.py:154
  234.1 5.7 %collective-permute-start.20 = (f32[64,64]{1,0:T(8,128)S(1)}, f32[64,64]{1,0:T(8,128)S(1)}, u32[]{:S(2)}, u32[]{:S(2)}) collective-permute-start(f32[64,64]{1,0:T(8,128)S(1)} %select_add_fusion.2), channel_id=1, source_target_pairs={{0,16},{4,20},{8,24},{12,28},{16,0},{20,4},{24,8},{28,12},{32,48},... | collective-permute-start | bytes 49160 | tf_op jit(solution)/shard_map/ppermute | solution.py:154
  234.8 5.2 %collective-permute-start.21 = (f32[64,64]{1,0:T(8,128)S(1)}, f32[64,64]{1,0:T(8,128)S(1)}, u32[]{:S(2)}, u32[]{:S(2)}) collective-permute-start(f32[64,64]{1,0:T(8,128)S(1)} %select_add_fusion.2), channel_id=1, source_target_pairs={{0,8},{4,12},{8,16},{12,20},{16,24},{20,28},{24,0},{28,4},{32,40},... | collective-permute-start | bytes 49160 | tf_op jit(solution)/shard_map/ppermute | solution.py:154
  240.1 4.0 %collective-permute-start.22 = (f32[64,64]{1,0:T(8,128)S(1)}, f32[64,64]{1,0:T(8,128)S(1)}, u32[]{:S(2)}, u32[]{:S(2)}) collective-permute-start(f32[64,64]{1,0:T(8,128)S(1)} %select_add_fusion.1), channel_id=1, source_target_pairs={{0,96},{4,100},{8,104},{12,108},{16,112},{20,116},{24,120},{28,124... | collective-permute-start | bytes 49160 | tf_op jit(solution)/shard_map/ppermute | solution.py:154
  240.2 5.5 %collective-permute-start.23 = (f32[64,64]{1,0:T(8,128)S(1)}, f32[64,64]{1,0:T(8,128)S(1)}, u32[]{:S(2)}, u32[]{:S(2)}) collective-permute-start(f32[64,64]{1,0:T(8,128)S(1)} %select_add_fusion.1), channel_id=1, source_target_pairs={{0,64},{4,68},{8,72},{12,76},{16,80},{20,84},{24,88},{28,92},{32,9... | collective-permute-start | bytes 49160 | tf_op jit(solution)/shard_map/ppermute | solution.py:154
  241.6 5.1 %collective-permute-start.24 = (f32[64,64]{1,0:T(8,128)S(1)}, f32[64,64]{1,0:T(8,128)S(1)}, u32[]{:S(2)}, u32[]{:S(2)}) collective-permute-start(f32[64,64]{1,0:T(8,128)S(1)} %select_add_fusion.1), channel_id=1, source_target_pairs={{0,32},{4,36},{8,40},{12,44},{16,48},{20,52},{24,56},{28,60},{32,6... | collective-permute-start | bytes 49160 | tf_op jit(solution)/shard_map/ppermute | solution.py:154
  246.8 4.0 %collective-permute-start.25 = (f32[64,64]{1,0:T(8,128)S(1)}, f32[64,64]{1,0:T(8,128)S(1)}, u32[]{:S(2)}, u32[]{:S(2)}) collective-permute-start(f32[64,64]{1,0:T(8,128)S(1)} %select_add_fusion), channel_id=1, source_target_pairs={{0,3},{1,0},{2,1},{3,2},{4,7},{5,4},{6,5},{7,6},{8,11},{9,8},{10,9... | collective-permute-start | bytes 49160 | tf_op jit(solution)/shard_map/ppermute | solution.py:154
  248.5 5.4 %collective-permute-start.26 = (f32[64,64]{1,0:T(8,128)S(1)}, f32[64,64]{1,0:T(8,128)S(1)}, u32[]{:S(2)}, u32[]{:S(2)}) collective-permute-start(f32[64,64]{1,0:T(8,128)S(1)} %select_add_fusion), channel_id=1, source_target_pairs={{0,2},{1,3},{2,0},{3,1},{4,6},{5,7},{6,4},{7,5},{8,10},{9,11},{10,... | collective-permute-start | bytes 49160 | tf_op jit(solution)/shard_map/ppermute | solution.py:154
  249.4 5.1 %collective-permute-start.27 = (f32[64,64]{1,0:T(8,128)S(1)}, f32[64,64]{1,0:T(8,128)S(1)}, u32[]{:S(2)}, u32[]{:S(2)}) collective-permute-start(f32[64,64]{1,0:T(8,128)S(1)} %select_add_fusion), channel_id=1, source_target_pairs={{0,1},{1,2},{2,3},{3,0},{4,5},{5,6},{6,7},{7,4},{8,9},{9,10},{10,1... | collective-permute-start | bytes 49160 | tf_op jit(solution)/shard_map/ppermute | solution.py:154
  270.8 55.4 %all-to-all-start.2 = ((f32[128,1,72,128]{3,2,1,0:T(8,128)}), f32[128,1,72,128]{3,2,1,0:T(8,128)}, u32[]{:S(2)}, u32[]{:S(2)}) async-start(f32[128,1,72,128]{3,2,1,0:T(8,128)} %copy.15), calls=%async_computation.2 | async-start | bytes 9437184 | tf_op jit(solution)/shard_map/all_to_all | solution.py:267
  (8 other events, 24.6 us)

commit v7 on v3

--- a/solution.py
+++ b/solution.py
@@ -190,7 +190,7 @@
     def column_step(column, carry):
         current = result_ref[pl.ds(column, 1), :]
         pivot_value = jnp.sum(jnp.where(lanes == column, current, 0.0), axis=1, keepdims=True)
-        inv_root = 1.0 / jnp.sqrt(pivot_value)
+        inv_root = lax.rsqrt(pivot_value)
         scaled = jnp.where(lanes >= column, current, 0.0) * inv_root
         whole = result_ref[...]
         below = jnp.sum(jnp.where(cols == column, whole, 0.0), axis=1, keepdims=True) * inv_root

time: 332 us -> 331 us (level)
  no operation moved by 1% of the time
where the time goes in v7:
time: 331 us; the launch traced here: 330 us
  waiting for transfers between devices  88.1 us (27%)
  starting transfers between devices  69.6 us (21%)
  other arithmetic  62.3 us (19%)
  Pallas kernels  39.4 us (12%)
  blocking collectives  33.3 us (10%)
  local copies, waits for them, and re-layouts  27.2 us (8%)
  matrix products  9.06 us (3%)
    add x3, other arithmetic, local_terms(): return -2.0 * total + potential[None] * orbital_field  54.2 us
    all_to_all x1, waiting for transfers between devices, local(): orbitals = lax.all_to_all(orbitals, 'orb', 0, 1, tiled=True)  49.6 us
    all_to_all x1, blocking collectives, spread_cells(): lax.all_to_all(chunks, 'orb', 1, 0, tiled=True)  33.3 us
    ppermute x4, starting transfers between devices, halo_planes(): before = lax.ppermute(last, axis, up)  32.7 us
    ppermute x20, waiting for transfers between devices, group_round(): received.append(lax.ppermute(value, axis, pairs))  26 us
    pallas_call x4, Pallas kernels, filter_step(): pl.pallas_call(functools.partial(combine_kernel, scale, base is not None)...  23.9 us
    ppermute x20, starting transfers between devices, group_round(): received.append(lax.ppermute(value, axis, pairs))  21.2 us
    pallas_call x2, Pallas kernels, eliminate(): pl.pallas_call(eliminate_kernel, out_shape=jax.ShapeDtypeStruct(source.sh...  15.5 us
  transfers between devices with their start and end apart: 30, of which 19 were waited for; matrix products, arithmetic and copies ran while one was open for 20% of the time, Pallas kernels for 7%

profile of v7, /device:TPU:0, one launch (start us, length us, event | category | flops | bytes accessed | tf_op | source)
XLA Modules:
  0.0 330.0 jit_solution(11318945605626673542)
XLA Ops:
  0.7 4.3 %fusion.113 = (f32[16,6,48,128]{3,2,1,0:T(8,128)S(1)}, f32[16,6,48,128]{3,2,1,0:T(8,128)}) fusion(f32[32,6,48,128]{3,2,1,0:T(8,128)} %refs_4_.3), kind=kLoop, calls=%fused_computation.213 | loop fusion | bytes 9437184 | tf_op jit(solution)/shard_map/slice | solution.py:241
  7.7 16.0 %multiply_add_fusion.refs_0_ = f32[32,6,48,128]{3,2,1,0:T(8,128)} fusion(f32[32,6,48,128]{3,2,1,0:T(8,128)S(1)} %copy-done, f32[6,48,128]{2,1,0:T(8,128)S(1)} %copy-done.6), kind=kLoop, calls=%fused_computation.114 | loop fusion | flops 47185920 | bytes 9584640 | tf_op jit(solution)/shard_map/add | solution.py:49
  25.1 17.4 %collective-permute-start.4 = (f32[16,6,48,128]{3,2,1,0:T(8,128)S(1)}, f32[16,6,48,128]{3,2,1,0:T(8,128)}, u32[]{:S(2)}, u32[]{:S(2)}) collective-permute-start(f32[16,6,48,128]{3,2,1,0:T(8,128)S(1)} %get-tuple-element.22), channel_id=1, source_target_pairs={{0,4},{4,8},{8,12},{12,16},{16,20},{20,24},{24,28},{28,32},{32,36}... | collective-permute-start | bytes 7077896 | tf_op jit(solution)/shard_map/ppermute | solution.py:30
  43.8 5.6 %shard_map.41.refs_1_ = f32[16,6,48,128]{3,2,1,0:T(8,128)} custom-call(f32[32,6,48,128]{3,2,1,0:T(8,128)} %multiply_add_fusion.refs_0_, f32[32,6,48,128]{3,2,1,0:T(8,128)} %refs_4_.3, f32[16,6,48,128]{3,2,1,0:T(8,128)} %copy-done.5, f32[16,6,48,128]{3,2,1,0:T(8,128)} %collective-permute-done.1.refs_3_), custom_call_target="tpu_custom_call" | custom-call | tf_op jit(solution)/shard_map/pallas_call | solution.py:97
  49.4 4.4 %collective-permute-start.2 = (f32[16,6,48,128]{3,2,1,0:T(8,128)}, f32[16,6,48,128]{3,2,1,0:T(8,128)}, u32[]{:S(2)}, u32[]{:S(2)}) collective-permute-start(f32[16,6,48,128]{3,2,1,0:T(8,128)} %shard_map.41.refs_1_), channel_id=1, source_target_pairs={{0,4},{4,8},{8,12},{12,16},{16,20},{20,24},{24,28},{28,32},{32,36}... | collective-permute-start | bytes 7077896 | tf_op jit(solution)/shard_map/ppermute | solution.py:30
  55.1 29.8 %multiply_add_fusion.2.refs_0_ = f32[16,6,48,128]{3,2,1,0:T(8,128)} fusion(f32[16,6,48,128]{3,2,1,0:T(8,128)} %shard_map.41.refs_1_, f32[6,48,128]{2,1,0:T(8,128)S(1)} %copy-done.6), kind=kLoop, calls=%fused_computation.191 | loop fusion | flops 23592960 | bytes 4866048 | tf_op jit(solution)/shard_map/add | solution.py:49
  84.9 5.6 %shard_map.42.refs_1_ = f32[16,6,48,128]{3,2,1,0:T(8,128)} custom-call(f32[32,6,48,128]{3,2,1,0:T(8,128)} %multiply_add_fusion.refs_0_, f32[32,6,48,128]{3,2,1,0:T(8,128)} %refs_4_.3, f32[16,6,48,128]{3,2,1,0:T(8,128)} %collective-permute-done.4.refs_2_, f32[16,6,48,128]{3,2,1,0:T(8,128)} %collective-permute-done.5.refs_3_), custom_call_target="tpu_custom_call" | custom-call | tf_op jit(solution)/shard_map/pallas_call | solution.py:97
  90.5 9.4 %collective-permute-start.6 = (f32[16,6,48,128]{3,2,1,0:T(8,128)}, f32[16,6,48,128]{3,2,1,0:T(8,128)}, u32[]{:S(2)}, u32[]{:S(2)}) collective-permute-start(f32[16,6,48,128]{3,2,1,0:T(8,128)} %shard_map.42.refs_1_), channel_id=1, source_target_pairs={{0,4},{4,8},{8,12},{12,16},{16,20},{20,24},{24,28},{28,32},{32,36}... | collective-permute-start | bytes 7077896 | tf_op jit(solution)/shard_map/ppermute | solution.py:30
  101.2 6.4 %shard_map.43 = f32[16,6,48,128]{3,2,1,0:T(8,128)} custom-call(f32[16,6,48,128]{3,2,1,0:T(8,128)} %multiply_add_fusion.2.refs_0_, f32[16,6,48,128]{3,2,1,0:T(8,128)} %shard_map.41.refs_1_, f32[16,6,48,128]{3,2,1,0:T(8,128)} %collective-permute-done.2.refs_2_, f32[16,6,48,128]{3,2,1,0:T(8,128)} %collective-permute-done.3.refs_3_, f32[32,6,48,128]{3,2,1,0:T(8,128)} %refs_4_.3), custom_call_target="tpu_custom_call" | custom-call | tf_op jit(solution)/shard_map/pallas_call | solution.py:97
  107.6 3.2 copy.9
  110.8 5.4 %all-to-all-start = ((f32[16,4,72,128]{3,2,0,1:T(8,128)}), f32[16,4,72,128]{3,2,0,1:T(8,128)}, u32[]{:S(2)}, u32[]{:S(2)}) async-start(f32[16,4,72,128]{3,2,0,1:T(8,128)} %copy.9), calls=%async_computation | async-start | bytes 4718592 | tf_op jit(solution)/shard_map/all_to_all | solution.py:112
  116.2 8.4 %multiply_add_fusion.1.refs_0_ = f32[16,6,48,128]{3,2,1,0:T(8,128)} fusion(f32[16,6,48,128]{3,2,1,0:T(8,128)S(1)} %copy-done.3, f32[6,48,128]{2,1,0:T(8,128)S(1)} %copy-done.6), kind=kLoop, calls=%fused_computation.190 | loop fusion | flops 23592960 | bytes 4866048 | tf_op jit(solution)/shard_map/add | solution.py:49
  124.7 6.4 %shard_map.44 = f32[16,6,48,128]{3,2,1,0:T(8,128)} custom-call(f32[16,6,48,128]{3,2,1,0:T(8,128)} %multiply_add_fusion.1.refs_0_, f32[16,6,48,128]{3,2,1,0:T(8,128)} %shard_map.42.refs_1_, f32[16,6,48,128]{3,2,1,0:T(8,128)} %collective-permute-done.6.refs_2_, f32[16,6,48,128]{3,2,1,0:T(8,128)} %collective-permute-done.7.refs_3_, f32[32,6,48,128]{3,2,1,0:T(8,128)} %refs_4_.3), custom_call_target="tpu_custom_call" | custom-call | tf_op jit(solution)/shard_map/pallas_call | solution.py:97
  131.0 3.2 copy.10
  134.3 12.5 %all-to-all-done = f32[16,4,72,128]{3,2,0,1:T(8,128)} async-done(((f32[16,4,72,128]{3,2,0,1:T(8,128)}), f32[16,4,72,128]{3,2,0,1:T(8,128)}, u32[]{:S(2)}, u32[]{:S(2)}) %all-to-all-start) | async-done | bytes 2359328 | tf_op jit(solution)/shard_map/all_to_all | solution.py:112
  146.8 33.3 %all_to_all.45 = f32[16,4,72,128]{3,2,0,1:T(8,128)S(1)} all-to-all(f32[16,4,72,128]{3,2,0,1:T(8,128)} %copy.10), channel_id=1, replica_groups=mesh['grid'=32,'orb'=4] {'orb'}, dimensions={1} | all-to-all | bytes 4718592 | tf_op jit(solution)/shard_map/all_to_all | solution.py:112
  182.1 3.4 %fusion.36 = (f32[2,2,16,72,128]{4,3,2,0,1:T(8,128)S(1)}, f32[2,2,16,72,128]{4,3,2,0,1:T(8,128)}) fusion(f32[4,1,16,72,128]{4,3,2,0,1:T(8,128)} %bitcast.3, f32[4,1,16,72,128]{4,3,2,0,1:T(8,128)S(1)} %bitcast.46), kind=kLoop, calls=%fused_computation.115 | loop fusion | flops 1179648 | bytes 9437184 | tf_op jit(solution)/shard_map/stack | solution.py:261
  186.8 2.6 convolution_bitcast_fusion.1
  190.7 3.0 collective-permute-start.10
  193.7 3.1 collective-permute-start.11
  200.9 3.5 %collective-permute-start.13 = (f32[64,128]{1,0:T(8,128)S(1)}, f32[64,128]{1,0:T(8,128)S(1)}, u32[]{:S(2)}, u32[]{:S(2)}) collective-permute-start(f32[64,128]{1,0:T(8,128)S(1)} %select_add_fusion.4), channel_id=1, source_target_pairs={{0,64},{4,68},{8,72},{12,76},{16,80},{20,84},{24,88},{28,92},{32,9... | collective-permute-start | bytes 98312 | tf_op jit(solution)/shard_map/ppermute | solution.py:154
  206.4 3.1 collective-permute-done.14
  212.4 3.6 %copy.13 = f32[2,2,16,72,128]{4,2,1,0,3:T(8,128)} copy(f32[2,2,16,72,128]{4,3,2,0,1:T(8,128)} %get-tuple-element.33) | data formatting | bytes 4718592 | tf_op jit(solution)/shard_map/slice | solution.py:222
  218.1 7.9 %shard_map.45 = f32[64,192]{1,0:T(8,128)} custom-call(f32[64,192]{1,0:T(8,128)} %pad_maximum_fusion.1.source_ref), custom_call_target="tpu_custom_call" | custom-call | tf_op jit(solution)/shard_map/pallas_call | solution.py:207
  235.8 3.1 collective-permute-done.20
  249.9 3.2 collective-permute-done.26
  254.4 7.5 %shard_map.46 = f32[64,128]{1,0:T(8,128)} custom-call(f32[64,128]{1,0:T(8,128)} %pad_maximum_fusion.2.source_ref), custom_call_target="tpu_custom_call" | custom-call | tf_op jit(solution)/shard_map/pallas_call | solution.py:207
  261.9 2.1 fusion.110
  264.5 4.9 %copy.15 = f32[128,1,72,128]{3,2,1,0:T(8,128)} copy(f32[128,1,72,128]{3,0,2,1:T(8,128)S(1)} %maximum_bitcast_fusion) | data formatting | bytes 9437184 | tf_op jit(solution)/shard_map/reshape | solution.py:266
  269.5 5.1 %all-to-all-start.2 = ((f32[128,1,72,128]{3,2,1,0:T(8,128)}), f32[128,1,72,128]{3,2,1,0:T(8,128)}, u32[]{:S(2)}, u32[]{:S(2)}) async-start(f32[128,1,72,128]{3,2,1,0:T(8,128)} %copy.15), calls=%async_computation.2 | async-start | bytes 9437184 | tf_op jit(solution)/shard_map/all_to_all | solution.py:267
  275.3 49.6 %all-to-all-done.2 = f32[128,1,72,128]{3,2,1,0:T(8,128)} async-done(((f32[128,1,72,128]{3,2,1,0:T(8,128)}), f32[128,1,72,128]{3,2,1,0:T(8,128)}, u32[]{:S(2)}, u32[]{:S(2)}) %all-to-all-start.2) | async-done | bytes 4718624 | tf_op jit(solution)/shard_map/all_to_all | solution.py:267
  324.9 5.1 %copy.16 = f32[32,4,1,72,128]{4,3,1,0,2:T(8,128)} copy(f32[32,4,1,72,128]{4,3,0,1,2:T(8,128)} %bitcast.18) | data formatting | bytes 9437184 | tf_op jit(solution)/shard_map/all_to_all | solution.py:267
  (86 shorter events, 46.8 us)
Async XLA Ops:
  0.6 7.1 %copy-start = (f32[32,6,48,128]{3,2,1,0:T(8,128)S(1)}, f32[32,6,48,128]{3,2,1,0:T(8,128)}, u32[]{:S(2)}) copy-start(f32[32,6,48,128]{3,2,1,0:T(8,128)} %refs_4_.3) | copy-start | bytes 14155780
  0.6 7.1 %copy-start.6 = (f32[6,48,128]{2,1,0:T(8,128)S(1)}, f32[6,48,128]{2,1,0:T(8,128)}, u32[]{:S(2)}) copy-start(f32[6,48,128]{2,1,0:T(8,128)} %param.3) | copy-start | bytes 442372
  5.0 18.7 %collective-permute-start = (f32[16,6,48,128]{3,2,1,0:T(8,128)}, f32[16,6,48,128]{3,2,1,0:T(8,128)S(1)}, u32[]{:S(2)}, u32[]{:S(2)}) collective-permute-start(f32[16,6,48,128]{3,2,1,0:T(8,128)} %get-tuple-element.35), channel_id=1, source_target_pairs={{0,4},{4,8},{8,12},{12,16},{16,20},{20,24},{24,28},{28,32},{32,36}... | collective-permute-start | bytes 7077896 | tf_op jit(solution)/shard_map/ppermute | solution.py:30
  6.4 17.3 %collective-permute-start.1 = (f32[16,6,48,128]{3,2,1,0:T(8,128)}, f32[16,6,48,128]{3,2,1,0:T(8,128)}, u32[]{:S(2)}, u32[]{:S(2)}) collective-permute-start(f32[16,6,48,128]{3,2,1,0:T(8,128)} %get-tuple-element.35), channel_id=1, source_target_pairs={{4,0},{8,4},{12,8},{16,12},{20,16},{24,20},{28,24},{32,28},{36,32}... | collective-permute-start | bytes 7077896 | tf_op jit(solution)/shard_map/ppermute | solution.py:31
  25.1 59.7 %collective-permute-start.4 = (f32[16,6,48,128]{3,2,1,0:T(8,128)S(1)}, f32[16,6,48,128]{3,2,1,0:T(8,128)}, u32[]{:S(2)}, u32[]{:S(2)}) collective-permute-start(f32[16,6,48,128]{3,2,1,0:T(8,128)S(1)} %get-tuple-element.22), channel_id=1, source_target_pairs={{0,4},{4,8},{8,12},{12,16},{16,20},{20,24},{24,28},{28,32},{32,36}... | collective-permute-start | bytes 7077896 | tf_op jit(solution)/shard_map/ppermute | solution.py:30
  42.5 42.4 %collective-permute-start.5 = (f32[16,6,48,128]{3,2,1,0:T(8,128)S(1)}, f32[16,6,48,128]{3,2,1,0:T(8,128)}, u32[]{:S(2)}, u32[]{:S(2)}) collective-permute-start(f32[16,6,48,128]{3,2,1,0:T(8,128)S(1)} %get-tuple-element.22), channel_id=1, source_target_pairs={{4,0},{8,4},{12,8},{16,12},{20,16},{24,20},{28,24},{32,28},{36,32}... | collective-permute-start | bytes 7077896 | tf_op jit(solution)/shard_map/ppermute | solution.py:31
  49.4 41.1 %collective-permute-start.2 = (f32[16,6,48,128]{3,2,1,0:T(8,128)}, f32[16,6,48,128]{3,2,1,0:T(8,128)}, u32[]{:S(2)}, u32[]{:S(2)}) collective-permute-start(f32[16,6,48,128]{3,2,1,0:T(8,128)} %shard_map.41.refs_1_), channel_id=1, source_target_pairs={{0,4},{4,8},{8,12},{12,16},{16,20},{20,24},{24,28},{28,32},{32,36}... | collective-permute-start | bytes 7077896 | tf_op jit(solution)/shard_map/ppermute | solution.py:30
  53.8 36.7 %collective-permute-start.3 = (f32[16,6,48,128]{3,2,1,0:T(8,128)}, f32[16,6,48,128]{3,2,1,0:T(8,128)}, u32[]{:S(2)}, u32[]{:S(2)}) collective-permute-start(f32[16,6,48,128]{3,2,1,0:T(8,128)} %shard_map.41.refs_1_), channel_id=1, source_target_pairs={{4,0},{8,4},{12,8},{16,12},{20,16},{24,20},{28,24},{32,28},{36,32}... | collective-permute-start | bytes 7077896 | tf_op jit(solution)/shard_map/ppermute | solution.py:31
  90.5 34.2 %collective-permute-start.6 = (f32[16,6,48,128]{3,2,1,0:T(8,128)}, f32[16,6,48,128]{3,2,1,0:T(8,128)}, u32[]{:S(2)}, u32[]{:S(2)}) collective-permute-start(f32[16,6,48,128]{3,2,1,0:T(8,128)} %shard_map.42.refs_1_), channel_id=1, source_target_pairs={{0,4},{4,8},{8,12},{12,16},{16,20},{20,24},{24,28},{28,32},{32,36}... | collective-permute-start | bytes 7077896 | tf_op jit(solution)/shard_map/ppermute | solution.py:30
  100.0 24.7 %collective-permute-start.7 = (f32[16,6,48,128]{3,2,1,0:T(8,128)}, f32[16,6,48,128]{3,2,1,0:T(8,128)}, u32[]{:S(2)}, u32[]{:S(2)}) collective-permute-start(f32[16,6,48,128]{3,2,1,0:T(8,128)} %shard_map.42.refs_1_), channel_id=1, source_target_pairs={{4,0},{8,4},{12,8},{16,12},{20,16},{24,20},{28,24},{32,28},{36,32}... | collective-permute-start | bytes 7077896 | tf_op jit(solution)/shard_map/ppermute | solution.py:31
  110.8 36.0 %all-to-all-start = ((f32[16,4,72,128]{3,2,0,1:T(8,128)}), f32[16,4,72,128]{3,2,0,1:T(8,128)}, u32[]{:S(2)}, u32[]{:S(2)}) async-start(f32[16,4,72,128]{3,2,0,1:T(8,128)} %copy.9), calls=%async_computation | async-start | bytes 4718592 | tf_op jit(solution)/shard_map/all_to_all | solution.py:112
  189.4 1.3 collective-permute-start.8
  190.7 6.3 %collective-permute-start.10 = (f32[64,128]{1,0:T(8,128)S(1)}, f32[64,128]{1,0:T(8,128)S(1)}, u32[]{:S(2)}, u32[]{:S(2)}) collective-permute-start(f32[64,128]{1,0:T(8,128)S(1)} %select_add_fusion.5), channel_id=1, source_target_pairs={{0,16},{4,20},{8,24},{12,28},{16,0},{20,4},{24,8},{28,12},{32,48},... | collective-permute-start | bytes 98312 | tf_op jit(solution)/shard_map/ppermute | solution.py:154
  193.7 5.1 %collective-permute-start.11 = (f32[64,128]{1,0:T(8,128)S(1)}, f32[64,128]{1,0:T(8,128)S(1)}, u32[]{:S(2)}, u32[]{:S(2)}) collective-permute-start(f32[64,128]{1,0:T(8,128)S(1)} %select_add_fusion.5), channel_id=1, source_target_pairs={{0,8},{4,12},{8,16},{12,20},{16,24},{20,28},{24,0},{28,4},{32,40},... | collective-permute-start | bytes 98312 | tf_op jit(solution)/shard_map/ppermute | solution.py:154
  196.8 3.9 %collective-permute-start.9 = (f32[64,128]{1,0:T(8,128)S(1)}, f32[64,128]{1,0:T(8,128)S(1)}, u32[]{:S(2)}, u32[]{:S(2)}) collective-permute-start(f32[64,128]{1,0:T(8,128)S(1)} %select_add_fusion.5), channel_id=1, source_target_pairs={{0,24},{4,28},{8,0},{12,4},{16,8},{20,12},{24,16},{28,20},{32,56},... | collective-permute-start | bytes 98312 | tf_op jit(solution)/shard_map/ppermute | solution.py:154
  200.8 4.2 %collective-permute-start.12 = (f32[64,128]{1,0:T(8,128)S(1)}, f32[64,128]{1,0:T(8,128)S(1)}, u32[]{:S(2)}, u32[]{:S(2)}) collective-permute-start(f32[64,128]{1,0:T(8,128)S(1)} %select_add_fusion.4), channel_id=1, source_target_pairs={{0,96},{4,100},{8,104},{12,108},{16,112},{20,116},{24,120},{28,124... | collective-permute-start | bytes 98312 | tf_op jit(solution)/shard_map/ppermute | solution.py:154
  200.9 5.5 %collective-permute-start.13 = (f32[64,128]{1,0:T(8,128)S(1)}, f32[64,128]{1,0:T(8,128)S(1)}, u32[]{:S(2)}, u32[]{:S(2)}) collective-permute-start(f32[64,128]{1,0:T(8,128)S(1)} %select_add_fusion.4), channel_id=1, source_target_pairs={{0,64},{4,68},{8,72},{12,76},{16,80},{20,84},{24,88},{28,92},{32,9... | collective-permute-start | bytes 98312 | tf_op jit(solution)/shard_map/ppermute | solution.py:154
  204.4 5.1 %collective-permute-start.14 = (f32[64,128]{1,0:T(8,128)S(1)}, f32[64,128]{1,0:T(8,128)S(1)}, u32[]{:S(2)}, u32[]{:S(2)}) collective-permute-start(f32[64,128]{1,0:T(8,128)S(1)} %select_add_fusion.4), channel_id=1, source_target_pairs={{0,32},{4,36},{8,40},{12,44},{16,48},{20,52},{24,56},{28,60},{32,6... | collective-permute-start | bytes 98312 | tf_op jit(solution)/shard_map/ppermute | solution.py:154
  209.6 6.4 %collective-permute-start.15 = (f32[64,128]{1,0:T(8,128)S(1)}, f32[64,128]{1,0:T(8,128)S(1)}, u32[]{:S(2)}, u32[]{:S(2)}) collective-permute-start(f32[64,128]{1,0:T(8,128)S(1)} %select_add_fusion.3), channel_id=1, source_target_pairs={{0,3},{1,0},{2,1},{3,2},{4,7},{5,4},{6,5},{7,6},{8,11},{9,8},{10,9... | collective-permute-start | bytes 98312 | tf_op jit(solution)/shard_map/ppermute | solution.py:154
  210.8 5.4 %collective-permute-start.16 = (f32[64,128]{1,0:T(8,128)S(1)}, f32[64,128]{1,0:T(8,128)S(1)}, u32[]{:S(2)}, u32[]{:S(2)}) collective-permute-start(f32[64,128]{1,0:T(8,128)S(1)} %select_add_fusion.3), channel_id=1, source_target_pairs={{0,2},{1,3},{2,0},{3,1},{4,6},{5,7},{6,4},{7,5},{8,10},{9,11},{10,... | collective-permute-start | bytes 98312 | tf_op jit(solution)/shard_map/ppermute | solution.py:154
  212.3 5.1 %collective-permute-start.17 = (f32[64,128]{1,0:T(8,128)S(1)}, f32[64,128]{1,0:T(8,128)S(1)}, u32[]{:S(2)}, u32[]{:S(2)}) collective-permute-start(f32[64,128]{1,0:T(8,128)S(1)} %select_add_fusion.3), channel_id=1, source_target_pairs={{0,1},{1,2},{2,3},{3,0},{4,5},{5,6},{6,7},{7,4},{8,9},{9,10},{10,1... | collective-permute-start | bytes 98312 | tf_op jit(solution)/shard_map/ppermute | solution.py:154
  230.5 1.3 collective-permute-start.18
  231.8 4.0 %collective-permute-start.19 = (f32[64,64]{1,0:T(8,128)S(1)}, f32[64,64]{1,0:T(8,128)S(1)}, u32[]{:S(2)}, u32[]{:S(2)}) collective-permute-start(f32[64,64]{1,0:T(8,128)S(1)} %select_add_fusion.2), channel_id=1, source_target_pairs={{0,24},{4,28},{8,0},{12,4},{16,8},{20,12},{24,16},{28,20},{32,56},... | collective-permute-start | bytes 49160 | tf_op jit(solution)/shard_map/ppermute | solution.py:154
  233.2 5.7 %collective-permute-start.20 = (f32[64,64]{1,0:T(8,128)S(1)}, f32[64,64]{1,0:T(8,128)S(1)}, u32[]{:S(2)}, u32[]{:S(2)}) collective-permute-start(f32[64,64]{1,0:T(8,128)S(1)} %select_add_fusion.2), channel_id=1, source_target_pairs={{0,16},{4,20},{8,24},{12,28},{16,0},{20,4},{24,8},{28,12},{32,48},... | collective-permute-start | bytes 49160 | tf_op jit(solution)/shard_map/ppermute | solution.py:154
  234.0 5.2 %collective-permute-start.21 = (f32[64,64]{1,0:T(8,128)S(1)}, f32[64,64]{1,0:T(8,128)S(1)}, u32[]{:S(2)}, u32[]{:S(2)}) collective-permute-start(f32[64,64]{1,0:T(8,128)S(1)} %select_add_fusion.2), channel_id=1, source_target_pairs={{0,8},{4,12},{8,16},{12,20},{16,24},{20,28},{24,0},{28,4},{32,40},... | collective-permute-start | bytes 49160 | tf_op jit(solution)/shard_map/ppermute | solution.py:154
  239.2 4.0 %collective-permute-start.22 = (f32[64,64]{1,0:T(8,128)S(1)}, f32[64,64]{1,0:T(8,128)S(1)}, u32[]{:S(2)}, u32[]{:S(2)}) collective-permute-start(f32[64,64]{1,0:T(8,128)S(1)} %select_add_fusion.1), channel_id=1, source_target_pairs={{0,96},{4,100},{8,104},{12,108},{16,112},{20,116},{24,120},{28,124... | collective-permute-start | bytes 49160 | tf_op jit(solution)/shard_map/ppermute | solution.py:154
  239.3 5.5 %collective-permute-start.23 = (f32[64,64]{1,0:T(8,128)S(1)}, f32[64,64]{1,0:T(8,128)S(1)}, u32[]{:S(2)}, u32[]{:S(2)}) collective-permute-start(f32[64,64]{1,0:T(8,128)S(1)} %select_add_fusion.1), channel_id=1, source_target_pairs={{0,64},{4,68},{8,72},{12,76},{16,80},{20,84},{24,88},{28,92},{32,9... | collective-permute-start | bytes 49160 | tf_op jit(solution)/shard_map/ppermute | solution.py:154
  240.7 5.1 %collective-permute-start.24 = (f32[64,64]{1,0:T(8,128)S(1)}, f32[64,64]{1,0:T(8,128)S(1)}, u32[]{:S(2)}, u32[]{:S(2)}) collective-permute-start(f32[64,64]{1,0:T(8,128)S(1)} %select_add_fusion.1), channel_id=1, source_target_pairs={{0,32},{4,36},{8,40},{12,44},{16,48},{20,52},{24,56},{28,60},{32,6... | collective-permute-start | bytes 49160 | tf_op jit(solution)/shard_map/ppermute | solution.py:154
  245.9 4.0 %collective-permute-start.25 = (f32[64,64]{1,0:T(8,128)S(1)}, f32[64,64]{1,0:T(8,128)S(1)}, u32[]{:S(2)}, u32[]{:S(2)}) collective-permute-start(f32[64,64]{1,0:T(8,128)S(1)} %select_add_fusion), channel_id=1, source_target_pairs={{0,3},{1,0},{2,1},{3,2},{4,7},{5,4},{6,5},{7,6},{8,11},{9,8},{10,9... | collective-permute-start | bytes 49160 | tf_op jit(solution)/shard_map/ppermute | solution.py:154
  247.7 5.4 %collective-permute-start.26 = (f32[64,64]{1,0:T(8,128)S(1)}, f32[64,64]{1,0:T(8,128)S(1)}, u32[]{:S(2)}, u32[]{:S(2)}) collective-permute-start(f32[64,64]{1,0:T(8,128)S(1)} %select_add_fusion), channel_id=1, source_target_pairs={{0,2},{1,3},{2,0},{3,1},{4,6},{5,7},{6,4},{7,5},{8,10},{9,11},{10,... | collective-permute-start | bytes 49160 | tf_op jit(solution)/shard_map/ppermute | solution.py:154
  248.5 5.1 %collective-permute-start.27 = (f32[64,64]{1,0:T(8,128)S(1)}, f32[64,64]{1,0:T(8,128)S(1)}, u32[]{:S(2)}, u32[]{:S(2)}) collective-permute-start(f32[64,64]{1,0:T(8,128)S(1)} %select_add_fusion), channel_id=1, source_target_pairs={{0,1},{1,2},{2,3},{3,0},{4,5},{5,6},{6,7},{7,4},{8,9},{9,10},{10,1... | collective-permute-start | bytes 49160 | tf_op jit(solution)/shard_map/ppermute | solution.py:154
  269.5 55.4 %all-to-all-start.2 = ((f32[128,1,72,128]{3,2,1,0:T(8,128)}), f32[128,1,72,128]{3,2,1,0:T(8,128)}, u32[]{:S(2)}, u32[]{:S(2)}) async-start(f32[128,1,72,128]{3,2,1,0:T(8,128)} %copy.15), calls=%async_computation.2 | async-start | bytes 9437184 | tf_op jit(solution)/shard_map/all_to_all | solution.py:267
  (8 other events, 24.6 us)

commit v8 on v7

--- a/solution.py
+++ b/solution.py
@@ -69,7 +69,7 @@
         for k in range(2, 7):
             acc = acc + coefs[k] * (plane(p + k) + plane(p - k))
         value = local_ref[:, p] - 2.0 * acc
-        value = scale * (value - centre * own_ref[:, p]) / radius
+        value = (value - centre * own_ref[:, p]) * (scale / radius)
         if with_base:
             value = value - base_ref[:, p]
         out_ref[:, p] = value

time: 331 us -> 331 us (level)
  no operation moved by 1% of the time
where the time goes in v8:
time: 331 us; the launch traced here: 330 us
  waiting for transfers between devices  88.2 us (27%)
  starting transfers between devices  69.6 us (21%)
  other arithmetic  62.3 us (19%)
  Pallas kernels  39.3 us (12%)
  blocking collectives  33.3 us (10%)
  local copies, waits for them, and re-layouts  27.2 us (8%)
  matrix products  9.06 us (3%)
    add x3, other arithmetic, local_terms(): return -2.0 * total + potential[None] * orbital_field  54.2 us
    all_to_all x1, waiting for transfers between devices, local(): orbitals = lax.all_to_all(orbitals, 'orb', 0, 1, tiled=True)  49.6 us
    all_to_all x1, blocking collectives, spread_cells(): lax.all_to_all(chunks, 'orb', 1, 0, tiled=True)  33.3 us
    ppermute x4, starting transfers between devices, halo_planes(): before = lax.ppermute(last, axis, up)  32.7 us
    ppermute x20, waiting for transfers between devices, group_round(): received.append(lax.ppermute(value, axis, pairs))  26 us
    pallas_call x4, Pallas kernels, filter_step(): pl.pallas_call(functools.partial(combine_kernel, scale, base is not None)...  23.9 us
    ppermute x20, starting transfers between devices, group_round(): received.append(lax.ppermute(value, axis, pairs))  21.2 us
    pallas_call x2, Pallas kernels, eliminate(): pl.pallas_call(eliminate_kernel, out_shape=jax.ShapeDtypeStruct(source.sh...  15.5 us
  transfers between devices with their start and end apart: 30, of which 19 were waited for; matrix products, arithmetic and copies ran while one was open for 20% of the time, Pallas kernels for 7%

profile of v8, /device:TPU:0, one launch (start us, length us, event | category | flops | bytes accessed | tf_op | source)
XLA Modules:
  0.0 329.9 jit_solution(18413527375694263849)
XLA Ops:
  0.7 4.3 %fusion.113 = (f32[16,6,48,128]{3,2,1,0:T(8,128)S(1)}, f32[16,6,48,128]{3,2,1,0:T(8,128)}) fusion(f32[32,6,48,128]{3,2,1,0:T(8,128)} %refs_4_.3), kind=kLoop, calls=%fused_computation.213 | loop fusion | bytes 9437184 | tf_op jit(solution)/shard_map/slice | solution.py:241
  7.7 16.0 %multiply_add_fusion.refs_0_ = f32[32,6,48,128]{3,2,1,0:T(8,128)} fusion(f32[32,6,48,128]{3,2,1,0:T(8,128)S(1)} %copy-done, f32[6,48,128]{2,1,0:T(8,128)S(1)} %copy-done.6), kind=kLoop, calls=%fused_computation.114 | loop fusion | flops 47185920 | bytes 9584640 | tf_op jit(solution)/shard_map/add | solution.py:49
  25.1 17.4 %collective-permute-start.4 = (f32[16,6,48,128]{3,2,1,0:T(8,128)S(1)}, f32[16,6,48,128]{3,2,1,0:T(8,128)}, u32[]{:S(2)}, u32[]{:S(2)}) collective-permute-start(f32[16,6,48,128]{3,2,1,0:T(8,128)S(1)} %get-tuple-element.22), channel_id=1, source_target_pairs={{0,4},{4,8},{8,12},{12,16},{16,20},{20,24},{24,28},{28,32},{32,36}... | collective-permute-start | bytes 7077896 | tf_op jit(solution)/shard_map/ppermute | solution.py:30
  43.8 5.6 %shard_map.41.refs_1_ = f32[16,6,48,128]{3,2,1,0:T(8,128)} custom-call(f32[32,6,48,128]{3,2,1,0:T(8,128)} %multiply_add_fusion.refs_0_, f32[32,6,48,128]{3,2,1,0:T(8,128)} %refs_4_.3, f32[16,6,48,128]{3,2,1,0:T(8,128)} %copy-done.5, f32[16,6,48,128]{3,2,1,0:T(8,128)} %collective-permute-done.1.refs_3_), custom_call_target="tpu_custom_call" | custom-call | tf_op jit(solution)/shard_map/pallas_call | solution.py:97
  49.4 4.4 %collective-permute-start.2 = (f32[16,6,48,128]{3,2,1,0:T(8,128)}, f32[16,6,48,128]{3,2,1,0:T(8,128)}, u32[]{:S(2)}, u32[]{:S(2)}) collective-permute-start(f32[16,6,48,128]{3,2,1,0:T(8,128)} %shard_map.41.refs_1_), channel_id=1, source_target_pairs={{0,4},{4,8},{8,12},{12,16},{16,20},{20,24},{24,28},{28,32},{32,36}... | collective-permute-start | bytes 7077896 | tf_op jit(solution)/shard_map/ppermute | solution.py:30
  55.1 29.8 %multiply_add_fusion.2.refs_0_ = f32[16,6,48,128]{3,2,1,0:T(8,128)} fusion(f32[16,6,48,128]{3,2,1,0:T(8,128)} %shard_map.41.refs_1_, f32[6,48,128]{2,1,0:T(8,128)S(1)} %copy-done.6), kind=kLoop, calls=%fused_computation.191 | loop fusion | flops 23592960 | bytes 4866048 | tf_op jit(solution)/shard_map/add | solution.py:49
  84.9 5.6 %shard_map.42.refs_1_ = f32[16,6,48,128]{3,2,1,0:T(8,128)} custom-call(f32[32,6,48,128]{3,2,1,0:T(8,128)} %multiply_add_fusion.refs_0_, f32[32,6,48,128]{3,2,1,0:T(8,128)} %refs_4_.3, f32[16,6,48,128]{3,2,1,0:T(8,128)} %collective-permute-done.4.refs_2_, f32[16,6,48,128]{3,2,1,0:T(8,128)} %collective-permute-done.5.refs_3_), custom_call_target="tpu_custom_call" | custom-call | tf_op jit(solution)/shard_map/pallas_call | solution.py:97
  90.5 9.4 %collective-permute-start.6 = (f32[16,6,48,128]{3,2,1,0:T(8,128)}, f32[16,6,48,128]{3,2,1,0:T(8,128)}, u32[]{:S(2)}, u32[]{:S(2)}) collective-permute-start(f32[16,6,48,128]{3,2,1,0:T(8,128)} %shard_map.42.refs_1_), channel_id=1, source_target_pairs={{0,4},{4,8},{8,12},{12,16},{16,20},{20,24},{24,28},{28,32},{32,36}... | collective-permute-start | bytes 7077896 | tf_op jit(solution)/shard_map/ppermute | solution.py:30
  101.2 6.3 %shard_map.43 = f32[16,6,48,128]{3,2,1,0:T(8,128)} custom-call(f32[16,6,48,128]{3,2,1,0:T(8,128)} %multiply_add_fusion.2.refs_0_, f32[16,6,48,128]{3,2,1,0:T(8,128)} %shard_map.41.refs_1_, f32[16,6,48,128]{3,2,1,0:T(8,128)} %collective-permute-done.2.refs_2_, f32[16,6,48,128]{3,2,1,0:T(8,128)} %collective-permute-done.3.refs_3_, f32[32,6,48,128]{3,2,1,0:T(8,128)} %refs_4_.3), custom_call_target="tpu_custom_call" | custom-call | tf_op jit(solution)/shard_map/pallas_call | solution.py:97
  107.6 3.2 copy.9
  110.8 5.4 %all-to-all-start = ((f32[16,4,72,128]{3,2,0,1:T(8,128)}), f32[16,4,72,128]{3,2,0,1:T(8,128)}, u32[]{:S(2)}, u32[]{:S(2)}) async-start(f32[16,4,72,128]{3,2,0,1:T(8,128)} %copy.9), calls=%async_computation | async-start | bytes 4718592 | tf_op jit(solution)/shard_map/all_to_all | solution.py:112
  116.2 8.4 %multiply_add_fusion.1.refs_0_ = f32[16,6,48,128]{3,2,1,0:T(8,128)} fusion(f32[16,6,48,128]{3,2,1,0:T(8,128)S(1)} %copy-done.3, f32[6,48,128]{2,1,0:T(8,128)S(1)} %copy-done.6), kind=kLoop, calls=%fused_computation.190 | loop fusion | flops 23592960 | bytes 4866048 | tf_op jit(solution)/shard_map/add | solution.py:49
  124.6 6.3 %shard_map.44 = f32[16,6,48,128]{3,2,1,0:T(8,128)} custom-call(f32[16,6,48,128]{3,2,1,0:T(8,128)} %multiply_add_fusion.1.refs_0_, f32[16,6,48,128]{3,2,1,0:T(8,128)} %shard_map.42.refs_1_, f32[16,6,48,128]{3,2,1,0:T(8,128)} %collective-permute-done.6.refs_2_, f32[16,6,48,128]{3,2,1,0:T(8,128)} %collective-permute-done.7.refs_3_, f32[32,6,48,128]{3,2,1,0:T(8,128)} %refs_4_.3), custom_call_target="tpu_custom_call" | custom-call | tf_op jit(solution)/shard_map/pallas_call | solution.py:97
  131.0 3.2 copy.10
  134.2 12.5 %all-to-all-done = f32[16,4,72,128]{3,2,0,1:T(8,128)} async-done(((f32[16,4,72,128]{3,2,0,1:T(8,128)}), f32[16,4,72,128]{3,2,0,1:T(8,128)}, u32[]{:S(2)}, u32[]{:S(2)}) %all-to-all-start) | async-done | bytes 2359328 | tf_op jit(solution)/shard_map/all_to_all | solution.py:112
  146.7 33.3 %all_to_all.45 = f32[16,4,72,128]{3,2,0,1:T(8,128)S(1)} all-to-all(f32[16,4,72,128]{3,2,0,1:T(8,128)} %copy.10), channel_id=1, replica_groups=mesh['grid'=32,'orb'=4] {'orb'}, dimensions={1} | all-to-all | bytes 4718592 | tf_op jit(solution)/shard_map/all_to_all | solution.py:112
  182.0 3.4 %fusion.36 = (f32[2,2,16,72,128]{4,3,2,0,1:T(8,128)S(1)}, f32[2,2,16,72,128]{4,3,2,0,1:T(8,128)}) fusion(f32[4,1,16,72,128]{4,3,2,0,1:T(8,128)} %bitcast.3, f32[4,1,16,72,128]{4,3,2,0,1:T(8,128)S(1)} %bitcast.46), kind=kLoop, calls=%fused_computation.115 | loop fusion | flops 1179648 | bytes 9437184 | tf_op jit(solution)/shard_map/stack | solution.py:261
  186.8 2.6 convolution_bitcast_fusion.1
  190.7 3.0 collective-permute-start.10
  193.7 3.1 collective-permute-start.11
  200.8 3.5 %collective-permute-start.13 = (f32[64,128]{1,0:T(8,128)S(1)}, f32[64,128]{1,0:T(8,128)S(1)}, u32[]{:S(2)}, u32[]{:S(2)}) collective-permute-start(f32[64,128]{1,0:T(8,128)S(1)} %select_add_fusion.4), channel_id=1, source_target_pairs={{0,64},{4,68},{8,72},{12,76},{16,80},{20,84},{24,88},{28,92},{32,9... | collective-permute-start | bytes 98312 | tf_op jit(solution)/shard_map/ppermute | solution.py:154
  206.4 3.1 collective-permute-done.14
  212.3 3.6 %copy.13 = f32[2,2,16,72,128]{4,2,1,0,3:T(8,128)} copy(f32[2,2,16,72,128]{4,3,2,0,1:T(8,128)} %get-tuple-element.33) | data formatting | bytes 4718592 | tf_op jit(solution)/shard_map/slice | solution.py:222
  218.0 7.9 %shard_map.45 = f32[64,192]{1,0:T(8,128)} custom-call(f32[64,192]{1,0:T(8,128)} %pad_maximum_fusion.1.source_ref), custom_call_target="tpu_custom_call" | custom-call | tf_op jit(solution)/shard_map/pallas_call | solution.py:207
  235.8 3.1 collective-permute-done.20
  249.9 3.2 collective-permute-done.26
  254.3 7.5 %shard_map.46 = f32[64,128]{1,0:T(8,128)} custom-call(f32[64,128]{1,0:T(8,128)} %pad_maximum_fusion.2.source_ref), custom_call_target="tpu_custom_call" | custom-call | tf_op jit(solution)/shard_map/pallas_call | solution.py:207
  261.9 2.1 fusion.110
  264.5 4.9 %copy.15 = f32[128,1,72,128]{3,2,1,0:T(8,128)} copy(f32[128,1,72,128]{3,0,2,1:T(8,128)S(1)} %maximum_bitcast_fusion) | data formatting | bytes 9437184 | tf_op jit(solution)/shard_map/reshape | solution.py:266
  269.4 5.1 %all-to-all-start.2 = ((f32[128,1,72,128]{3,2,1,0:T(8,128)}), f32[128,1,72,128]{3,2,1,0:T(8,128)}, u32[]{:S(2)}, u32[]{:S(2)}) async-start(f32[128,1,72,128]{3,2,1,0:T(8,128)} %copy.15), calls=%async_computation.2 | async-start | bytes 9437184 | tf_op jit(solution)/shard_map/all_to_all | solution.py:267
  275.3 49.6 %all-to-all-done.2 = f32[128,1,72,128]{3,2,1,0:T(8,128)} async-done(((f32[128,1,72,128]{3,2,1,0:T(8,128)}), f32[128,1,72,128]{3,2,1,0:T(8,128)}, u32[]{:S(2)}, u32[]{:S(2)}) %all-to-all-start.2) | async-done | bytes 4718624 | tf_op jit(solution)/shard_map/all_to_all | solution.py:267
  324.8 5.1 %copy.16 = f32[32,4,1,72,128]{4,3,1,0,2:T(8,128)} copy(f32[32,4,1,72,128]{4,3,0,1,2:T(8,128)} %bitcast.18) | data formatting | bytes 9437184 | tf_op jit(solution)/shard_map/all_to_all | solution.py:267
  (86 shorter events, 46.8 us)
Async XLA Ops:
  0.6 7.1 %copy-start = (f32[32,6,48,128]{3,2,1,0:T(8,128)S(1)}, f32[32,6,48,128]{3,2,1,0:T(8,128)}, u32[]{:S(2)}) copy-start(f32[32,6,48,128]{3,2,1,0:T(8,128)} %refs_4_.3) | copy-start | bytes 14155780
  0.6 7.1 %copy-start.6 = (f32[6,48,128]{2,1,0:T(8,128)S(1)}, f32[6,48,128]{2,1,0:T(8,128)}, u32[]{:S(2)}) copy-start(f32[6,48,128]{2,1,0:T(8,128)} %param.3) | copy-start | bytes 442372
  5.0 18.7 %collective-permute-start = (f32[16,6,48,128]{3,2,1,0:T(8,128)}, f32[16,6,48,128]{3,2,1,0:T(8,128)S(1)}, u32[]{:S(2)}, u32[]{:S(2)}) collective-permute-start(f32[16,6,48,128]{3,2,1,0:T(8,128)} %get-tuple-element.35), channel_id=1, source_target_pairs={{0,4},{4,8},{8,12},{12,16},{16,20},{20,24},{24,28},{28,32},{32,36}... | collective-permute-start | bytes 7077896 | tf_op jit(solution)/shard_map/ppermute | solution.py:30
  6.4 17.3 %collective-permute-start.1 = (f32[16,6,48,128]{3,2,1,0:T(8,128)}, f32[16,6,48,128]{3,2,1,0:T(8,128)}, u32[]{:S(2)}, u32[]{:S(2)}) collective-permute-start(f32[16,6,48,128]{3,2,1,0:T(8,128)} %get-tuple-element.35), channel_id=1, source_target_pairs={{4,0},{8,4},{12,8},{16,12},{20,16},{24,20},{28,24},{32,28},{36,32}... | collective-permute-start | bytes 7077896 | tf_op jit(solution)/shard_map/ppermute | solution.py:31
  25.1 59.7 %collective-permute-start.4 = (f32[16,6,48,128]{3,2,1,0:T(8,128)S(1)}, f32[16,6,48,128]{3,2,1,0:T(8,128)}, u32[]{:S(2)}, u32[]{:S(2)}) collective-permute-start(f32[16,6,48,128]{3,2,1,0:T(8,128)S(1)} %get-tuple-element.22), channel_id=1, source_target_pairs={{0,4},{4,8},{8,12},{12,16},{16,20},{20,24},{24,28},{28,32},{32,36}... | collective-permute-start | bytes 7077896 | tf_op jit(solution)/shard_map/ppermute | solution.py:30
  42.5 42.4 %collective-permute-start.5 = (f32[16,6,48,128]{3,2,1,0:T(8,128)S(1)}, f32[16,6,48,128]{3,2,1,0:T(8,128)}, u32[]{:S(2)}, u32[]{:S(2)}) collective-permute-start(f32[16,6,48,128]{3,2,1,0:T(8,128)S(1)} %get-tuple-element.22), channel_id=1, source_target_pairs={{4,0},{8,4},{12,8},{16,12},{20,16},{24,20},{28,24},{32,28},{36,32}... | collective-permute-start | bytes 7077896 | tf_op jit(solution)/shard_map/ppermute | solution.py:31
  49.4 41.1 %collective-permute-start.2 = (f32[16,6,48,128]{3,2,1,0:T(8,128)}, f32[16,6,48,128]{3,2,1,0:T(8,128)}, u32[]{:S(2)}, u32[]{:S(2)}) collective-permute-start(f32[16,6,48,128]{3,2,1,0:T(8,128)} %shard_map.41.refs_1_), channel_id=1, source_target_pairs={{0,4},{4,8},{8,12},{12,16},{16,20},{20,24},{24,28},{28,32},{32,36}... | collective-permute-start | bytes 7077896 | tf_op jit(solution)/shard_map/ppermute | solution.py:30
  53.8 36.7 %collective-permute-start.3 = (f32[16,6,48,128]{3,2,1,0:T(8,128)}, f32[16,6,48,128]{3,2,1,0:T(8,128)}, u32[]{:S(2)}, u32[]{:S(2)}) collective-permute-start(f32[16,6,48,128]{3,2,1,0:T(8,128)} %shard_map.41.refs_1_), channel_id=1, source_target_pairs={{4,0},{8,4},{12,8},{16,12},{20,16},{24,20},{28,24},{32,28},{36,32}... | collective-permute-start | bytes 7077896 | tf_op jit(solution)/shard_map/ppermute | solution.py:31
  90.5 34.1 %collective-permute-start.6 = (f32[16,6,48,128]{3,2,1,0:T(8,128)}, f32[16,6,48,128]{3,2,1,0:T(8,128)}, u32[]{:S(2)}, u32[]{:S(2)}) collective-permute-start(f32[16,6,48,128]{3,2,1,0:T(8,128)} %shard_map.42.refs_1_), channel_id=1, source_target_pairs={{0,4},{4,8},{8,12},{12,16},{16,20},{20,24},{24,28},{28,32},{32,36}... | collective-permute-start | bytes 7077896 | tf_op jit(solution)/shard_map/ppermute | solution.py:30
  100.0 24.7 %collective-permute-start.7 = (f32[16,6,48,128]{3,2,1,0:T(8,128)}, f32[16,6,48,128]{3,2,1,0:T(8,128)}, u32[]{:S(2)}, u32[]{:S(2)}) collective-permute-start(f32[16,6,48,128]{3,2,1,0:T(8,128)} %shard_map.42.refs_1_), channel_id=1, source_target_pairs={{4,0},{8,4},{12,8},{16,12},{20,16},{24,20},{28,24},{32,28},{36,32}... | collective-permute-start | bytes 7077896 | tf_op jit(solution)/shard_map/ppermute | solution.py:31
  110.8 36.0 %all-to-all-start = ((f32[16,4,72,128]{3,2,0,1:T(8,128)}), f32[16,4,72,128]{3,2,0,1:T(8,128)}, u32[]{:S(2)}, u32[]{:S(2)}) async-start(f32[16,4,72,128]{3,2,0,1:T(8,128)} %copy.9), calls=%async_computation | async-start | bytes 4718592 | tf_op jit(solution)/shard_map/all_to_all | solution.py:112
  189.4 1.3 collective-permute-start.8
  190.7 6.3 %collective-permute-start.10 = (f32[64,128]{1,0:T(8,128)S(1)}, f32[64,128]{1,0:T(8,128)S(1)}, u32[]{:S(2)}, u32[]{:S(2)}) collective-permute-start(f32[64,128]{1,0:T(8,128)S(1)} %select_add_fusion.5), channel_id=1, source_target_pairs={{0,16},{4,20},{8,24},{12,28},{16,0},{20,4},{24,8},{28,12},{32,48},... | collective-permute-start | bytes 98312 | tf_op jit(solution)/shard_map/ppermute | solution.py:154
  193.7 5.1 %collective-permute-start.11 = (f32[64,128]{1,0:T(8,128)S(1)}, f32[64,128]{1,0:T(8,128)S(1)}, u32[]{:S(2)}, u32[]{:S(2)}) collective-permute-start(f32[64,128]{1,0:T(8,128)S(1)} %select_add_fusion.5), channel_id=1, source_target_pairs={{0,8},{4,12},{8,16},{12,20},{16,24},{20,28},{24,0},{28,4},{32,40},... | collective-permute-start | bytes 98312 | tf_op jit(solution)/shard_map/ppermute | solution.py:154
  196.8 3.9 %collective-permute-start.9 = (f32[64,128]{1,0:T(8,128)S(1)}, f32[64,128]{1,0:T(8,128)S(1)}, u32[]{:S(2)}, u32[]{:S(2)}) collective-permute-start(f32[64,128]{1,0:T(8,128)S(1)} %select_add_fusion.5), channel_id=1, source_target_pairs={{0,24},{4,28},{8,0},{12,4},{16,8},{20,12},{24,16},{28,20},{32,56},... | collective-permute-start | bytes 98312 | tf_op jit(solution)/shard_map/ppermute | solution.py:154
  200.8 4.2 %collective-permute-start.12 = (f32[64,128]{1,0:T(8,128)S(1)}, f32[64,128]{1,0:T(8,128)S(1)}, u32[]{:S(2)}, u32[]{:S(2)}) collective-permute-start(f32[64,128]{1,0:T(8,128)S(1)} %select_add_fusion.4), channel_id=1, source_target_pairs={{0,96},{4,100},{8,104},{12,108},{16,112},{20,116},{24,120},{28,124... | collective-permute-start | bytes 98312 | tf_op jit(solution)/shard_map/ppermute | solution.py:154
  200.8 5.5 %collective-permute-start.13 = (f32[64,128]{1,0:T(8,128)S(1)}, f32[64,128]{1,0:T(8,128)S(1)}, u32[]{:S(2)}, u32[]{:S(2)}) collective-permute-start(f32[64,128]{1,0:T(8,128)S(1)} %select_add_fusion.4), channel_id=1, source_target_pairs={{0,64},{4,68},{8,72},{12,76},{16,80},{20,84},{24,88},{28,92},{32,9... | collective-permute-start | bytes 98312 | tf_op jit(solution)/shard_map/ppermute | solution.py:154
  204.4 5.1 %collective-permute-start.14 = (f32[64,128]{1,0:T(8,128)S(1)}, f32[64,128]{1,0:T(8,128)S(1)}, u32[]{:S(2)}, u32[]{:S(2)}) collective-permute-start(f32[64,128]{1,0:T(8,128)S(1)} %select_add_fusion.4), channel_id=1, source_target_pairs={{0,32},{4,36},{8,40},{12,44},{16,48},{20,52},{24,56},{28,60},{32,6... | collective-permute-start | bytes 98312 | tf_op jit(solution)/shard_map/ppermute | solution.py:154
  209.5 6.4 %collective-permute-start.15 = (f32[64,128]{1,0:T(8,128)S(1)}, f32[64,128]{1,0:T(8,128)S(1)}, u32[]{:S(2)}, u32[]{:S(2)}) collective-permute-start(f32[64,128]{1,0:T(8,128)S(1)} %select_add_fusion.3), channel_id=1, source_target_pairs={{0,3},{1,0},{2,1},{3,2},{4,7},{5,4},{6,5},{7,6},{8,11},{9,8},{10,9... | collective-permute-start | bytes 98312 | tf_op jit(solution)/shard_map/ppermute | solution.py:154
  210.8 5.4 %collective-permute-start.16 = (f32[64,128]{1,0:T(8,128)S(1)}, f32[64,128]{1,0:T(8,128)S(1)}, u32[]{:S(2)}, u32[]{:S(2)}) collective-permute-start(f32[64,128]{1,0:T(8,128)S(1)} %select_add_fusion.3), channel_id=1, source_target_pairs={{0,2},{1,3},{2,0},{3,1},{4,6},{5,7},{6,4},{7,5},{8,10},{9,11},{10,... | collective-permute-start | bytes 98312 | tf_op jit(solution)/shard_map/ppermute | solution.py:154
  212.2 5.1 %collective-permute-start.17 = (f32[64,128]{1,0:T(8,128)S(1)}, f32[64,128]{1,0:T(8,128)S(1)}, u32[]{:S(2)}, u32[]{:S(2)}) collective-permute-start(f32[64,128]{1,0:T(8,128)S(1)} %select_add_fusion.3), channel_id=1, source_target_pairs={{0,1},{1,2},{2,3},{3,0},{4,5},{5,6},{6,7},{7,4},{8,9},{9,10},{10,1... | collective-permute-start | bytes 98312 | tf_op jit(solution)/shard_map/ppermute | solution.py:154
  230.5 1.3 collective-permute-start.18
  231.8 4.0 %collective-permute-start.19 = (f32[64,64]{1,0:T(8,128)S(1)}, f32[64,64]{1,0:T(8,128)S(1)}, u32[]{:S(2)}, u32[]{:S(2)}) collective-permute-start(f32[64,64]{1,0:T(8,128)S(1)} %select_add_fusion.2), channel_id=1, source_target_pairs={{0,24},{4,28},{8,0},{12,4},{16,8},{20,12},{24,16},{28,20},{32,56},... | collective-permute-start | bytes 49160 | tf_op jit(solution)/shard_map/ppermute | solution.py:154
  233.2 5.7 %collective-permute-start.20 = (f32[64,64]{1,0:T(8,128)S(1)}, f32[64,64]{1,0:T(8,128)S(1)}, u32[]{:S(2)}, u32[]{:S(2)}) collective-permute-start(f32[64,64]{1,0:T(8,128)S(1)} %select_add_fusion.2), channel_id=1, source_target_pairs={{0,16},{4,20},{8,24},{12,28},{16,0},{20,4},{24,8},{28,12},{32,48},... | collective-permute-start | bytes 49160 | tf_op jit(solution)/shard_map/ppermute | solution.py:154
  233.9 5.2 %collective-permute-start.21 = (f32[64,64]{1,0:T(8,128)S(1)}, f32[64,64]{1,0:T(8,128)S(1)}, u32[]{:S(2)}, u32[]{:S(2)}) collective-permute-start(f32[64,64]{1,0:T(8,128)S(1)} %select_add_fusion.2), channel_id=1, source_target_pairs={{0,8},{4,12},{8,16},{12,20},{16,24},{20,28},{24,0},{28,4},{32,40},... | collective-permute-start | bytes 49160 | tf_op jit(solution)/shard_map/ppermute | solution.py:154
  239.2 4.0 %collective-permute-start.22 = (f32[64,64]{1,0:T(8,128)S(1)}, f32[64,64]{1,0:T(8,128)S(1)}, u32[]{:S(2)}, u32[]{:S(2)}) collective-permute-start(f32[64,64]{1,0:T(8,128)S(1)} %select_add_fusion.1), channel_id=1, source_target_pairs={{0,96},{4,100},{8,104},{12,108},{16,112},{20,116},{24,120},{28,124... | collective-permute-start | bytes 49160 | tf_op jit(solution)/shard_map/ppermute | solution.py:154
  239.3 5.5 %collective-permute-start.23 = (f32[64,64]{1,0:T(8,128)S(1)}, f32[64,64]{1,0:T(8,128)S(1)}, u32[]{:S(2)}, u32[]{:S(2)}) collective-permute-start(f32[64,64]{1,0:T(8,128)S(1)} %select_add_fusion.1), channel_id=1, source_target_pairs={{0,64},{4,68},{8,72},{12,76},{16,80},{20,84},{24,88},{28,92},{32,9... | collective-permute-start | bytes 49160 | tf_op jit(solution)/shard_map/ppermute | solution.py:154
  240.7 5.1 %collective-permute-start.24 = (f32[64,64]{1,0:T(8,128)S(1)}, f32[64,64]{1,0:T(8,128)S(1)}, u32[]{:S(2)}, u32[]{:S(2)}) collective-permute-start(f32[64,64]{1,0:T(8,128)S(1)} %select_add_fusion.1), channel_id=1, source_target_pairs={{0,32},{4,36},{8,40},{12,44},{16,48},{20,52},{24,56},{28,60},{32,6... | collective-permute-start | bytes 49160 | tf_op jit(solution)/shard_map/ppermute | solution.py:154
  245.9 4.0 %collective-permute-start.25 = (f32[64,64]{1,0:T(8,128)S(1)}, f32[64,64]{1,0:T(8,128)S(1)}, u32[]{:S(2)}, u32[]{:S(2)}) collective-permute-start(f32[64,64]{1,0:T(8,128)S(1)} %select_add_fusion), channel_id=1, source_target_pairs={{0,3},{1,0},{2,1},{3,2},{4,7},{5,4},{6,5},{7,6},{8,11},{9,8},{10,9... | collective-permute-start | bytes 49160 | tf_op jit(solution)/shard_map/ppermute | solution.py:154
  247.6 5.4 %collective-permute-start.26 = (f32[64,64]{1,0:T(8,128)S(1)}, f32[64,64]{1,0:T(8,128)S(1)}, u32[]{:S(2)}, u32[]{:S(2)}) collective-permute-start(f32[64,64]{1,0:T(8,128)S(1)} %select_add_fusion), channel_id=1, source_target_pairs={{0,2},{1,3},{2,0},{3,1},{4,6},{5,7},{6,4},{7,5},{8,10},{9,11},{10,... | collective-permute-start | bytes 49160 | tf_op jit(solution)/shard_map/ppermute | solution.py:154
  248.5 5.1 %collective-permute-start.27 = (f32[64,64]{1,0:T(8,128)S(1)}, f32[64,64]{1,0:T(8,128)S(1)}, u32[]{:S(2)}, u32[]{:S(2)}) collective-permute-start(f32[64,64]{1,0:T(8,128)S(1)} %select_add_fusion), channel_id=1, source_target_pairs={{0,1},{1,2},{2,3},{3,0},{4,5},{5,6},{6,7},{7,4},{8,9},{9,10},{10,1... | collective-permute-start | bytes 49160 | tf_op jit(solution)/shard_map/ppermute | solution.py:154
  269.4 55.4 %all-to-all-start.2 = ((f32[128,1,72,128]{3,2,1,0:T(8,128)}), f32[128,1,72,128]{3,2,1,0:T(8,128)}, u32[]{:S(2)}, u32[]{:S(2)}) async-start(f32[128,1,72,128]{3,2,1,0:T(8,128)} %copy.15), calls=%async_computation.2 | async-start | bytes 9437184 | tf_op jit(solution)/shard_map/all_to_all | solution.py:267
  (8 other events, 24.6 us)

commit v9 on v7

--- a/solution.py
+++ b/solution.py
@@ -199,7 +199,7 @@
         result_ref[...] = jnp.where(row_ids == column, scaled, whole)
         return carry
 
-    lax.fori_loop(0, rows, column_step, 0)
+    lax.fori_loop(0, rows, column_step, 0, unroll=2)
 
 
 def eliminate(matrix, extra):

time: 331 us -> 331 us (level)
  no operation moved by 1% of the time
where the time goes in v9:
time: 331 us; the launch traced here: 330 us
  waiting for transfers between devices  88.1 us (27%)
  starting transfers between devices  69.6 us (21%)
  other arithmetic  62.3 us (19%)
  Pallas kernels  39.4 us (12%)
  blocking collectives  33.3 us (10%)
  local copies, waits for them, and re-layouts  27.2 us (8%)
  matrix products  9.06 us (3%)
    add x3, other arithmetic, local_terms(): return -2.0 * total + potential[None] * orbital_field  54.2 us
    all_to_all x1, waiting for transfers between devices, local(): orbitals = lax.all_to_all(orbitals, 'orb', 0, 1, tiled=True)  49.6 us
    all_to_all x1, blocking collectives, spread_cells(): lax.all_to_all(chunks, 'orb', 1, 0, tiled=True)  33.3 us
    ppermute x4, starting transfers between devices, halo_planes(): before = lax.ppermute(last, axis, up)  32.7 us
    ppermute x20, waiting for transfers between devices, group_round(): received.append(lax.ppermute(value, axis, pairs))  26 us
    pallas_call x4, Pallas kernels, filter_step(): pl.pallas_call(functools.partial(combine_kernel, scale, base is not None)...  23.9 us
    ppermute x20, starting transfers between devices, group_round(): received.append(lax.ppermute(value, axis, pairs))  21.2 us
    pallas_call x2, Pallas kernels, eliminate(): pl.pallas_call(eliminate_kernel, out_shape=jax.ShapeDtypeStruct(source.sh...  15.5 us
  transfers between devices with their start and end apart: 30, of which 19 were waited for; matrix products, arithmetic and copies ran while one was open for 20% of the time, Pallas kernels for 7%

profile of v9, /device:TPU:0, one launch (start us, length us, event | category | flops | bytes accessed | tf_op | source)
XLA Modules:
  0.0 330.0 jit_solution(5507827952523081204)
XLA Ops:
  0.7 4.3 %fusion.113 = (f32[16,6,48,128]{3,2,1,0:T(8,128)S(1)}, f32[16,6,48,128]{3,2,1,0:T(8,128)}) fusion(f32[32,6,48,128]{3,2,1,0:T(8,128)} %refs_4_.3), kind=kLoop, calls=%fused_computation.213 | loop fusion | bytes 9437184 | tf_op jit(solution)/shard_map/slice | solution.py:241
  7.7 16.0 %multiply_add_fusion.refs_0_ = f32[32,6,48,128]{3,2,1,0:T(8,128)} fusion(f32[32,6,48,128]{3,2,1,0:T(8,128)S(1)} %copy-done, f32[6,48,128]{2,1,0:T(8,128)S(1)} %copy-done.6), kind=kLoop, calls=%fused_computation.114 | loop fusion | flops 47185920 | bytes 9584640 | tf_op jit(solution)/shard_map/add | solution.py:49
  25.1 17.4 %collective-permute-start.4 = (f32[16,6,48,128]{3,2,1,0:T(8,128)S(1)}, f32[16,6,48,128]{3,2,1,0:T(8,128)}, u32[]{:S(2)}, u32[]{:S(2)}) collective-permute-start(f32[16,6,48,128]{3,2,1,0:T(8,128)S(1)} %get-tuple-element.22), channel_id=1, source_target_pairs={{0,4},{4,8},{8,12},{12,16},{16,20},{20,24},{24,28},{28,32},{32,36}... | collective-permute-start | bytes 7077896 | tf_op jit(solution)/shard_map/ppermute | solution.py:30
  43.8 5.6 %shard_map.41.refs_1_ = f32[16,6,48,128]{3,2,1,0:T(8,128)} custom-call(f32[32,6,48,128]{3,2,1,0:T(8,128)} %multiply_add_fusion.refs_0_, f32[32,6,48,128]{3,2,1,0:T(8,128)} %refs_4_.3, f32[16,6,48,128]{3,2,1,0:T(8,128)} %copy-done.5, f32[16,6,48,128]{3,2,1,0:T(8,128)} %collective-permute-done.1.refs_3_), custom_call_target="tpu_custom_call" | custom-call | tf_op jit(solution)/shard_map/pallas_call | solution.py:97
  49.4 4.4 %collective-permute-start.2 = (f32[16,6,48,128]{3,2,1,0:T(8,128)}, f32[16,6,48,128]{3,2,1,0:T(8,128)}, u32[]{:S(2)}, u32[]{:S(2)}) collective-permute-start(f32[16,6,48,128]{3,2,1,0:T(8,128)} %shard_map.41.refs_1_), channel_id=1, source_target_pairs={{0,4},{4,8},{8,12},{12,16},{16,20},{20,24},{24,28},{28,32},{32,36}... | collective-permute-start | bytes 7077896 | tf_op jit(solution)/shard_map/ppermute | solution.py:30
  55.1 29.8 %multiply_add_fusion.2.refs_0_ = f32[16,6,48,128]{3,2,1,0:T(8,128)} fusion(f32[16,6,48,128]{3,2,1,0:T(8,128)} %shard_map.41.refs_1_, f32[6,48,128]{2,1,0:T(8,128)S(1)} %copy-done.6), kind=kLoop, calls=%fused_computation.191 | loop fusion | flops 23592960 | bytes 4866048 | tf_op jit(solution)/shard_map/add | solution.py:49
  84.9 5.6 %shard_map.42.refs_1_ = f32[16,6,48,128]{3,2,1,0:T(8,128)} custom-call(f32[32,6,48,128]{3,2,1,0:T(8,128)} %multiply_add_fusion.refs_0_, f32[32,6,48,128]{3,2,1,0:T(8,128)} %refs_4_.3, f32[16,6,48,128]{3,2,1,0:T(8,128)} %collective-permute-done.4.refs_2_, f32[16,6,48,128]{3,2,1,0:T(8,128)} %collective-permute-done.5.refs_3_), custom_call_target="tpu_custom_call" | custom-call | tf_op jit(solution)/shard_map/pallas_call | solution.py:97
  90.5 9.4 %collective-permute-start.6 = (f32[16,6,48,128]{3,2,1,0:T(8,128)}, f32[16,6,48,128]{3,2,1,0:T(8,128)}, u32[]{:S(2)}, u32[]{:S(2)}) collective-permute-start(f32[16,6,48,128]{3,2,1,0:T(8,128)} %shard_map.42.refs_1_), channel_id=1, source_target_pairs={{0,4},{4,8},{8,12},{12,16},{16,20},{20,24},{24,28},{28,32},{32,36}... | collective-permute-start | bytes 7077896 | tf_op jit(solution)/shard_map/ppermute | solution.py:30
  101.2 6.4 %shard_map.43 = f32[16,6,48,128]{3,2,1,0:T(8,128)} custom-call(f32[16,6,48,128]{3,2,1,0:T(8,128)} %multiply_add_fusion.2.refs_0_, f32[16,6,48,128]{3,2,1,0:T(8,128)} %shard_map.41.refs_1_, f32[16,6,48,128]{3,2,1,0:T(8,128)} %collective-permute-done.2.refs_2_, f32[16,6,48,128]{3,2,1,0:T(8,128)} %collective-permute-done.3.refs_3_, f32[32,6,48,128]{3,2,1,0:T(8,128)} %refs_4_.3), custom_call_target="tpu_custom_call" | custom-call | tf_op jit(solution)/shard_map/pallas_call | solution.py:97
  107.6 3.2 copy.9
  110.8 5.4 %all-to-all-start = ((f32[16,4,72,128]{3,2,0,1:T(8,128)}), f32[16,4,72,128]{3,2,0,1:T(8,128)}, u32[]{:S(2)}, u32[]{:S(2)}) async-start(f32[16,4,72,128]{3,2,0,1:T(8,128)} %copy.9), calls=%async_computation | async-start | bytes 4718592 | tf_op jit(solution)/shard_map/all_to_all | solution.py:112
  116.2 8.4 %multiply_add_fusion.1.refs_0_ = f32[16,6,48,128]{3,2,1,0:T(8,128)} fusion(f32[16,6,48,128]{3,2,1,0:T(8,128)S(1)} %copy-done.3, f32[6,48,128]{2,1,0:T(8,128)S(1)} %copy-done.6), kind=kLoop, calls=%fused_computation.190 | loop fusion | flops 23592960 | bytes 4866048 | tf_op jit(solution)/shard_map/add | solution.py:49
  124.7 6.4 %shard_map.44 = f32[16,6,48,128]{3,2,1,0:T(8,128)} custom-call(f32[16,6,48,128]{3,2,1,0:T(8,128)} %multiply_add_fusion.1.refs_0_, f32[16,6,48,128]{3,2,1,0:T(8,128)} %shard_map.42.refs_1_, f32[16,6,48,128]{3,2,1,0:T(8,128)} %collective-permute-done.6.refs_2_, f32[16,6,48,128]{3,2,1,0:T(8,128)} %collective-permute-done.7.refs_3_, f32[32,6,48,128]{3,2,1,0:T(8,128)} %refs_4_.3), custom_call_target="tpu_custom_call" | custom-call | tf_op jit(solution)/shard_map/pallas_call | solution.py:97
  131.0 3.2 copy.10
  134.3 12.5 %all-to-all-done = f32[16,4,72,128]{3,2,0,1:T(8,128)} async-done(((f32[16,4,72,128]{3,2,0,1:T(8,128)}), f32[16,4,72,128]{3,2,0,1:T(8,128)}, u32[]{:S(2)}, u32[]{:S(2)}) %all-to-all-start) | async-done | bytes 2359328 | tf_op jit(solution)/shard_map/all_to_all | solution.py:112
  146.8 33.3 %all_to_all.45 = f32[16,4,72,128]{3,2,0,1:T(8,128)S(1)} all-to-all(f32[16,4,72,128]{3,2,0,1:T(8,128)} %copy.10), channel_id=1, replica_groups=mesh['grid'=32,'orb'=4] {'orb'}, dimensions={1} | all-to-all | bytes 4718592 | tf_op jit(solution)/shard_map/all_to_all | solution.py:112
  182.1 3.4 %fusion.36 = (f32[2,2,16,72,128]{4,3,2,0,1:T(8,128)S(1)}, f32[2,2,16,72,128]{4,3,2,0,1:T(8,128)}) fusion(f32[4,1,16,72,128]{4,3,2,0,1:T(8,128)} %bitcast.3, f32[4,1,16,72,128]{4,3,2,0,1:T(8,128)S(1)} %bitcast.46), kind=kLoop, calls=%fused_computation.115 | loop fusion | flops 1179648 | bytes 9437184 | tf_op jit(solution)/shard_map/stack | solution.py:261
  186.8 2.6 convolution_bitcast_fusion.1
  190.7 3.0 collective-permute-start.10
  193.7 3.1 collective-permute-start.11
  200.9 3.5 %collective-permute-start.13 = (f32[64,128]{1,0:T(8,128)S(1)}, f32[64,128]{1,0:T(8,128)S(1)}, u32[]{:S(2)}, u32[]{:S(2)}) collective-permute-start(f32[64,128]{1,0:T(8,128)S(1)} %select_add_fusion.4), channel_id=1, source_target_pairs={{0,64},{4,68},{8,72},{12,76},{16,80},{20,84},{24,88},{28,92},{32,9... | collective-permute-start | bytes 98312 | tf_op jit(solution)/shard_map/ppermute | solution.py:154
  206.4 3.1 collective-permute-done.14
  212.4 3.6 %copy.13 = f32[2,2,16,72,128]{4,2,1,0,3:T(8,128)} copy(f32[2,2,16,72,128]{4,3,2,0,1:T(8,128)} %get-tuple-element.33) | data formatting | bytes 4718592 | tf_op jit(solution)/shard_map/slice | solution.py:222
  218.1 8.0 %shard_map.45 = f32[64,192]{1,0:T(8,128)} custom-call(f32[64,192]{1,0:T(8,128)} %pad_maximum_fusion.1.source_ref), custom_call_target="tpu_custom_call" | custom-call | tf_op jit(solution)/shard_map/pallas_call | solution.py:207
  235.8 3.1 collective-permute-done.20
  249.9 3.2 collective-permute-done.26
  254.4 7.5 %shard_map.46 = f32[64,128]{1,0:T(8,128)} custom-call(f32[64,128]{1,0:T(8,128)} %pad_maximum_fusion.2.source_ref), custom_call_target="tpu_custom_call" | custom-call | tf_op jit(solution)/shard_map/pallas_call | solution.py:207
  261.9 2.1 fusion.110
  264.5 4.9 %copy.15 = f32[128,1,72,128]{3,2,1,0:T(8,128)} copy(f32[128,1,72,128]{3,0,2,1:T(8,128)S(1)} %maximum_bitcast_fusion) | data formatting | bytes 9437184 | tf_op jit(solution)/shard_map/reshape | solution.py:266
  269.5 5.1 %all-to-all-start.2 = ((f32[128,1,72,128]{3,2,1,0:T(8,128)}), f32[128,1,72,128]{3,2,1,0:T(8,128)}, u32[]{:S(2)}, u32[]{:S(2)}) async-start(f32[128,1,72,128]{3,2,1,0:T(8,128)} %copy.15), calls=%async_computation.2 | async-start | bytes 9437184 | tf_op jit(solution)/shard_map/all_to_all | solution.py:267
  275.3 49.6 %all-to-all-done.2 = f32[128,1,72,128]{3,2,1,0:T(8,128)} async-done(((f32[128,1,72,128]{3,2,1,0:T(8,128)}), f32[128,1,72,128]{3,2,1,0:T(8,128)}, u32[]{:S(2)}, u32[]{:S(2)}) %all-to-all-start.2) | async-done | bytes 4718624 | tf_op jit(solution)/shard_map/all_to_all | solution.py:267
  324.9 5.1 %copy.16 = f32[32,4,1,72,128]{4,3,1,0,2:T(8,128)} copy(f32[32,4,1,72,128]{4,3,0,1,2:T(8,128)} %bitcast.18) | data formatting | bytes 9437184 | tf_op jit(solution)/shard_map/all_to_all | solution.py:267
  (86 shorter events, 46.8 us)
Async XLA Ops:
  0.6 7.1 %copy-start = (f32[32,6,48,128]{3,2,1,0:T(8,128)S(1)}, f32[32,6,48,128]{3,2,1,0:T(8,128)}, u32[]{:S(2)}) copy-start(f32[32,6,48,128]{3,2,1,0:T(8,128)} %refs_4_.3) | copy-start | bytes 14155780
  0.6 7.1 %copy-start.6 = (f32[6,48,128]{2,1,0:T(8,128)S(1)}, f32[6,48,128]{2,1,0:T(8,128)}, u32[]{:S(2)}) copy-start(f32[6,48,128]{2,1,0:T(8,128)} %param.3) | copy-start | bytes 442372
  5.0 18.7 %collective-permute-start = (f32[16,6,48,128]{3,2,1,0:T(8,128)}, f32[16,6,48,128]{3,2,1,0:T(8,128)S(1)}, u32[]{:S(2)}, u32[]{:S(2)}) collective-permute-start(f32[16,6,48,128]{3,2,1,0:T(8,128)} %get-tuple-element.35), channel_id=1, source_target_pairs={{0,4},{4,8},{8,12},{12,16},{16,20},{20,24},{24,28},{28,32},{32,36}... | collective-permute-start | bytes 7077896 | tf_op jit(solution)/shard_map/ppermute | solution.py:30
  6.4 17.3 %collective-permute-start.1 = (f32[16,6,48,128]{3,2,1,0:T(8,128)}, f32[16,6,48,128]{3,2,1,0:T(8,128)}, u32[]{:S(2)}, u32[]{:S(2)}) collective-permute-start(f32[16,6,48,128]{3,2,1,0:T(8,128)} %get-tuple-element.35), channel_id=1, source_target_pairs={{4,0},{8,4},{12,8},{16,12},{20,16},{24,20},{28,24},{32,28},{36,32}... | collective-permute-start | bytes 7077896 | tf_op jit(solution)/shard_map/ppermute | solution.py:31
  25.1 59.7 %collective-permute-start.4 = (f32[16,6,48,128]{3,2,1,0:T(8,128)S(1)}, f32[16,6,48,128]{3,2,1,0:T(8,128)}, u32[]{:S(2)}, u32[]{:S(2)}) collective-permute-start(f32[16,6,48,128]{3,2,1,0:T(8,128)S(1)} %get-tuple-element.22), channel_id=1, source_target_pairs={{0,4},{4,8},{8,12},{12,16},{16,20},{20,24},{24,28},{28,32},{32,36}... | collective-permute-start | bytes 7077896 | tf_op jit(solution)/shard_map/ppermute | solution.py:30
  42.5 42.4 %collective-permute-start.5 = (f32[16,6,48,128]{3,2,1,0:T(8,128)S(1)}, f32[16,6,48,128]{3,2,1,0:T(8,128)}, u32[]{:S(2)}, u32[]{:S(2)}) collective-permute-start(f32[16,6,48,128]{3,2,1,0:T(8,128)S(1)} %get-tuple-element.22), channel_id=1, source_target_pairs={{4,0},{8,4},{12,8},{16,12},{20,16},{24,20},{28,24},{32,28},{36,32}... | collective-permute-start | bytes 7077896 | tf_op jit(solution)/shard_map/ppermute | solution.py:31
  49.4 41.1 %collective-permute-start.2 = (f32[16,6,48,128]{3,2,1,0:T(8,128)}, f32[16,6,48,128]{3,2,1,0:T(8,128)}, u32[]{:S(2)}, u32[]{:S(2)}) collective-permute-start(f32[16,6,48,128]{3,2,1,0:T(8,128)} %shard_map.41.refs_1_), channel_id=1, source_target_pairs={{0,4},{4,8},{8,12},{12,16},{16,20},{20,24},{24,28},{28,32},{32,36}... | collective-permute-start | bytes 7077896 | tf_op jit(solution)/shard_map/ppermute | solution.py:30
  53.8 36.7 %collective-permute-start.3 = (f32[16,6,48,128]{3,2,1,0:T(8,128)}, f32[16,6,48,128]{3,2,1,0:T(8,128)}, u32[]{:S(2)}, u32[]{:S(2)}) collective-permute-start(f32[16,6,48,128]{3,2,1,0:T(8,128)} %shard_map.41.refs_1_), channel_id=1, source_target_pairs={{4,0},{8,4},{12,8},{16,12},{20,16},{24,20},{28,24},{32,28},{36,32}... | collective-permute-start | bytes 7077896 | tf_op jit(solution)/shard_map/ppermute | solution.py:31
  90.5 34.2 %collective-permute-start.6 = (f32[16,6,48,128]{3,2,1,0:T(8,128)}, f32[16,6,48,128]{3,2,1,0:T(8,128)}, u32[]{:S(2)}, u32[]{:S(2)}) collective-permute-start(f32[16,6,48,128]{3,2,1,0:T(8,128)} %shard_map.42.refs_1_), channel_id=1, source_target_pairs={{0,4},{4,8},{8,12},{12,16},{16,20},{20,24},{24,28},{28,32},{32,36}... | collective-permute-start | bytes 7077896 | tf_op jit(solution)/shard_map/ppermute | solution.py:30
  100.0 24.7 %collective-permute-start.7 = (f32[16,6,48,128]{3,2,1,0:T(8,128)}, f32[16,6,48,128]{3,2,1,0:T(8,128)}, u32[]{:S(2)}, u32[]{:S(2)}) collective-permute-start(f32[16,6,48,128]{3,2,1,0:T(8,128)} %shard_map.42.refs_1_), channel_id=1, source_target_pairs={{4,0},{8,4},{12,8},{16,12},{20,16},{24,20},{28,24},{32,28},{36,32}... | collective-permute-start | bytes 7077896 | tf_op jit(solution)/shard_map/ppermute | solution.py:31
  110.8 36.0 %all-to-all-start = ((f32[16,4,72,128]{3,2,0,1:T(8,128)}), f32[16,4,72,128]{3,2,0,1:T(8,128)}, u32[]{:S(2)}, u32[]{:S(2)}) async-start(f32[16,4,72,128]{3,2,0,1:T(8,128)} %copy.9), calls=%async_computation | async-start | bytes 4718592 | tf_op jit(solution)/shard_map/all_to_all | solution.py:112
  189.4 1.3 collective-permute-start.8
  190.7 6.3 %collective-permute-start.10 = (f32[64,128]{1,0:T(8,128)S(1)}, f32[64,128]{1,0:T(8,128)S(1)}, u32[]{:S(2)}, u32[]{:S(2)}) collective-permute-start(f32[64,128]{1,0:T(8,128)S(1)} %select_add_fusion.5), channel_id=1, source_target_pairs={{0,16},{4,20},{8,24},{12,28},{16,0},{20,4},{24,8},{28,12},{32,48},... | collective-permute-start | bytes 98312 | tf_op jit(solution)/shard_map/ppermute | solution.py:154
  193.7 5.1 %collective-permute-start.11 = (f32[64,128]{1,0:T(8,128)S(1)}, f32[64,128]{1,0:T(8,128)S(1)}, u32[]{:S(2)}, u32[]{:S(2)}) collective-permute-start(f32[64,128]{1,0:T(8,128)S(1)} %select_add_fusion.5), channel_id=1, source_target_pairs={{0,8},{4,12},{8,16},{12,20},{16,24},{20,28},{24,0},{28,4},{32,40},... | collective-permute-start | bytes 98312 | tf_op jit(solution)/shard_map/ppermute | solution.py:154
  196.8 3.9 %collective-permute-start.9 = (f32[64,128]{1,0:T(8,128)S(1)}, f32[64,128]{1,0:T(8,128)S(1)}, u32[]{:S(2)}, u32[]{:S(2)}) collective-permute-start(f32[64,128]{1,0:T(8,128)S(1)} %select_add_fusion.5), channel_id=1, source_target_pairs={{0,24},{4,28},{8,0},{12,4},{16,8},{20,12},{24,16},{28,20},{32,56},... | collective-permute-start | bytes 98312 | tf_op jit(solution)/shard_map/ppermute | solution.py:154
  200.8 4.2 %collective-permute-start.12 = (f32[64,128]{1,0:T(8,128)S(1)}, f32[64,128]{1,0:T(8,128)S(1)}, u32[]{:S(2)}, u32[]{:S(2)}) collective-permute-start(f32[64,128]{1,0:T(8,128)S(1)} %select_add_fusion.4), channel_id=1, source_target_pairs={{0,96},{4,100},{8,104},{12,108},{16,112},{20,116},{24,120},{28,124... | collective-permute-start | bytes 98312 | tf_op jit(solution)/shard_map/ppermute | solution.py:154
  200.9 5.5 %collective-permute-start.13 = (f32[64,128]{1,0:T(8,128)S(1)}, f32[64,128]{1,0:T(8,128)S(1)}, u32[]{:S(2)}, u32[]{:S(2)}) collective-permute-start(f32[64,128]{1,0:T(8,128)S(1)} %select_add_fusion.4), channel_id=1, source_target_pairs={{0,64},{4,68},{8,72},{12,76},{16,80},{20,84},{24,88},{28,92},{32,9... | collective-permute-start | bytes 98312 | tf_op jit(solution)/shard_map/ppermute | solution.py:154
  204.4 5.1 %collective-permute-start.14 = (f32[64,128]{1,0:T(8,128)S(1)}, f32[64,128]{1,0:T(8,128)S(1)}, u32[]{:S(2)}, u32[]{:S(2)}) collective-permute-start(f32[64,128]{1,0:T(8,128)S(1)} %select_add_fusion.4), channel_id=1, source_target_pairs={{0,32},{4,36},{8,40},{12,44},{16,48},{20,52},{24,56},{28,60},{32,6... | collective-permute-start | bytes 98312 | tf_op jit(solution)/shard_map/ppermute | solution.py:154
  209.6 6.4 %collective-permute-start.15 = (f32[64,128]{1,0:T(8,128)S(1)}, f32[64,128]{1,0:T(8,128)S(1)}, u32[]{:S(2)}, u32[]{:S(2)}) collective-permute-start(f32[64,128]{1,0:T(8,128)S(1)} %select_add_fusion.3), channel_id=1, source_target_pairs={{0,3},{1,0},{2,1},{3,2},{4,7},{5,4},{6,5},{7,6},{8,11},{9,8},{10,9... | collective-permute-start | bytes 98312 | tf_op jit(solution)/shard_map/ppermute | solution.py:154
  210.8 5.4 %collective-permute-start.16 = (f32[64,128]{1,0:T(8,128)S(1)}, f32[64,128]{1,0:T(8,128)S(1)}, u32[]{:S(2)}, u32[]{:S(2)}) collective-permute-start(f32[64,128]{1,0:T(8,128)S(1)} %select_add_fusion.3), channel_id=1, source_target_pairs={{0,2},{1,3},{2,0},{3,1},{4,6},{5,7},{6,4},{7,5},{8,10},{9,11},{10,... | collective-permute-start | bytes 98312 | tf_op jit(solution)/shard_map/ppermute | solution.py:154
  212.3 5.1 %collective-permute-start.17 = (f32[64,128]{1,0:T(8,128)S(1)}, f32[64,128]{1,0:T(8,128)S(1)}, u32[]{:S(2)}, u32[]{:S(2)}) collective-permute-start(f32[64,128]{1,0:T(8,128)S(1)} %select_add_fusion.3), channel_id=1, source_target_pairs={{0,1},{1,2},{2,3},{3,0},{4,5},{5,6},{6,7},{7,4},{8,9},{9,10},{10,1... | collective-permute-start | bytes 98312 | tf_op jit(solution)/shard_map/ppermute | solution.py:154
  230.6 1.3 collective-permute-start.18
  231.9 4.0 %collective-permute-start.19 = (f32[64,64]{1,0:T(8,128)S(1)}, f32[64,64]{1,0:T(8,128)S(1)}, u32[]{:S(2)}, u32[]{:S(2)}) collective-permute-start(f32[64,64]{1,0:T(8,128)S(1)} %select_add_fusion.2), channel_id=1, source_target_pairs={{0,24},{4,28},{8,0},{12,4},{16,8},{20,12},{24,16},{28,20},{32,56},... | collective-permute-start | bytes 49160 | tf_op jit(solution)/shard_map/ppermute | solution.py:154
  233.2 5.7 %collective-permute-start.20 = (f32[64,64]{1,0:T(8,128)S(1)}, f32[64,64]{1,0:T(8,128)S(1)}, u32[]{:S(2)}, u32[]{:S(2)}) collective-permute-start(f32[64,64]{1,0:T(8,128)S(1)} %select_add_fusion.2), channel_id=1, source_target_pairs={{0,16},{4,20},{8,24},{12,28},{16,0},{20,4},{24,8},{28,12},{32,48},... | collective-permute-start | bytes 49160 | tf_op jit(solution)/shard_map/ppermute | solution.py:154
  234.0 5.2 %collective-permute-start.21 = (f32[64,64]{1,0:T(8,128)S(1)}, f32[64,64]{1,0:T(8,128)S(1)}, u32[]{:S(2)}, u32[]{:S(2)}) collective-permute-start(f32[64,64]{1,0:T(8,128)S(1)} %select_add_fusion.2), channel_id=1, source_target_pairs={{0,8},{4,12},{8,16},{12,20},{16,24},{20,28},{24,0},{28,4},{32,40},... | collective-permute-start | bytes 49160 | tf_op jit(solution)/shard_map/ppermute | solution.py:154
  239.3 4.0 %collective-permute-start.22 = (f32[64,64]{1,0:T(8,128)S(1)}, f32[64,64]{1,0:T(8,128)S(1)}, u32[]{:S(2)}, u32[]{:S(2)}) collective-permute-start(f32[64,64]{1,0:T(8,128)S(1)} %select_add_fusion.1), channel_id=1, source_target_pairs={{0,96},{4,100},{8,104},{12,108},{16,112},{20,116},{24,120},{28,124... | collective-permute-start | bytes 49160 | tf_op jit(solution)/shard_map/ppermute | solution.py:154
  239.4 5.5 %collective-permute-start.23 = (f32[64,64]{1,0:T(8,128)S(1)}, f32[64,64]{1,0:T(8,128)S(1)}, u32[]{:S(2)}, u32[]{:S(2)}) collective-permute-start(f32[64,64]{1,0:T(8,128)S(1)} %select_add_fusion.1), channel_id=1, source_target_pairs={{0,64},{4,68},{8,72},{12,76},{16,80},{20,84},{24,88},{28,92},{32,9... | collective-permute-start | bytes 49160 | tf_op jit(solution)/shard_map/ppermute | solution.py:154
  240.8 5.1 %collective-permute-start.24 = (f32[64,64]{1,0:T(8,128)S(1)}, f32[64,64]{1,0:T(8,128)S(1)}, u32[]{:S(2)}, u32[]{:S(2)}) collective-permute-start(f32[64,64]{1,0:T(8,128)S(1)} %select_add_fusion.1), channel_id=1, source_target_pairs={{0,32},{4,36},{8,40},{12,44},{16,48},{20,52},{24,56},{28,60},{32,6... | collective-permute-start | bytes 49160 | tf_op jit(solution)/shard_map/ppermute | solution.py:154
  246.0 4.0 %collective-permute-start.25 = (f32[64,64]{1,0:T(8,128)S(1)}, f32[64,64]{1,0:T(8,128)S(1)}, u32[]{:S(2)}, u32[]{:S(2)}) collective-permute-start(f32[64,64]{1,0:T(8,128)S(1)} %select_add_fusion), channel_id=1, source_target_pairs={{0,3},{1,0},{2,1},{3,2},{4,7},{5,4},{6,5},{7,6},{8,11},{9,8},{10,9... | collective-permute-start | bytes 49160 | tf_op jit(solution)/shard_map/ppermute | solution.py:154
  247.7 5.4 %collective-permute-start.26 = (f32[64,64]{1,0:T(8,128)S(1)}, f32[64,64]{1,0:T(8,128)S(1)}, u32[]{:S(2)}, u32[]{:S(2)}) collective-permute-start(f32[64,64]{1,0:T(8,128)S(1)} %select_add_fusion), channel_id=1, source_target_pairs={{0,2},{1,3},{2,0},{3,1},{4,6},{5,7},{6,4},{7,5},{8,10},{9,11},{10,... | collective-permute-start | bytes 49160 | tf_op jit(solution)/shard_map/ppermute | solution.py:154
  248.6 5.1 %collective-permute-start.27 = (f32[64,64]{1,0:T(8,128)S(1)}, f32[64,64]{1,0:T(8,128)S(1)}, u32[]{:S(2)}, u32[]{:S(2)}) collective-permute-start(f32[64,64]{1,0:T(8,128)S(1)} %select_add_fusion), channel_id=1, source_target_pairs={{0,1},{1,2},{2,3},{3,0},{4,5},{5,6},{6,7},{7,4},{8,9},{9,10},{10,1... | collective-permute-start | bytes 49160 | tf_op jit(solution)/shard_map/ppermute | solution.py:154
  269.5 55.4 %all-to-all-start.2 = ((f32[128,1,72,128]{3,2,1,0:T(8,128)}), f32[128,1,72,128]{3,2,1,0:T(8,128)}, u32[]{:S(2)}, u32[]{:S(2)}) async-start(f32[128,1,72,128]{3,2,1,0:T(8,128)} %copy.15), calls=%async_computation.2 | async-start | bytes 9437184 | tf_op jit(solution)/shard_map/all_to_all | solution.py:267
  (8 other events, 24.6 us)
